TPU v7x, 128 devices: a whole 4x4x4 slice. The times are simulated.
128 devices in a mesh: row: 8 (over y, z_hi), col: 16 (over z_lo, x, core).
Axes of the slice: x: 4, y: 4, z: 4 (z_hi: 2, z_lo: 2; z = z_hi * 2 + z_lo), core: 2. Of those that a mesh axis runs over, the one named last changes fastest.
Arguments:
- upper_stored: bfloat16 [6144, 6144], P('row', 'col'), may hold values from -6 to 6
- block_cells: int32 [96, 3], replicated, may hold values from 0 to 15
Outputs:
- purified: bfloat16 [6144, 6144], P('row', 'col')
Inputs may be any that keep to these rules, and one draw needn't show every extreme that they name: `block_cells`: integer cell coordinates of each atom block on a periodic lattice of 16 cells a side.
All inputs are finite; a program needn't handle non-finite values.
Results may differ from a plain program's by a relative error of at most 0.0067.
Values may be sent and summed in bfloat16 or wider, within the bound.
No kernel may reach another device: no remote copies, remote signals or barrier semaphores. Data moves between devices by JAX's collectives and lax.ppermute only.
A program may use at most 64 MiB of HBM per device.

v0:
```python
import math

import jax
import jax.numpy as jnp
from jax import lax
from jax.sharding import PartitionSpec as P

BLK = 64
BOX = 16
NEAR = 40
FAR = 90


def shifted_2(array, axis, by):
    length = lax.axis_size(axis)
    return lax.ppermute(array, axis, [(i, (i + by) % length) for i in range(length)])


def partner(value, axis, bit):
    mask = 2**bit
    pairs = [(source, source ^ mask) for source in range(lax.axis_size(axis))]
    return lax.ppermute(value, axis, pairs)


def cell_mask(block_cells, row_start, row_count, col_start, col_count, bound_sq):
    row_cells = lax.dynamic_slice_in_dim(block_cells, row_start, row_count, 0)
    col_cells = lax.dynamic_slice_in_dim(block_cells, col_start, col_count, 0)
    offset_abs = jnp.abs(row_cells[:, None, :] - col_cells[None, :, :])
    wrapped = jnp.minimum(offset_abs, BOX - offset_abs)
    return jnp.sum(wrapped * wrapped, axis=2) <= bound_sq


def block_keep(matrix_tile, keep_mask):
    row_count, col_count = matrix_tile.shape
    row_blocks, col_blocks = keep_mask.shape
    shaped = matrix_tile.reshape(
        row_blocks, row_count // row_blocks, col_blocks, col_count // col_blocks
    )
    kept = jnp.where(keep_mask[:, None, :, None], shaped, jnp.zeros_like(shaped))
    return kept.reshape(row_count, col_count)


def own_part(matrix_tile, layer_bit, half_width):
    return jnp.where(layer_bit == 0, matrix_tile[:, :half_width], matrix_tile[:, half_width:])


def partner_part(matrix_tile, layer_bit, half_width):
    return jnp.where(layer_bit == 0, matrix_tile[:, half_width:], matrix_tile[:, :half_width])


def join_halves(own_piece, partner_piece, layer_bit):
    first_order = jnp.concatenate([own_piece, partner_piece], 1)
    second_order = jnp.concatenate([partner_piece, own_piece], 1)
    return jnp.where(layer_bit == 0, first_order, second_order)


def skew_left(operand, row_id, layer_bit, grid_size):
    steps_wanted = (row_id + layer_bit * (grid_size // 2)) % grid_size
    for bit_pos in range((grid_size - 1).bit_length()):
        shifted = shifted_2(operand, "col", -(2 << bit_pos))
        operand = jnp.where((steps_wanted >> bit_pos) % 2 == 1, shifted, operand)
    return operand


def skew_right(operand, tile_col, layer_bit, grid_size):
    steps_wanted = (tile_col + layer_bit * (grid_size // 2)) % grid_size
    for bit_pos in range((grid_size - 1).bit_length()):
        shifted = shifted_2(operand, "row", -(1 << bit_pos))
        operand = jnp.where((steps_wanted >> bit_pos) % 2 == 1, shifted, operand)
    return operand


def cannon_half(left, right, grid_size):
    running = jnp.zeros((left.shape[0], right.shape[1]), jnp.float32)
    for section in range(grid_size // 2):
        running = running + jnp.dot(left, right, preferred_element_type=jnp.float32)
        if section + 1 < grid_size // 2:
            left = shifted_2(left, "col", -2)
            right = shifted_2(right, "row", -1)
    return running


def per_device(upper_stored, block_cells):
    grid_size = lax.axis_size("row")
    row_id = lax.axis_index("row")
    col_id = lax.axis_index("col")
    layer_bit = col_id % 2
    tile_col = col_id // 2
    tile_side, half_width = upper_stored.shape
    order_total = tile_side * grid_size
    tile_blocks = tile_side // BLK
    half_blocks = half_width // BLK
    slab_width = half_width // grid_size
    stacked = lax.all_to_all(
        lax.all_to_all(upper_stored, "row", split_axis=1, concat_axis=0, tiled=True),
        "col",
        split_axis=0,
        concat_axis=1,
        tiled=True,
    )
    gathered = lax.all_to_all(stacked.T, "row", split_axis=0, concat_axis=0, tiled=True)
    mirrored = (
        gathered.reshape(grid_size, 2, slab_width, half_width)
        .transpose(1, 0, 2, 3)
        .reshape(tile_side, half_width)
    )
    global_rows = row_id * tile_side + lax.broadcasted_iota(jnp.int32, (tile_side, half_width), 0)
    global_cols = col_id * half_width + lax.broadcasted_iota(jnp.int32, (tile_side, half_width), 1)
    symmetric = jnp.where(global_rows <= global_cols, upper_stored, mirrored)
    near_own = cell_mask(
        block_cells, row_id * tile_blocks, tile_blocks, col_id * half_blocks, half_blocks, NEAR
    )
    diagonal = jnp.where(global_rows == global_cols, 0.5, 0.0).astype(jnp.float32)
    value_scale = 2.0 / math.sqrt(order_total)
    own_density = block_keep(
        diagonal + value_scale * symmetric.astype(jnp.float32), near_own
    ).astype(jnp.bfloat16)
    partner_density = partner(own_density, "col", 0)
    density = join_halves(own_density, partner_density, layer_bit)
    right_start = skew_right(density, tile_col, layer_bit, grid_size)
    left_start = skew_left(density, row_id, layer_bit, grid_size)
    running = cannon_half(left_start, right_start, grid_size)
    far_full = cell_mask(
        block_cells, row_id * tile_blocks, tile_blocks, tile_col * tile_blocks, tile_blocks, FAR
    )
    partner_running = partner(running, "col", 0)
    square = block_keep(running + partner_running, far_full)
    square_low = square.astype(jnp.bfloat16)
    own_square = own_part(square, layer_bit, half_width)
    right_again = skew_right(density, tile_col, layer_bit, grid_size)
    left_again = skew_left(square_low, row_id, layer_bit, grid_size)
    cubic_running = cannon_half(left_again, right_again, grid_size)
    received_cubic = partner(partner_part(cubic_running, layer_bit, half_width), "col", 0)
    cubic = own_part(cubic_running, layer_bit, half_width) + received_cubic
    return block_keep(3.0 * own_square - 2.0 * cubic, near_own).astype(jnp.bfloat16)


def solution(mesh):
    return jax.shard_map(
        per_device,
        mesh=mesh,
        in_specs=(P("row", "col"), P()),
        out_specs=P("row", "col"),
        check_vma=False,
    )
```

profile of v0, /device:TPU:1, one launch (start us, length us, event | category | flops | bytes accessed | tf_op | source)
XLA Modules:
  0.0 518.1 jit_solution(772302218898402563)
XLA Ops:
  1.3 19.3 %all_to_all.44 = bf16[768,8,48]{0,2,1:T(8,128)(2,1)S(1)} all-to-all(bf16[768,8,48]{0,2,1:T(8,128)(2,1)S(1)} %bitcast.34), channel_id=1, replica_groups=mesh['row'=8,'col'=16] {'row'}, dimensions={1} | all-to-all | bytes 1179648 | tf_op jit(solution)/shard_map/all_to_all | solution.py:95
  21.9 6.8 %all-to-all-start.1 = ((bf16[16,384,48]{1,2,0:T(8,128)(2,1)}), bf16[16,384,48]{1,2,0:T(8,128)(2,1)}, u32[]{:S(2)}, u32[]{:S(2)}) async-start(bf16[16,384,48]{1,2,0:T(8,128)(2,1)} %copy.26), calls=%async_computation.1 | async-start | bytes 1179648 | tf_op jit(solution)/shard_map/all_to_all | solution.py:94
  28.9 10.1 %all-to-all-done.1 = bf16[16,384,48]{1,2,0:T(8,128)(2,1)} async-done(((bf16[16,384,48]{1,2,0:T(8,128)(2,1)}), bf16[16,384,48]{1,2,0:T(8,128)(2,1)}, u32[]{:S(2)}, u32[]{:S(2)}) %all-to-all-start.1) | async-done | bytes 589856 | tf_op jit(solution)/shard_map/all_to_all | solution.py:94
  39.0 3.5 all-to-all-start.2
  44.2 8.9 %all-to-all-done.2 = bf16[8,96,384]{2,1,0:T(8,128)(2,1)S(1)} async-done(((bf16[8,96,384]{2,1,0:T(8,128)(2,1)}), bf16[8,96,384]{2,1,0:T(8,128)(2,1)S(1)}, u32[]{:S(2)}, u32[]{:S(2)}) %all-to-all-start.2) | async-done | bytes 589856 | tf_op jit(solution)/shard_map/all_to_all | solution.py:101
  61.1 25.1 %collective-permute-done.4 = bf16[768,768]{1,0:T(8,128)(2,1)S(1)} collective-permute-done((bf16[768,768]{1,0:T(8,128)(2,1)S(1)}, bf16[768,768]{1,0:T(8,128)(2,1)S(1)}, u32[]{:S(2)}, u32[]{:S(2)}) %collective-permute-start.4) | collective-permute-done | bytes 1179680 | tf_op jit(solution)/shard_map/ppermute | solution.py:16
  87.3 13.3 %collective-permute-done.1 = bf16[768,768]{1,0:T(8,128)(2,1)} collective-permute-done((bf16[768,768]{1,0:T(8,128)(2,1)S(1)}, bf16[768,768]{1,0:T(8,128)(2,1)}, u32[]{:S(2)}, u32[]{:S(2)}) %collective-permute-start.1) | collective-permute-done | bytes 1179680 | tf_op jit(solution)/shard_map/ppermute | solution.py:16
  100.9 6.5 %collective-permute-start.5 = (bf16[768,768]{1,0:T(8,128)(2,1)S(1)}, bf16[768,768]{1,0:T(8,128)(2,1)}, u32[]{:S(2)}, u32[]{:S(2)}) collective-permute-start(bf16[768,768]{1,0:T(8,128)(2,1)S(1)} %get-tuple-element.7), channel_id=1, source_target_pairs={{0,96},{16,112},{32,0},{48,16},{64,32},{80,48},{96,64},{112,80},{1... | collective-permute-start | bytes 3538952 | tf_op jit(solution)/shard_map/ppermute | solution.py:16
  107.4 20.4 %collective-permute-done.2 = bf16[768,768]{1,0:T(8,128)(2,1)} collective-permute-done((bf16[768,768]{1,0:T(8,128)(2,1)S(1)}, bf16[768,768]{1,0:T(8,128)(2,1)}, u32[]{:S(2)}, u32[]{:S(2)}) %collective-permute-start.2) | collective-permute-done | bytes 1179680 | tf_op jit(solution)/shard_map/ppermute | solution.py:16
  130.2 2.4 collective-permute-start.6
  132.6 19.9 %collective-permute-done.3 = bf16[768,768]{1,0:T(8,128)(2,1)} collective-permute-done((bf16[768,768]{1,0:T(8,128)(2,1)S(1)}, bf16[768,768]{1,0:T(8,128)(2,1)}, u32[]{:S(2)}, u32[]{:S(2)}) %collective-permute-start.3) | collective-permute-done | bytes 1179680 | tf_op jit(solution)/shard_map/ppermute | solution.py:16
  153.9 17.7 %collective-permute-start.7 = (bf16[768,768]{1,0:T(8,128)(2,1)S(1)}, bf16[768,768]{1,0:T(8,128)(2,1)S(1)}, u32[]{:S(2)}, u32[]{:S(2)}) collective-permute-start(bf16[768,768]{1,0:T(8,128)(2,1)S(1)} %broadcast_select_fusion.8), channel_id=1, source_target_pairs={{0,14},{1,15},{2,0},{3,1},{4,2},{5,3},{6,4},{7,5},{8,6},{9,7},{10,... | collective-permute-start | bytes 3538952 | tf_op jit(solution)/shard_map/ppermute | solution.py:16
  174.5 31.7 %collective-permute-done.7 = bf16[768,768]{1,0:T(8,128)(2,1)S(1)} collective-permute-done((bf16[768,768]{1,0:T(8,128)(2,1)S(1)}, bf16[768,768]{1,0:T(8,128)(2,1)S(1)}, u32[]{:S(2)}, u32[]{:S(2)}) %collective-permute-start.7) | collective-permute-done | bytes 1179680 | tf_op jit(solution)/shard_map/ppermute | solution.py:16
  206.3 5.5 %collective-permute-start.9 = (bf16[768,768]{1,0:T(8,128)(2,1)S(1)}, bf16[768,768]{1,0:T(8,128)(2,1)S(1)}, u32[]{:S(2)}, u32[]{:S(2)}) collective-permute-start(bf16[768,768]{1,0:T(8,128)(2,1)S(1)} %collective-permute-done.7), channel_id=1, source_target_pairs={{0,14},{1,15},{2,0},{3,1},{4,2},{5,3},{6,4},{7,5},{8,6},{9,7},{10,... | collective-permute-start | bytes 3538952 | tf_op jit(solution)/shard_map/ppermute | solution.py:16
  211.8 32.6 %collective-permute-done.9 = bf16[768,768]{1,0:T(8,128)(2,1)S(1)} collective-permute-done((bf16[768,768]{1,0:T(8,128)(2,1)S(1)}, bf16[768,768]{1,0:T(8,128)(2,1)S(1)}, u32[]{:S(2)}, u32[]{:S(2)}) %collective-permute-start.9) | collective-permute-done | bytes 1179680 | tf_op jit(solution)/shard_map/ppermute | solution.py:16
  244.4 9.5 %collective-permute-start.11 = (bf16[768,768]{1,0:T(8,128)(2,1)S(1)}, bf16[768,768]{1,0:T(8,128)(2,1)S(1)}, u32[]{:S(2)}, u32[]{:S(2)}) collective-permute-start(bf16[768,768]{1,0:T(8,128)(2,1)S(1)} %collective-permute-done.9), channel_id=1, source_target_pairs={{0,14},{1,15},{2,0},{3,1},{4,2},{5,3},{6,4},{7,5},{8,6},{9,7},{10,... | collective-permute-start | bytes 3538952 | tf_op jit(solution)/shard_map/ppermute | solution.py:16
  253.8 3.0 collective-permute-start.12
  260.1 33.1 %collective-permute-done.11 = bf16[768,768]{1,0:T(8,128)(2,1)S(1)} collective-permute-done((bf16[768,768]{1,0:T(8,128)(2,1)S(1)}, bf16[768,768]{1,0:T(8,128)(2,1)S(1)}, u32[]{:S(2)}, u32[]{:S(2)}) %collective-permute-start.11) | collective-permute-done | bytes 1179680 | tf_op jit(solution)/shard_map/ppermute | solution.py:16
  294.4 2.5 collective-permute-start.13
  298.6 4.4 broadcast_in_dim.44
  305.3 41.9 %collective-permute-start.14 = (bf16[768,768]{1,0:T(8,128)(2,1)S(1)}, bf16[768,768]{1,0:T(8,128)(2,1)S(1)}, u32[]{:S(2)}, u32[]{:S(2)}) collective-permute-start(bf16[768,768]{1,0:T(8,128)(2,1)S(1)} %get-tuple-element.5), channel_id=1, source_target_pairs={{0,14},{1,15},{2,0},{3,1},{4,2},{5,3},{6,4},{7,5},{8,6},{9,7},{10,... | collective-permute-start | bytes 3538952 | tf_op jit(solution)/shard_map/ppermute | solution.py:16
  347.2 25.3 %collective-permute-done.14 = bf16[768,768]{1,0:T(8,128)(2,1)S(1)} collective-permute-done((bf16[768,768]{1,0:T(8,128)(2,1)S(1)}, bf16[768,768]{1,0:T(8,128)(2,1)S(1)}, u32[]{:S(2)}, u32[]{:S(2)}) %collective-permute-start.14) | collective-permute-done | bytes 1179680 | tf_op jit(solution)/shard_map/ppermute | solution.py:16
  374.9 26.0 %collective-permute-done.15 = bf16[768,768]{1,0:T(8,128)(2,1)S(1)} collective-permute-done((bf16[768,768]{1,0:T(8,128)(2,1)S(1)}, bf16[768,768]{1,0:T(8,128)(2,1)S(1)}, u32[]{:S(2)}, u32[]{:S(2)}) %collective-permute-start.15) | collective-permute-done | bytes 1179680 | tf_op jit(solution)/shard_map/ppermute | solution.py:16
  402.9 24.6 %collective-permute-done.16 = bf16[768,768]{1,0:T(8,128)(2,1)S(1)} collective-permute-done((bf16[768,768]{1,0:T(8,128)(2,1)S(1)}, bf16[768,768]{1,0:T(8,128)(2,1)S(1)}, u32[]{:S(2)}, u32[]{:S(2)}) %collective-permute-start.16) | collective-permute-done | bytes 1179680 | tf_op jit(solution)/shard_map/ppermute | solution.py:16
  427.7 5.3 %collective-permute-start.17 = (bf16[768,768]{1,0:T(8,128)(2,1)S(1)}, bf16[768,768]{1,0:T(8,128)(2,1)S(1)}, u32[]{:S(2)}, u32[]{:S(2)}) collective-permute-start(bf16[768,768]{1,0:T(8,128)(2,1)S(1)} %broadcast_select_fusion.7), channel_id=1, source_target_pairs={{0,14},{1,15},{2,0},{3,1},{4,2},{5,3},{6,4},{7,5},{8,6},{9,7},{10,... | collective-permute-start | bytes 3538952 | tf_op jit(solution)/shard_map/ppermute | solution.py:16
  432.9 23.0 %collective-permute-done.17 = bf16[768,768]{1,0:T(8,128)(2,1)S(1)} collective-permute-done((bf16[768,768]{1,0:T(8,128)(2,1)S(1)}, bf16[768,768]{1,0:T(8,128)(2,1)S(1)}, u32[]{:S(2)}, u32[]{:S(2)}) %collective-permute-start.17) | collective-permute-done | bytes 1179680 | tf_op jit(solution)/shard_map/ppermute | solution.py:16
  456.0 4.3 collective-permute-start.18
  460.3 22.2 %collective-permute-done.18 = bf16[768,768]{1,0:T(8,128)(2,1)S(1)} collective-permute-done((bf16[768,768]{1,0:T(8,128)(2,1)S(1)}, bf16[768,768]{1,0:T(8,128)(2,1)S(1)}, u32[]{:S(2)}, u32[]{:S(2)}) %collective-permute-start.18) | collective-permute-done | bytes 1179680 | tf_op jit(solution)/shard_map/ppermute | solution.py:16
  482.4 4.3 collective-permute-start.19
  490.2 17.8 %collective-permute-done.19 = bf16[768,768]{1,0:T(8,128)(2,1)S(1)} collective-permute-done((bf16[768,768]{1,0:T(8,128)(2,1)S(1)}, bf16[768,768]{1,0:T(8,128)(2,1)S(1)}, u32[]{:S(2)}, u32[]{:S(2)}) %collective-permute-start.19) | collective-permute-done | bytes 1179680 | tf_op jit(solution)/shard_map/ppermute | solution.py:16
  509.4 4.9 collective-permute-start.20
  514.3 2.5 collective-permute-done.20
  (76 shorter events, 39.4 us)
Async XLA Ops:
  21.0 7.8 %copy-start.6 = (s32[96,3]{0,1:T(4,128)S(1)}, s32[96,3]{0,1:T(4,128)}, u32[]{:S(2)}) copy-start(s32[96,3]{0,1:T(4,128)} %param.3) | copy-start | bytes 3460
  21.9 17.1 %all-to-all-start.1 = ((bf16[16,384,48]{1,2,0:T(8,128)(2,1)}), bf16[16,384,48]{1,2,0:T(8,128)(2,1)}, u32[]{:S(2)}, u32[]{:S(2)}) async-start(bf16[16,384,48]{1,2,0:T(8,128)(2,1)} %copy.26), calls=%async_computation.1 | async-start | bytes 1179648 | tf_op jit(solution)/shard_map/all_to_all | solution.py:94
  39.0 14.0 %all-to-all-start.2 = ((bf16[8,96,384]{2,1,0:T(8,128)(2,1)}), bf16[8,96,384]{2,1,0:T(8,128)(2,1)S(1)}, u32[]{:S(2)}, u32[]{:S(2)}) async-start(bf16[8,96,384]{2,1,0:T(8,128)(2,1)} %bitcast.5), calls=%async_computation.2 | async-start | bytes 1179648 | tf_op jit(solution)/shard_map/all_to_all | solution.py:101
  43.1 10.1 %copy-start.2 = (bf16[768,384]{1,0:T(8,128)(2,1)S(1)}, bf16[768,384]{1,0:T(8,128)(2,1)}, u32[]{:S(2)}) copy-start(bf16[768,384]{1,0:T(8,128)(2,1)} %param.2) | copy-start | bytes 1769476
  44.1 9.6 %copy-start = (pred[768,384]{1,0:T(8,128)(4,1)}, pred[768,384]{1,0:T(8,128)(4,1)S(1)}, u32[]{:S(2)}) copy-start(pred[768,384]{1,0:T(8,128)(4,1)S(1)} %broadcast_in_dim.42) | copy-start | bytes 884740
  53.7 3.6 collective-permute-start
  57.6 28.7 %collective-permute-start.4 = (bf16[768,768]{1,0:T(8,128)(2,1)S(1)}, bf16[768,768]{1,0:T(8,128)(2,1)S(1)}, u32[]{:S(2)}, u32[]{:S(2)}) collective-permute-start(bf16[768,768]{1,0:T(8,128)(2,1)S(1)} %maximum_select_fusion), channel_id=1, source_target_pairs={{0,112},{16,0},{32,16},{48,32},{64,48},{80,64},{96,80},{112,96},{1... | collective-permute-start | bytes 3538952 | tf_op jit(solution)/shard_map/ppermute | solution.py:16
  59.6 41.0 %collective-permute-start.1 = (bf16[768,768]{1,0:T(8,128)(2,1)S(1)}, bf16[768,768]{1,0:T(8,128)(2,1)}, u32[]{:S(2)}, u32[]{:S(2)}) collective-permute-start(bf16[768,768]{1,0:T(8,128)(2,1)S(1)} %maximum_select_fusion), channel_id=1, source_target_pairs={{0,14},{1,15},{2,0},{3,1},{4,2},{5,3},{6,4},{7,5},{8,6},{9,7},{10,... | collective-permute-start | bytes 3538952 | tf_op jit(solution)/shard_map/ppermute | solution.py:16
  100.8 27.0 %collective-permute-start.2 = (bf16[768,768]{1,0:T(8,128)(2,1)S(1)}, bf16[768,768]{1,0:T(8,128)(2,1)}, u32[]{:S(2)}, u32[]{:S(2)}) collective-permute-start(bf16[768,768]{1,0:T(8,128)(2,1)S(1)} %get-tuple-element.8), channel_id=1, source_target_pairs={{0,12},{1,13},{2,14},{3,15},{4,0},{5,1},{6,2},{7,3},{8,4},{9,5},{1... | collective-permute-start | bytes 3538952 | tf_op jit(solution)/shard_map/ppermute | solution.py:16
  100.9 29.2 %collective-permute-start.5 = (bf16[768,768]{1,0:T(8,128)(2,1)S(1)}, bf16[768,768]{1,0:T(8,128)(2,1)}, u32[]{:S(2)}, u32[]{:S(2)}) collective-permute-start(bf16[768,768]{1,0:T(8,128)(2,1)S(1)} %get-tuple-element.7), channel_id=1, source_target_pairs={{0,96},{16,112},{32,0},{48,16},{64,32},{80,48},{96,64},{112,80},{1... | collective-permute-start | bytes 3538952 | tf_op jit(solution)/shard_map/ppermute | solution.py:16
  127.9 24.6 %collective-permute-start.3 = (bf16[768,768]{1,0:T(8,128)(2,1)S(1)}, bf16[768,768]{1,0:T(8,128)(2,1)}, u32[]{:S(2)}, u32[]{:S(2)}) collective-permute-start(bf16[768,768]{1,0:T(8,128)(2,1)S(1)} %broadcast_select_fusion.6), channel_id=1, source_target_pairs={{0,8},{1,9},{2,10},{3,11},{4,12},{5,13},{6,14},{7,15},{8,0},{9,1},... | collective-permute-start | bytes 3538952 | tf_op jit(solution)/shard_map/ppermute | solution.py:16
  130.2 41.4 %collective-permute-start.6 = (bf16[768,768]{1,0:T(8,128)(2,1)S(1)}, bf16[768,768]{1,0:T(8,128)(2,1)}, u32[]{:S(2)}, u32[]{:S(2)}) collective-permute-start(bf16[768,768]{1,0:T(8,128)(2,1)S(1)} %broadcast_select_fusion.1), channel_id=1, source_target_pairs={{0,64},{16,80},{32,96},{48,112},{64,0},{80,16},{96,32},{112,48},{1... | collective-permute-start | bytes 3538952 | tf_op jit(solution)/shard_map/ppermute | solution.py:16
  153.9 52.3 %collective-permute-start.7 = (bf16[768,768]{1,0:T(8,128)(2,1)S(1)}, bf16[768,768]{1,0:T(8,128)(2,1)S(1)}, u32[]{:S(2)}, u32[]{:S(2)}) collective-permute-start(bf16[768,768]{1,0:T(8,128)(2,1)S(1)} %broadcast_select_fusion.8), channel_id=1, source_target_pairs={{0,14},{1,15},{2,0},{3,1},{4,2},{5,3},{6,4},{7,5},{8,6},{9,7},{10,... | collective-permute-start | bytes 3538952 | tf_op jit(solution)/shard_map/ppermute | solution.py:16
  173.0 84.9 %copy-start.3 = (bf16[768,768]{1,0:T(8,128)(2,1)}, bf16[768,768]{1,0:T(8,128)(2,1)S(1)}, u32[]{:S(2)}) copy-start(bf16[768,768]{1,0:T(8,128)(2,1)S(1)} %broadcast_select_fusion.2) | copy-start | bytes 3538948
  173.0 38.7 %collective-permute-start.8 = (bf16[768,768]{1,0:T(8,128)(2,1)S(1)}, bf16[768,768]{1,0:T(8,128)(2,1)S(1)}, u32[]{:S(2)}, u32[]{:S(2)}) collective-permute-start(bf16[768,768]{1,0:T(8,128)(2,1)S(1)} %broadcast_select_fusion.2), channel_id=1, source_target_pairs={{0,112},{16,0},{32,16},{48,32},{64,48},{80,64},{96,80},{112,96},{1... | collective-permute-start | bytes 3538952 | tf_op jit(solution)/shard_map/ppermute | solution.py:16
  206.3 38.1 %collective-permute-start.9 = (bf16[768,768]{1,0:T(8,128)(2,1)S(1)}, bf16[768,768]{1,0:T(8,128)(2,1)S(1)}, u32[]{:S(2)}, u32[]{:S(2)}) collective-permute-start(bf16[768,768]{1,0:T(8,128)(2,1)S(1)} %collective-permute-done.7), channel_id=1, source_target_pairs={{0,14},{1,15},{2,0},{3,1},{4,2},{5,3},{6,4},{7,5},{8,6},{9,7},{10,... | collective-permute-start | bytes 3538952 | tf_op jit(solution)/shard_map/ppermute | solution.py:16
  211.8 46.2 %copy-start.7 = (bf16[768,768]{1,0:T(8,128)(2,1)}, bf16[768,768]{1,0:T(8,128)(2,1)S(1)}, u32[]{:S(2)}) copy-start(bf16[768,768]{1,0:T(8,128)(2,1)S(1)} %collective-permute-done.8) | copy-start | bytes 3538948
  211.8 42.0 %collective-permute-start.10 = (bf16[768,768]{1,0:T(8,128)(2,1)S(1)}, bf16[768,768]{1,0:T(8,128)(2,1)S(1)}, u32[]{:S(2)}, u32[]{:S(2)}) collective-permute-start(bf16[768,768]{1,0:T(8,128)(2,1)S(1)} %collective-permute-done.8), channel_id=1, source_target_pairs={{0,112},{16,0},{32,16},{48,32},{64,48},{80,64},{96,80},{112,96},{1... | collective-permute-start | bytes 3538952 | tf_op jit(solution)/shard_map/ppermute | solution.py:16
  244.4 48.9 %collective-permute-start.11 = (bf16[768,768]{1,0:T(8,128)(2,1)S(1)}, bf16[768,768]{1,0:T(8,128)(2,1)S(1)}, u32[]{:S(2)}, u32[]{:S(2)}) collective-permute-start(bf16[768,768]{1,0:T(8,128)(2,1)S(1)} %collective-permute-done.9), channel_id=1, source_target_pairs={{0,14},{1,15},{2,0},{3,1},{4,2},{5,3},{6,4},{7,5},{8,6},{9,7},{10,... | collective-permute-start | bytes 3538952 | tf_op jit(solution)/shard_map/ppermute | solution.py:16
  253.8 5.2 %copy-start.9 = (bf16[768,768]{1,0:T(8,128)(2,1)}, bf16[768,768]{1,0:T(8,128)(2,1)S(1)}, u32[]{:S(2)}) copy-start(bf16[768,768]{1,0:T(8,128)(2,1)S(1)} %collective-permute-done.10) | copy-start | bytes 3538948
  253.8 39.4 %collective-permute-start.12 = (bf16[768,768]{1,0:T(8,128)(2,1)S(1)}, bf16[768,768]{1,0:T(8,128)(2,1)S(1)}, u32[]{:S(2)}, u32[]{:S(2)}) collective-permute-start(bf16[768,768]{1,0:T(8,128)(2,1)S(1)} %collective-permute-done.10), channel_id=1, source_target_pairs={{0,112},{16,0},{32,16},{48,32},{64,48},{80,64},{96,80},{112,96},{1... | collective-permute-start | bytes 3538952 | tf_op jit(solution)/shard_map/ppermute | solution.py:16
  294.4 8.7 %collective-permute-start.13 = (f32[768,768]{1,0:T(8,128)S(1)}, f32[768,768]{1,0:T(8,128)}, u32[]{:S(2)}, u32[]{:S(2)}) collective-permute-start(f32[768,768]{1,0:T(8,128)S(1)} %add_add_fusion.1), channel_id=1, source_target_pairs={{0,1},{1,0},{2,3},{3,2},{4,5},{5,4},{6,7},{7,6},{8,9},{9,8},{10,11... | collective-permute-start | bytes 7077896 | tf_op jit(solution)/shard_map/ppermute | solution.py:22
  305.3 67.2 %collective-permute-start.14 = (bf16[768,768]{1,0:T(8,128)(2,1)S(1)}, bf16[768,768]{1,0:T(8,128)(2,1)S(1)}, u32[]{:S(2)}, u32[]{:S(2)}) collective-permute-start(bf16[768,768]{1,0:T(8,128)(2,1)S(1)} %get-tuple-element.5), channel_id=1, source_target_pairs={{0,14},{1,15},{2,0},{3,1},{4,2},{5,3},{6,4},{7,5},{8,6},{9,7},{10,... | collective-permute-start | bytes 3538952 | tf_op jit(solution)/shard_map/ppermute | solution.py:16
  372.7 28.2 %collective-permute-start.15 = (bf16[768,768]{1,0:T(8,128)(2,1)S(1)}, bf16[768,768]{1,0:T(8,128)(2,1)S(1)}, u32[]{:S(2)}, u32[]{:S(2)}) collective-permute-start(bf16[768,768]{1,0:T(8,128)(2,1)S(1)} %broadcast_select_fusion.3), channel_id=1, source_target_pairs={{0,12},{1,13},{2,14},{3,15},{4,0},{5,1},{6,2},{7,3},{8,4},{9,5},{1... | collective-permute-start | bytes 3538952 | tf_op jit(solution)/shard_map/ppermute | solution.py:16
  401.0 85.7 %copy-start.4 = (bf16[768,768]{1,0:T(8,128)(2,1)S(1)}, bf16[768,768]{1,0:T(8,128)(2,1)}, u32[]{:S(2)}) copy-start(bf16[768,768]{1,0:T(8,128)(2,1)} %copy-done.3) | copy-start | bytes 3538948
  401.0 26.5 %collective-permute-start.16 = (bf16[768,768]{1,0:T(8,128)(2,1)S(1)}, bf16[768,768]{1,0:T(8,128)(2,1)S(1)}, u32[]{:S(2)}, u32[]{:S(2)}) collective-permute-start(bf16[768,768]{1,0:T(8,128)(2,1)S(1)} %broadcast_select_fusion.5), channel_id=1, source_target_pairs={{0,8},{1,9},{2,10},{3,11},{4,12},{5,13},{6,14},{7,15},{8,0},{9,1},... | collective-permute-start | bytes 3538952 | tf_op jit(solution)/shard_map/ppermute | solution.py:16
  427.6 60.2 %copy-start.8 = (bf16[768,768]{1,0:T(8,128)(2,1)S(1)}, bf16[768,768]{1,0:T(8,128)(2,1)}, u32[]{:S(2)}) copy-start(bf16[768,768]{1,0:T(8,128)(2,1)} %copy-done.7) | copy-start | bytes 3538948
  427.7 28.3 %collective-permute-start.17 = (bf16[768,768]{1,0:T(8,128)(2,1)S(1)}, bf16[768,768]{1,0:T(8,128)(2,1)S(1)}, u32[]{:S(2)}, u32[]{:S(2)}) collective-permute-start(bf16[768,768]{1,0:T(8,128)(2,1)S(1)} %broadcast_select_fusion.7), channel_id=1, source_target_pairs={{0,14},{1,15},{2,0},{3,1},{4,2},{5,3},{6,4},{7,5},{8,6},{9,7},{10,... | collective-permute-start | bytes 3538952 | tf_op jit(solution)/shard_map/ppermute | solution.py:16
  456.0 26.5 %collective-permute-start.18 = (bf16[768,768]{1,0:T(8,128)(2,1)S(1)}, bf16[768,768]{1,0:T(8,128)(2,1)S(1)}, u32[]{:S(2)}, u32[]{:S(2)}) collective-permute-start(bf16[768,768]{1,0:T(8,128)(2,1)S(1)} %collective-permute-done.17), channel_id=1, source_target_pairs={{0,14},{1,15},{2,0},{3,1},{4,2},{5,3},{6,4},{7,5},{8,6},{9,7},{10,... | collective-permute-start | bytes 3538952 | tf_op jit(solution)/shard_map/ppermute | solution.py:16
  482.4 25.6 %collective-permute-start.19 = (bf16[768,768]{1,0:T(8,128)(2,1)S(1)}, bf16[768,768]{1,0:T(8,128)(2,1)S(1)}, u32[]{:S(2)}, u32[]{:S(2)}) collective-permute-start(bf16[768,768]{1,0:T(8,128)(2,1)S(1)} %collective-permute-done.18), channel_id=1, source_target_pairs={{0,14},{1,15},{2,0},{3,1},{4,2},{5,3},{6,4},{7,5},{8,6},{9,7},{10,... | collective-permute-start | bytes 3538952 | tf_op jit(solution)/shard_map/ppermute | solution.py:16
  509.2 7.6 %copy-start.1 = (pred[768,384]{1,0:T(8,128)(4,1)S(1)}, pred[768,384]{1,0:T(8,128)(4,1)}, u32[]{:S(2)}) copy-start(pred[768,384]{1,0:T(8,128)(4,1)} %copy-done) | copy-start | bytes 884740
  509.4 7.4 %collective-permute-start.20 = (f32[768,384]{1,0:T(8,128)S(1)}, f32[768,384]{1,0:T(8,128)S(1)}, u32[]{:S(2)}, u32[]{:S(2)}) collective-permute-start(f32[768,384]{1,0:T(8,128)S(1)} %slice_select_fusion.1), channel_id=1, source_target_pairs={{0,1},{1,0},{2,3},{3,2},{4,5},{5,4},{6,7},{7,6},{8,9},{9,8},{10,11... | collective-permute-start | bytes 3538952 | tf_op jit(solution)/shard_map/ppermute | solution.py:22
  (2 other events, 2.3 us)
where the time goes:
time: 519 us; the launch traced here: 518 us
  waiting for transfers between devices  339 us (65%)
  starting transfers between devices  131 us (25%)
  blocking collectives  19.3 us (4%)
  local copies, waits for them, and re-layouts  11.5 us (2%)
  matrix products  8.84 us (2%)
  other arithmetic  8.33 us (2%)
    ppermute x18, waiting for transfers between devices, shifted_2(): lax.ppermute(array, axis, [(i, (i + by) % length) for i in range(length)])  316 us
    ppermute x18, starting transfers between devices, shifted_2(): lax.ppermute(array, axis, [(i, (i + by) % length) for i in range(length)])  111 us
    all_to_all x1, blocking collectives, per_device(): lax.all_to_all(upper_stored, 'row', split_axis=1, concat_axis=0, tiled=True)  19.3 us
  transfers between devices with their start and end apart: 23, of which 18 were waited for; matrix products, arithmetic and copies ran while one was open for 3% of the time, Pallas kernels for 0%

commit v1 on v0

v1 whole, which is shorter than its diff:
```python
import math

import jax
import jax.numpy as jnp
from jax import lax
from jax.sharding import PartitionSpec as P

BLK = 64
BOX = 16
NEAR = 40
FAR = 90


def cell_mask(block_cells, row_start, row_count, col_start, col_count, bound_sq):
    row_cells = lax.dynamic_slice_in_dim(block_cells, row_start, row_count, 0)
    col_cells = lax.dynamic_slice_in_dim(block_cells, col_start, col_count, 0)
    offset_abs = jnp.abs(row_cells[:, None, :] - col_cells[None, :, :])
    wrapped = jnp.minimum(offset_abs, BOX - offset_abs)
    return jnp.sum(wrapped * wrapped, axis=2) <= bound_sq


def block_keep(matrix_tile, keep_mask):
    row_count, col_count = matrix_tile.shape
    row_blocks, col_blocks = keep_mask.shape
    shaped = matrix_tile.reshape(
        row_blocks, row_count // row_blocks, col_blocks, col_count // col_blocks
    )
    kept = jnp.where(keep_mask[:, None, :, None], shaped, jnp.zeros_like(shaped))
    return kept.reshape(row_count, col_count)


def mirror_tile(upper_stored, rows, cols):
    tile_side, half_width = upper_stored.shape
    row_id = lax.axis_index("row")
    col_id = lax.axis_index("col")
    pieces = []
    for k in range(2):
        half = (col_id + k) % 2
        piece = lax.dynamic_slice_in_dim(upper_stored, half * half_width, half_width, 0)
        pairs = []
        for a in range(rows):
            for b in range(cols):
                h = (b + k) % 2
                pairs.append((a * cols + b, (b // 2) * cols + 2 * a + h))
        pieces.append(lax.ppermute(piece, ("row", "col"), pairs))
    h_own = col_id % 2
    first = jnp.where(h_own == 0, pieces[0], pieces[1])
    second = jnp.where(h_own == 0, pieces[1], pieces[0])
    return jnp.concatenate([first, second], 1).T


def per_device(upper_stored, block_cells):
    rows = lax.axis_size("row")
    cols = lax.axis_size("col")
    row_id = lax.axis_index("row")
    col_id = lax.axis_index("col")
    tile_side, half_width = upper_stored.shape
    order_total = tile_side * rows
    tile_blocks = tile_side // BLK
    half_blocks = half_width // BLK
    mirrored = mirror_tile(upper_stored, rows, cols)
    global_rows = row_id * tile_side + lax.broadcasted_iota(jnp.int32, (tile_side, half_width), 0)
    global_cols = col_id * half_width + lax.broadcasted_iota(jnp.int32, (tile_side, half_width), 1)
    symmetric = jnp.where(global_rows <= global_cols, upper_stored, mirrored)
    near_own = cell_mask(
        block_cells, row_id * tile_blocks, tile_blocks, col_id * half_blocks, half_blocks, NEAR
    )
    far_own = cell_mask(
        block_cells, row_id * tile_blocks, tile_blocks, col_id * half_blocks, half_blocks, FAR
    )
    diagonal = jnp.where(global_rows == global_cols, 0.5, 0.0).astype(jnp.float32)
    value_scale = 2.0 / math.sqrt(order_total)
    density = block_keep(
        diagonal + value_scale * symmetric.astype(jnp.float32), near_own
    ).astype(jnp.bfloat16)
    row_panel = lax.all_gather(density, "col", axis=1, tiled=True)
    col_panel = lax.all_gather(density, "row", axis=0, tiled=True)
    square = block_keep(
        jnp.dot(row_panel, col_panel, preferred_element_type=jnp.float32), far_own
    )
    square_low = square.astype(jnp.bfloat16)
    low_panel = lax.all_gather(square_low, "col", axis=1, tiled=True)
    cubic = jnp.dot(low_panel, col_panel, preferred_element_type=jnp.float32)
    return block_keep(3.0 * square - 2.0 * cubic, near_own).astype(jnp.bfloat16)


def solution(mesh):
    return jax.shard_map(
        per_device,
        mesh=mesh,
        in_specs=(P("row", "col"), P()),
        out_specs=P("row", "col"),
        check_vma=False,
    )
```

time: 519 us -> 260 us (0.50)
  starting transfers between devices: 131 us -> 2.22 us
  waiting for transfers between devices: 339 us -> 218 us
  blocking collectives: 19.3 us -> 0 us
  between operations: 0.32 us -> 13.2 us
  matrix products: 8.84 us -> 19.4 us
  other arithmetic: 8.33 us -> 1.5 us
  local copies, waits for them, and re-layouts: 11.5 us -> 5.25 us
    ppermute x21 -> x2, waiting for transfers between devices: 320 us -> 0.01 us  [mirror_tile(): pieces.append(lax.ppermute(piece, ('row', 'col'), pairs))]
    all_gather x0 -> x3, waiting for transfers between devices: none -> 218 us  [the longest x1 102 us: per_device(): col_panel = lax.all_gather(density, 'row', axis=0, tiled=True)]
    ppermute x21 -> x2, starting transfers between devices: 120 us -> 2.14 us  [mirror_tile(): pieces.append(lax.ppermute(piece, ('row', 'col'), pairs))]
    all_to_all x1 -> x0, blocking collectives: 19.3 us -> none  [per_device(): lax.all_to_all(upper_stored, 'row', split_axis=1, concat_axis=0, tiled=True)]
    all_to_all x2 -> x0, waiting for transfers between devices: 19 us -> none  [the longest x1 10.1 us: per_device(): lax.all_to_all(lax.all_to_all(upper_stored, 'row', split_axis=1, concat_a...]
    dot_general x8 -> x2, matrix products: 8.84 us -> 19.4 us  [the longest x1 9.75 us: per_device(): cubic = jnp.dot(low_panel, col_panel, preferred_element_type=jnp.float32)]
    all_to_all x2 -> x0, starting transfers between devices: 10.4 us -> none  [the longest x1 6.84 us: per_device(): lax.all_to_all(lax.all_to_all(upper_stored, 'row', split_axis=1, concat_a...]
  transfers between devices with their start and end apart: 23 -> 5, of which waited for: 18 -> 3; matrix products, arithmetic and copies ran while one was open for 3% -> 2% of each run, Pallas kernels for 0% -> 0%
where the time goes in v1:
time: 260 us
  waiting for transfers between devices  218 us (84%)
  matrix products  19.4 us (7%)
  between operations  13.2 us (5%)
  local copies, waits for them, and re-layouts  5.25 us (2%)
    all_gather x1, waiting for transfers between devices, per_device(): col_panel = lax.all_gather(density, 'row', axis=0, tiled=True)  102 us
    all_gather x1, waiting for transfers between devices, per_device(): low_panel = lax.all_gather(square_low, 'col', axis=1, tiled=True)  58 us
    all_gather x1, waiting for transfers between devices, per_device(): row_panel = lax.all_gather(density, 'col', axis=1, tiled=True)  57.4 us
    dot_general x1, matrix products, per_device(): cubic = jnp.dot(low_panel, col_panel, preferred_element_type=jnp.float32)  9.75 us
    dot_general x1, matrix products, per_device(): jnp.dot(row_panel, col_panel, preferred_element_type=jnp.float32)  9.69 us
  transfers between devices with their start and end apart: 5, of which 3 were waited for; matrix products, arithmetic and copies ran while one was open for 2% of the time, Pallas kernels for 0%

profile of v1, /device:TPU:1, one launch (start us, length us, event | category | flops | bytes accessed | tf_op | source)
XLA Modules:
  0.0 260.0 jit_solution(1769030043585015134)
XLA Ops:
  6.5 0.0 copy-start
  6.5 0.0 all-gather.6.cloned.1.call-start
  6.5 1.1 constant_dynamic-slice_fusion.1
  7.7 0.2 copy.16
  7.9 1.5 collective-permute-start.1
  9.3 0.2 copy.15
  9.6 0.7 collective-permute-start
  10.3 0.1 constant_dynamic-slice_fusion.2
  10.3 0.1 constant_dynamic-slice_fusion.3
  10.4 0.1 fusion.4
  10.5 0.1 copy.11
  10.6 0.3 broadcast_in_dim.35
  10.9 0.0 copy-start.1
  10.9 1.4 broadcast_in_dim.36
  12.3 0.0 collective-permute-done.1
  12.3 0.0 collective-permute-done
  12.4 0.1 broadcast_select_fusion.1
  12.4 0.0 copy-done.1
  12.4 1.3 select_convert_fusion
  13.8 0.0 all-gather.6.cloned.1.call-update
  13.8 0.0 all-gather.4.cloned.1.call-start
  13.9 0.7 all-gather.4.cloned.1.call-update
  14.6 0.0 all-gather.8.cloned.1.call-start
  14.6 0.1 copy.12
  14.7 0.3 broadcast_in_dim.37
  15.0 1.4 broadcast_in_dim.38
  16.4 102.2 %all-gather.6.cloned.1.call-done = bf16[6144,384]{1,0:T(8,128)(2,1)} async-done(((bf16[768,384]{1,0:T(8,128)(2,1)}), bf16[6144,384]{1,0:T(8,128)(2,1)}) %all-gather.6.cloned.1.call-update) | async-done | bytes 4718608 | tf_op jit(solution)/shard_map/all_gather | solution.py:77
  118.6 57.4 %all-gather.4.cloned.1.call-done = bf16[768,6144]{1,0:T(8,128)(2,1)} async-done(((bf16[768,384]{1,0:T(8,128)(2,1)}), bf16[768,6144]{1,0:T(8,128)(2,1)}) %all-gather.4.cloned.1.call-update) | async-done | bytes 9437200 | tf_op jit(solution)/shard_map/all_gather | solution.py:76
  176.0 9.7 %fusion.5 = (bf16[768,384]{1,0:T(8,128)(2,1)}, f32[768,384]{1,0:T(8,128)S(1)}) fusion(pred[768,384]{1,0:T(32,128)(4,1)S(1)} %broadcast_in_dim.38, bf16[768,6144]{1,0:T(8,128)(2,1)} %all-gather.4.cloned.1.call-done, bf16[6144,384]{1,0:T(8,128)(2,1)} %all-gather.6.cloned.1.call-done), kind=kOutput, calls=%fused_computation.21 | convolution fusion | flops 3624468480 | bytes 16220160 | tf_op jit(solution)/shard_map/dot_general | solution.py:79
  185.7 0.0 all-gather.8.cloned.1.call-update
  185.7 58.0 %all-gather.8.cloned.1.call-done = bf16[768,6144]{1,0:T(8,128)(2,1)} async-done(((bf16[768,384]{1,0:T(8,128)(2,1)}), bf16[768,6144]{1,0:T(8,128)(2,1)}) %all-gather.8.cloned.1.call-update) | async-done | bytes 9437200 | tf_op jit(solution)/shard_map/all_gather | solution.py:82
  243.7 9.7 %fusion.2 = bf16[768,384]{1,0:T(8,128)(2,1)} fusion(pred[768,384]{1,0:T(32,128)(4,1)S(1)} %broadcast_in_dim.36, bf16[768,6144]{1,0:T(8,128)(2,1)} %all-gather.8.cloned.1.call-done, bf16[6144,384]{1,0:T(8,128)(2,1)} %all-gather.6.cloned.1.call-done, f32[768,384]{1,0:T(8,128)S(1)} %get-tuple-element.12), kind=kOutput, calls=%fused_computation.4 | convolution fusion | flops 3625353216 | bytes 16220160 | tf_op jit(solution)/shard_map/dot_general | solution.py:83
  (4 shorter events, 0.0 us)
Async XLA Ops:
  6.5 3.7 %copy-start = (s32[96,3]{0,1:T(4,128)S(1)}, s32[96,3]{0,1:T(4,128)}, u32[]{:S(2)}) copy-start(s32[96,3]{0,1:T(4,128)} %param.3) | copy-start | bytes 3460
  6.5 112.0 %all-gather.6.cloned.1.call-start = ((), (), s32[]{:S(2)}) async-start(), calls=%async_computation.1 | async-start | bytes 5308416 | tf_op jit(solution)/shard_map/all_gather | solution.py:77
  7.9 4.5 %collective-permute-start.1 = (bf16[384,384]{0,1:T(8,128)(2,1)S(1)}, bf16[384,384]{0,1:T(8,128)(2,1)S(1)}, u32[]{:S(2)}, u32[]{:S(2)}) collective-permute-start(bf16[384,384]{0,1:T(8,128)(2,1)S(1)} %copy.16), channel_id=1, source_target_pairs={{0,1},{1,0},{2,17},{3,16},{4,33},{5,32},{6,49},{7,48},{8,65},{9,64... | collective-permute-start | bytes 884744 | tf_op jit(solution)/shard_map/ppermute | solution.py:45
  9.6 2.8 %collective-permute-start = (bf16[384,384]{0,1:T(8,128)(2,1)S(1)}, bf16[384,384]{0,1:T(8,128)(2,1)S(1)}, u32[]{:S(2)}, u32[]{:S(2)}) collective-permute-start(bf16[384,384]{0,1:T(8,128)(2,1)S(1)} %copy.15), channel_id=1, source_target_pairs={{0,0},{1,1},{2,16},{3,17},{4,32},{5,33},{6,48},{7,49},{8,64},{9,65... | collective-permute-start | bytes 884744 | tf_op jit(solution)/shard_map/ppermute | solution.py:45
  10.9 1.5 copy-start.1
  13.8 162.2 %all-gather.4.cloned.1.call-start = ((), (), s32[]{:S(2)}) async-start(), calls=%async_computation | async-start | bytes 10027008 | tf_op jit(solution)/shard_map/all_gather | solution.py:76
  14.6 229.1 %all-gather.8.cloned.1.call-start = ((), (), s32[]{:S(2)}) async-start(), calls=%async_computation.2 | async-start | bytes 10027008 | tf_op jit(solution)/shard_map/all_gather | solution.py:82
Sparse Core Ops, SparseCore 0:
  13.9 104.6 all-gather.5
  120.2 55.7 all-gather.3
  185.9 57.7 all-gather.7

commit v2 on v1

--- a/solution.py
+++ b/solution.py
@@ -3,6 +3,7 @@
 import jax
 import jax.numpy as jnp
 from jax import lax
+from jax.sharding import Mesh
 from jax.sharding import PartitionSpec as P
 
 BLK = 64
@@ -29,10 +30,29 @@
     return kept.reshape(row_count, col_count)
 
 
+ROW = ("y", "zh")
+COL = ("zl", "x", "core")
+
+
+def column_panel(tile):
+    partner = lax.ppermute(tile, "zh", [(0, 1), (1, 0)])
+    zh_id = lax.axis_index("zh")
+    pair = jnp.where(zh_id == 0, jnp.concatenate([tile, partner], 0), jnp.concatenate([partner, tile], 0))
+    ring = lax.axis_size("y")
+    from_below = lax.ppermute(pair, "y", [(i, (i + 1) % ring) for i in range(ring)])
+    from_above = lax.ppermute(pair, "y", [(i, (i - 1) % ring) for i in range(ring)])
+    from_two_below = lax.ppermute(from_below, "y", [(i, (i + 1) % ring) for i in range(ring)])
+    y_id = lax.axis_index("y")
+    panel = jnp.zeros((ring,) + pair.shape, pair.dtype)
+    for offset, part in ((0, pair), (-1, from_below), (-2, from_two_below), (1, from_above)):
+        panel = lax.dynamic_update_index_in_dim(panel, part, (y_id + offset) % ring, 0)
+    return panel.reshape(ring * pair.shape[0], pair.shape[1])
+
+
 def mirror_tile(upper_stored, rows, cols):
     tile_side, half_width = upper_stored.shape
-    row_id = lax.axis_index("row")
-    col_id = lax.axis_index("col")
+    row_id = lax.axis_index(ROW)
+    col_id = lax.axis_index(COL)
     pieces = []
     for k in range(2):
         half = (col_id + k) % 2
@@ -42,7 +62,7 @@
             for b in range(cols):
                 h = (b + k) % 2
                 pairs.append((a * cols + b, (b // 2) * cols + 2 * a + h))
-        pieces.append(lax.ppermute(piece, ("row", "col"), pairs))
+        pieces.append(lax.ppermute(piece, ROW + COL, pairs))
     h_own = col_id % 2
     first = jnp.where(h_own == 0, pieces[0], pieces[1])
     second = jnp.where(h_own == 0, pieces[1], pieces[0])
@@ -50,10 +70,10 @@
 
 
 def per_device(upper_stored, block_cells):
-    rows = lax.axis_size("row")
-    cols = lax.axis_size("col")
-    row_id = lax.axis_index("row")
-    col_id = lax.axis_index("col")
+    rows = lax.axis_size(ROW)
+    cols = lax.axis_size(COL)
+    row_id = lax.axis_index(ROW)
+    col_id = lax.axis_index(COL)
     tile_side, half_width = upper_stored.shape
     order_total = tile_side * rows
     tile_blocks = tile_side // BLK
@@ -73,22 +93,25 @@
     density = block_keep(
         diagonal + value_scale * symmetric.astype(jnp.float32), near_own
     ).astype(jnp.bfloat16)
-    row_panel = lax.all_gather(density, "col", axis=1, tiled=True)
-    col_panel = lax.all_gather(density, "row", axis=0, tiled=True)
+    row_panel = lax.all_gather(density, COL, axis=1, tiled=True)
+    col_panel = column_panel(density)
     square = block_keep(
         jnp.dot(row_panel, col_panel, preferred_element_type=jnp.float32), far_own
     )
     square_low = square.astype(jnp.bfloat16)
-    low_panel = lax.all_gather(square_low, "col", axis=1, tiled=True)
+    low_panel = lax.all_gather(square_low, COL, axis=1, tiled=True)
     cubic = jnp.dot(low_panel, col_panel, preferred_element_type=jnp.float32)
     return block_keep(3.0 * square - 2.0 * cubic, near_own).astype(jnp.bfloat16)
 
 
 def solution(mesh):
+    y_size = mesh.devices.shape[0] // 2
+    x_size = mesh.devices.shape[1] // 4
+    split_mesh = Mesh(mesh.devices.reshape(y_size, 2, 2, x_size, 2), ROW + COL)
     return jax.shard_map(
         per_device,
-        mesh=mesh,
-        in_specs=(P("row", "col"), P()),
-        out_specs=P("row", "col"),
+        mesh=split_mesh,
+        in_specs=(P(ROW, COL), P()),
+        out_specs=P(ROW, COL),
         check_vma=False,
     )

time: 260 us -> 225 us (0.87)
  waiting for transfers between devices: 218 us -> 121 us
  starting transfers between devices: 2.22 us -> 38.6 us
  local copies, waits for them, and re-layouts: 5.25 us -> 24.9 us
  other arithmetic: 1.5 us -> 4.91 us
  matrix products: 19.4 us -> 22.4 us
    all_gather x3 -> x2, waiting for transfers between devices: 218 us -> 60.5 us  [the longest x1 60.5 us: per_device(): low_panel = lax.all_gather(square_low, COL, axis=1, tiled=True)]
    ppermute x2 -> x6, waiting for transfers between devices: 0.01 us -> 60.2 us  [the longest x1 25.2 us: column_panel(): lax.ppermute(pair, 'y', [(i, (i + 1) % ring) for i in range(ring)])]
    ppermute x2 -> x6, starting transfers between devices: 2.14 us -> 38.5 us  [the longest x1 22.1 us: column_panel(): partner = lax.ppermute(tile, 'zh', [(0, 1), (1, 0)])]
    dot_general x0 -> x1, local copies, waits for them, and re-layouts: none -> 6.69 us  [per_device(): jnp.dot(row_panel, col_panel, preferred_element_type=jnp.float32)]
    dynamic_update_slice x0 -> x3, local copies, waits for them, and re-layouts: none -> 4.74 us  [column_panel(): lax.dynamic_update_index_in_dim(panel, part, (y_id + offset) % ring, 0)]
    mul x0 -> x2, local copies, waits for them, and re-layouts: none -> 4.74 us  [per_device(): return block_keep(3.0 * square - 2.0 * cubic, near_own).astype(jnp.bfloat16)]
    dot_general x1, matrix products: 9.69 us -> 12.5 us  [per_device(): jnp.dot(row_panel, col_panel, preferred_element_type=jnp.float32)]
    convert_element_type x0 -> x2, local copies, waits for them, and re-layouts: none -> 2.62 us  [per_device(): square_low = square.astype(jnp.bfloat16)]
  transfers between devices with their start and end apart: 5 -> 8, of which waited for: 3 -> 4; matrix products, arithmetic and copies ran while one was open for 2% -> 11% of each run, Pallas kernels for 0% -> 0%
where the time goes in v2:
time: 225 us
  waiting for transfers between devices  121 us (54%)
  starting transfers between devices  38.6 us (17%)
  local copies, waits for them, and re-layouts  24.9 us (11%)
  matrix products  22.4 us (10%)
  between operations  13.5 us (6%)
  other arithmetic  4.91 us (2%)
    all_gather x1, waiting for transfers between devices, per_device(): low_panel = lax.all_gather(square_low, COL, axis=1, tiled=True)  60.5 us
    ppermute x1, waiting for transfers between devices, column_panel(): lax.ppermute(pair, 'y', [(i, (i + 1) % ring) for i in range(ring)])  25.2 us
    ppermute x1, starting transfers between devices, column_panel(): partner = lax.ppermute(tile, 'zh', [(0, 1), (1, 0)])  22.1 us
    ppermute x1, waiting for transfers between devices, column_panel(): partner = lax.ppermute(tile, 'zh', [(0, 1), (1, 0)])  17.7 us
    ppermute x1, waiting for transfers between devices, column_panel(): lax.ppermute(from_below, 'y', [(i, (i + 1) % ring) for i in range(ring)])  17.2 us
    dot_general x1, matrix products, per_device(): jnp.dot(row_panel, col_panel, preferred_element_type=jnp.float32)  12.5 us
    ppermute x1, starting transfers between devices, column_panel(): lax.ppermute(pair, 'y', [(i, (i + 1) % ring) for i in range(ring)])  11.5 us
    dot_general x1, matrix products, per_device(): cubic = jnp.dot(low_panel, col_panel, preferred_element_type=jnp.float32)  9.9 us
  transfers between devices with their start and end apart: 8, of which 4 were waited for; matrix products, arithmetic and copies ran while one was open for 11% of the time, Pallas kernels for 0%

profile of v2, /device:TPU:1, one launch (start us, length us, event | category | flops | bytes accessed | tf_op | source)
XLA Modules:
  0.0 225.0 jit_solution(16357479815874871506)
XLA Ops:
  6.5 1.1 constant_dynamic-slice_fusion.1
  7.7 0.2 copy.29
  7.9 0.7 collective-permute-start
  8.6 0.2 copy.30
  8.8 1.5 collective-permute-start.1
  10.4 0.1 fusion.5
  10.5 0.1 copy.21
  10.6 0.3 broadcast_in_dim.47
  10.9 1.4 broadcast_in_dim.48
  12.4 1.3 select_convert_fusion.1
  13.8 22.1 %collective-permute-start.2 = (bf16[768,384]{1,0:T(8,128)(2,1)}, bf16[768,384]{1,0:T(8,128)(2,1)S(1)}, u32[]{:S(2)}, u32[]{:S(2)}) collective-permute-start(bf16[768,384]{1,0:T(8,128)(2,1)} %select_convert_fusion.1), channel_id=1, source_target_pairs={{0,16},{16,0},{1,17},{17,1},{2,18},{18,2},{3,19},{19,3},{4,20},{20... | collective-permute-start | bytes 1769480 | tf_op jit(solution)/shard_map/ppermute | solution.py:38
  35.9 17.7 %collective-permute-done.2 = bf16[768,384]{1,0:T(8,128)(2,1)S(1)} collective-permute-done((bf16[768,384]{1,0:T(8,128)(2,1)}, bf16[768,384]{1,0:T(8,128)(2,1)S(1)}, u32[]{:S(2)}, u32[]{:S(2)}) %collective-permute-start.2) | collective-permute-done | bytes 589856 | tf_op jit(solution)/shard_map/ppermute | solution.py:38
  53.6 1.7 maximum_select_fusion.1
  55.3 11.5 %collective-permute-start.3 = (bf16[1536,384]{1,0:T(8,128)(2,1)S(1)}, bf16[1536,384]{1,0:T(8,128)(2,1)S(1)}, u32[]{:S(2)}, u32[]{:S(2)}) collective-permute-start(bf16[1536,384]{1,0:T(8,128)(2,1)S(1)} %maximum_select_fusion.1), channel_id=1, source_target_pairs={{0,32},{32,64},{64,96},{96,0},{1,33},{33,65},{65,97},{97,1},{2,34}... | collective-permute-start | bytes 3538952 | tf_op jit(solution)/shard_map/ppermute | solution.py:42
  66.8 25.2 %collective-permute-done.3 = bf16[1536,384]{1,0:T(8,128)(2,1)S(1)} collective-permute-done((bf16[1536,384]{1,0:T(8,128)(2,1)S(1)}, bf16[1536,384]{1,0:T(8,128)(2,1)S(1)}, u32[]{:S(2)}, u32[]{:S(2)}) %collective-permute-start.3) | collective-permute-done | bytes 1179680 | tf_op jit(solution)/shard_map/ppermute | solution.py:42
  92.0 0.1 copy.22
  92.1 2.9 %collective-permute-start.5 = (bf16[1536,384]{1,0:T(8,128)(2,1)S(1)}, bf16[1536,384]{1,0:T(8,128)(2,1)S(1)}, u32[]{:S(2)}, u32[]{:S(2)}) collective-permute-start(bf16[1536,384]{1,0:T(8,128)(2,1)S(1)} %maximum_select_fusion.1), channel_id=1, source_target_pairs={{0,96},{32,0},{64,32},{96,64},{1,97},{33,1},{65,33},{97,65},{2,98}... | collective-permute-start | bytes 3538952 | tf_op jit(solution)/shard_map/ppermute | solution.py:43
  95.0 2.5 %broadcast_in_dim.52 = bf16[4,1536,384]{2,1,0:T(8,128)(2,1)} broadcast(bf16[]{:T(256)} %constant.100.clone.1), dimensions={} | broadcast | bytes 4718594 | tf_op jit(solution)/shard_map/broadcast_in_dim | solution.py:46
  97.5 1.4 fusion.3
  98.9 1.2 bitcast_dynamic-update-slice_fusion.2
  100.1 17.2 %collective-permute-done.4 = bf16[1536,384]{1,0:T(8,128)(2,1)} collective-permute-done((bf16[1536,384]{1,0:T(8,128)(2,1)S(1)}, bf16[1536,384]{1,0:T(8,128)(2,1)}, u32[]{:S(2)}, u32[]{:S(2)}) %collective-permute-start.4) | collective-permute-done | bytes 1179680 | tf_op jit(solution)/shard_map/ppermute | solution.py:44
  117.3 2.4 %bitcast_dynamic-update-slice_fusion.1 = bf16[4,1536,384]{2,1,0:T(8,128)(2,1)} fusion(bf16[4,1536,384]{2,1,0:T(8,128)(2,1)} %bitcast_dynamic-update-slice_fusion.2, s32[]{:T(128)S(6)} %select_n.128, bf16[1536,384]{1,0:T(8,128)(2,1)} %collective-permute-done.4), kind=kLoop, calls=%fused_computation.10 | loop fusion | bytes 2359300 | tf_op jit(solution)/shard_map/jit(dynamic_update_index_in_dim)/dynamic_update_slice | solution.py:48
  119.7 1.2 bitcast_dynamic-update-slice_fusion
  120.9 6.7 %copy.25 = bf16[384,6144]{1,0:T(8,128)(2,1)} copy(bf16[384,6144]{0,1:T(8,128)(2,1)} %bitcast.10) | data formatting | bytes 9437184 | tf_op jit(solution)/shard_map/dot_general | solution.py:99
  127.6 12.5 %select_multiply_fusion = (f32[12,64,6,64]{3,1,2,0:T(8,128)}, bf16[12,64,6,64]{3,1,2,0:T(8,128)(2,1)S(1)}) fusion(pred[12,6]{1,0:T(8,128)(4,1)S(1)} %copy.22, bf16[12,64,6144,1]{2,1,3,0:T(8,128)(2,1)} %bitcast.30, bf16[6,64,6144,1]{2,1,0,3:T(8,128)(2,1)} %bitcast.28), kind=kOutput, calls=%fused_computation.1 | convolution fusion | flops 3624763392 | bytes 15925320 | tf_op jit(solution)/shard_map/dot_general | solution.py:99
  140.1 0.3 select_convert_fusion
  140.4 0.9 copy.27
  141.3 1.7 convert_element_type.18
  143.1 3.1 %copy.26 = f32[12,64,6,64]{3,2,1,0:T(8,128)S(1)} copy(f32[12,64,6,64]{3,1,2,0:T(8,128)} %get-tuple-element.11) | data formatting | bytes 2359296 | tf_op jit(solution)/shard_map/mul | solution.py:104
  146.2 1.6 mul.70
  147.8 60.5 %all-gather.5.cloned.1.call-done = bf16[768,6144]{1,0:T(8,128)(2,1)} async-done(((bf16[768,384]{1,0:T(8,128)(2,1)}), bf16[768,6144]{1,0:T(8,128)(2,1)}) %all-gather.5.cloned.1.call-update) | async-done | bytes 9437200 | tf_op jit(solution)/shard_map/all_gather | solution.py:102
  208.3 9.9 %fusion.2 = bf16[768,384]{1,0:T(8,128)(2,1)} fusion(pred[768,384]{1,0:T(32,128)(4,1)S(1)} %broadcast_in_dim.48, f32[768,384]{1,0:T(8,128)} %mul.70, bf16[768,6144]{1,0:T(8,128)(2,1)} %all-gather.5.cloned.1.call-done, bf16[6144,384]{1,0:T(8,128)(2,1)} %bitcast.9), kind=kOutput, calls=%fused_computation.5 | convolution fusion | flops 3625058304 | bytes 16220160 | tf_op jit(solution)/shard_map/dot_general | solution.py:103
  (21 shorter events, 0.3 us)
Async XLA Ops:
  6.5 3.7 %copy-start = (s32[96,3]{0,1:T(4,128)S(1)}, s32[96,3]{0,1:T(4,128)}, u32[]{:S(2)}) copy-start(s32[96,3]{0,1:T(4,128)} %param.3) | copy-start | bytes 3460
  6.5 121.0 %all-gather.3.cloned.1.call-start = ((), (), s32[]{:S(2)}) async-start(), calls=%async_computation | async-start | bytes 10027008 | tf_op jit(solution)/shard_map/all_gather | solution.py:96
  7.7 4.8 %copy-start.2 = (bf16[768,384]{1,0:T(8,128)(2,1)S(1)}, bf16[768,384]{1,0:T(8,128)(2,1)}, u32[]{:S(2)}) copy-start(bf16[768,384]{1,0:T(8,128)(2,1)} %param.2) | copy-start | bytes 1769476
  7.9 4.4 %collective-permute-start = (bf16[384,384]{0,1:T(8,128)(2,1)S(1)}, bf16[384,384]{0,1:T(8,128)(2,1)S(1)}, u32[]{:S(2)}, u32[]{:S(2)}) collective-permute-start(bf16[384,384]{0,1:T(8,128)(2,1)S(1)} %copy.29), channel_id=1, source_target_pairs={{0,0},{1,1},{2,16},{3,17},{4,32},{5,33},{6,48},{7,49},{8,64},{9,65... | collective-permute-start | bytes 884744 | tf_op jit(solution)/shard_map/ppermute | solution.py:65
  8.8 3.5 %collective-permute-start.1 = (bf16[384,384]{0,1:T(8,128)(2,1)S(1)}, bf16[384,384]{0,1:T(8,128)(2,1)S(1)}, u32[]{:S(2)}, u32[]{:S(2)}) collective-permute-start(bf16[384,384]{0,1:T(8,128)(2,1)S(1)} %copy.30), channel_id=1, source_target_pairs={{0,1},{1,0},{2,17},{3,16},{4,33},{5,32},{6,49},{7,48},{8,65},{9,64... | collective-permute-start | bytes 884744 | tf_op jit(solution)/shard_map/ppermute | solution.py:65
  13.8 194.5 %all-gather.5.cloned.1.call-start = ((), (), s32[]{:S(2)}) async-start(), calls=%async_computation.1 | async-start | bytes 10027008 | tf_op jit(solution)/shard_map/all_gather | solution.py:102
  13.8 39.8 %collective-permute-start.2 = (bf16[768,384]{1,0:T(8,128)(2,1)}, bf16[768,384]{1,0:T(8,128)(2,1)S(1)}, u32[]{:S(2)}, u32[]{:S(2)}) collective-permute-start(bf16[768,384]{1,0:T(8,128)(2,1)} %select_convert_fusion.1), channel_id=1, source_target_pairs={{0,16},{16,0},{1,17},{17,1},{2,18},{18,2},{3,19},{19,3},{4,20},{20... | collective-permute-start | bytes 1769480 | tf_op jit(solution)/shard_map/ppermute | solution.py:38
  55.3 36.7 %collective-permute-start.3 = (bf16[1536,384]{1,0:T(8,128)(2,1)S(1)}, bf16[1536,384]{1,0:T(8,128)(2,1)S(1)}, u32[]{:S(2)}, u32[]{:S(2)}) collective-permute-start(bf16[1536,384]{1,0:T(8,128)(2,1)S(1)} %maximum_select_fusion.1), channel_id=1, source_target_pairs={{0,32},{32,64},{64,96},{96,0},{1,33},{33,65},{65,97},{97,1},{2,34}... | collective-permute-start | bytes 3538952 | tf_op jit(solution)/shard_map/ppermute | solution.py:42
  92.0 25.3 %collective-permute-start.4 = (bf16[1536,384]{1,0:T(8,128)(2,1)S(1)}, bf16[1536,384]{1,0:T(8,128)(2,1)}, u32[]{:S(2)}, u32[]{:S(2)}) collective-permute-start(bf16[1536,384]{1,0:T(8,128)(2,1)S(1)} %collective-permute-done.3), channel_id=1, source_target_pairs={{0,32},{32,64},{64,96},{96,0},{1,33},{33,65},{65,97},{97,1},{2,34}... | collective-permute-start | bytes 3538952 | tf_op jit(solution)/shard_map/ppermute | solution.py:44
  92.1 27.6 %collective-permute-start.5 = (bf16[1536,384]{1,0:T(8,128)(2,1)S(1)}, bf16[1536,384]{1,0:T(8,128)(2,1)S(1)}, u32[]{:S(2)}, u32[]{:S(2)}) collective-permute-start(bf16[1536,384]{1,0:T(8,128)(2,1)S(1)} %maximum_select_fusion.1), channel_id=1, source_target_pairs={{0,96},{32,0},{64,32},{96,64},{1,97},{33,1},{65,33},{97,65},{2,98}... | collective-permute-start | bytes 3538952 | tf_op jit(solution)/shard_map/ppermute | solution.py:43
  95.0 2.5 %copy-start.1 = (bf16[768,384]{1,0:T(8,128)(2,1)S(1)}, bf16[768,384]{1,0:T(8,128)(2,1)}, u32[]{:S(2)}) copy-start(bf16[768,384]{1,0:T(8,128)(2,1)} %select_convert_fusion.1) | copy-start | bytes 1769476
Sparse Core Ops, SparseCore 0:
  13.9 90.3 all-gather.2
  143.2 65.0 all-gather.4

commit v3 on v2

v3 whole, which is shorter than its diff:
```python
import math

import jax
import jax.numpy as jnp
from jax import lax
from jax.sharding import Mesh
from jax.sharding import PartitionSpec as P

BLK = 64
BOX = 16
NEAR = 40
FAR = 90
ROW = ("y", "zh")
COL = ("zl", "x", "core")
CHUNKS = 4


def cell_mask(block_cells, row_start, row_count, col_start, col_count, bound_sq):
    row_cells = lax.dynamic_slice_in_dim(block_cells, row_start, row_count, 0)
    col_cells = lax.dynamic_slice_in_dim(block_cells, col_start, col_count, 0)
    offset_abs = jnp.abs(row_cells[:, None, :] - col_cells[None, :, :])
    wrapped = jnp.minimum(offset_abs, BOX - offset_abs)
    keep = jnp.sum(wrapped * wrapped, axis=2) <= bound_sq
    return jnp.repeat(jnp.repeat(keep, BLK, axis=0), BLK, axis=1)


def chunked_shift(value, axis, pairs):
    step = value.shape[0] // CHUNKS
    parts = [lax.ppermute(value[i * step:(i + 1) * step], axis, pairs) for i in range(CHUNKS)]
    return jnp.concatenate(parts, 0)


def column_panel_t(tile_t):
    partner = chunked_shift(tile_t, "zh", [(0, 1), (1, 0)])
    zh_id = lax.axis_index("zh")
    pair = jnp.where(zh_id == 0, jnp.concatenate([tile_t, partner], 1), jnp.concatenate([partner, tile_t], 1))
    ring = lax.axis_size("y")
    up = [(i, (i + 1) % ring) for i in range(ring)]
    down = [(i, (i - 1) % ring) for i in range(ring)]
    from_below = chunked_shift(pair, "y", up)
    from_above = chunked_shift(pair, "y", down)
    from_two_below = chunked_shift(from_below, "y", up)
    y_id = lax.axis_index("y")
    width = pair.shape[1]
    panel = jnp.zeros((pair.shape[0], ring * width), pair.dtype)
    for offset, part in ((0, pair), (-1, from_below), (-2, from_two_below), (1, from_above)):
        panel = lax.dynamic_update_slice_in_dim(panel, part, ((y_id + offset) % ring) * width, 1)
    return panel


def mirror_tile(upper_stored, rows, cols):
    tile_side, half_width = upper_stored.shape
    col_id = lax.axis_index(COL)
    pieces = []
    for k in range(2):
        half = (col_id + k) % 2
        piece = lax.dynamic_slice_in_dim(upper_stored, half * half_width, half_width, 0)
        pairs = []
        for a in range(rows):
            for b in range(cols):
                h = (b + k) % 2
                pairs.append((a * cols + b, (b // 2) * cols + 2 * a + h))
        pieces.append(lax.ppermute(piece, ROW + COL, pairs))
    h_own = col_id % 2
    first = jnp.where(h_own == 0, pieces[0], pieces[1])
    second = jnp.where(h_own == 0, pieces[1], pieces[0])
    return jnp.concatenate([first, second], 1).T


def dot_t(left, right_t):
    return lax.dot_general(left, right_t, (((1,), (1,)), ((), ())), preferred_element_type=jnp.float32)


def per_device(upper_stored, block_cells):
    rows = lax.axis_size(ROW)
    cols = lax.axis_size(COL)
    row_id = lax.axis_index(ROW)
    col_id = lax.axis_index(COL)
    tile_side, half_width = upper_stored.shape
    order_total = tile_side * rows
    tile_blocks = tile_side // BLK
    half_blocks = half_width // BLK
    mirrored = mirror_tile(upper_stored, rows, cols)
    global_rows = row_id * tile_side + lax.broadcasted_iota(jnp.int32, (tile_side, half_width), 0)
    global_cols = col_id * half_width + lax.broadcasted_iota(jnp.int32, (tile_side, half_width), 1)
    symmetric = jnp.where(global_rows <= global_cols, upper_stored, mirrored)
    near_own = cell_mask(
        block_cells, row_id * tile_blocks, tile_blocks, col_id * half_blocks, half_blocks, NEAR
    )
    far_own = cell_mask(
        block_cells, row_id * tile_blocks, tile_blocks, col_id * half_blocks, half_blocks, FAR
    )
    diagonal = jnp.where(global_rows == global_cols, 0.5, 0.0).astype(jnp.float32)
    value_scale = 2.0 / math.sqrt(order_total)
    density_full = diagonal + value_scale * symmetric.astype(jnp.float32)
    density = jnp.where(near_own, density_full, 0.0).astype(jnp.bfloat16)
    row_panel = lax.all_gather(density, COL, axis=1, tiled=True)
    col_panel_t = column_panel_t(density.T)
    square = jnp.where(far_own, dot_t(row_panel, col_panel_t), 0.0)
    square_low = square.astype(jnp.bfloat16)
    low_panel = lax.all_gather(square_low, COL, axis=1, tiled=True)
    cubic = dot_t(low_panel, col_panel_t)
    return jnp.where(near_own, 3.0 * square - 2.0 * cubic, 0.0).astype(jnp.bfloat16)


def solution(mesh):
    y_size = mesh.devices.shape[0] // 2
    x_size = mesh.devices.shape[1] // 4
    split_mesh = Mesh(mesh.devices.reshape(y_size, 2, 2, x_size, 2), ROW + COL)
    return jax.shard_map(
        per_device,
        mesh=split_mesh,
        in_specs=(P(ROW, COL), P()),
        out_specs=P(ROW, COL),
        check_vma=False,
    )
```

time: 225 us -> 247 us (1.098)
  waiting for transfers between devices: 121 us -> 142 us
  local copies, waits for them, and re-layouts: 24.9 us -> 7.21 us
  starting transfers between devices: 38.6 us -> 51.6 us
  other arithmetic: 4.91 us -> 13.8 us
  matrix products: 22.4 us -> 19.4 us
    ppermute x4 -> x16, waiting for transfers between devices: 60.2 us -> 76.1 us  [chunked_shift(): lax.ppermute(value[i * step:(i + 1) * step], axis, pairs)]
    ppermute x4 -> x16, starting transfers between devices: 36.4 us -> 49.4 us  [chunked_shift(): lax.ppermute(value[i * step:(i + 1) * step], axis, pairs)]
    dynamic_update_slice x1 -> x4, other arithmetic: 1.43 us -> 12.3 us  [column_panel_t(): lax.dynamic_update_slice_in_dim(panel, part, (y_id + offset) % ring * wid...]
    dot_general x1 -> x0, local copies, waits for them, and re-layouts: 6.69 us -> none  [per_device(): jnp.dot(row_panel, col_panel, preferred_element_type=jnp.float32)]
    dynamic_update_slice x3 -> x0, local copies, waits for them, and re-layouts: 4.74 us -> none  [column_panel(): lax.dynamic_update_index_in_dim(panel, part, (y_id + offset) % ring, 0)]
    mul x2 -> x0, local copies, waits for them, and re-layouts: 4.74 us -> none  [per_device(): return block_keep(3.0 * square - 2.0 * cubic, near_own).astype(jnp.bfloat16)]
    all_gather x1, waiting for transfers between devices: 60.5 us -> 65.2 us  [per_device(): low_panel = lax.all_gather(square_low, COL, axis=1, tiled=True)]
    broadcast_in_dim x3 -> x5, local copies, waits for them, and re-layouts: 4.18 us -> 0.72 us  [the longest x1 0.41 us: column_panel_t(): panel = jnp.zeros((pair.shape[0], ring * width), pair.dtype)]
  transfers between devices with their start and end apart: 8 -> 20, of which waited for: 4 -> 14; matrix products, arithmetic and copies ran while one was open for 11% -> 7% of each run, Pallas kernels for 0% -> 0%
where the time goes in v3:
time: 247 us
  waiting for transfers between devices  142 us (57%)
  starting transfers between devices  51.6 us (21%)
  matrix products  19.4 us (8%)
  other arithmetic  13.8 us (6%)
  between operations  13.6 us (6%)
  local copies, waits for them, and re-layouts  7.21 us (3%)
    ppermute x16, waiting for transfers between devices, chunked_shift(): lax.ppermute(value[i * step:(i + 1) * step], axis, pairs)  76.1 us
    all_gather x1, waiting for transfers between devices, per_device(): low_panel = lax.all_gather(square_low, COL, axis=1, tiled=True)  65.2 us
    ppermute x16, starting transfers between devices, chunked_shift(): lax.ppermute(value[i * step:(i + 1) * step], axis, pairs)  49.4 us
    dot_general x2, matrix products, dot_t(): lax.dot_general(left, right_t, (((1,), (1,)), ((), ())), preferred_elemen...  19.4 us
    dynamic_update_slice x4, other arithmetic, column_panel_t(): lax.dynamic_update_slice_in_dim(panel, part, (y_id + offset) % ring * wid...  12.3 us
  transfers between devices with their start and end apart: 20, of which 14 were waited for; matrix products, arithmetic and copies ran while one was open for 7% of the time, Pallas kernels for 0%

profile of v3, /device:TPU:1, one launch (start us, length us, event | category | flops | bytes accessed | tf_op | source)
XLA Modules:
  0.0 247.3 jit_solution(16120007364873904586)
XLA Ops:
  6.5 1.2 constant_dynamic-slice_fusion.1
  8.9 1.5 collective-permute-start.1
  11.6 1.3 select_convert_fusion
  13.0 1.5 fusion.6
  14.6 22.9 %collective-permute-start.2 = (bf16[96,768]{0,1:T(8,128)(2,1)S(1)}, bf16[96,768]{0,1:T(8,128)(2,1)S(1)}, u32[]{:S(2)}, u32[]{:S(2)}) collective-permute-start(bf16[96,768]{0,1:T(8,128)(2,1)S(1)} %get-tuple-element.11), channel_id=1, source_target_pairs={{0,16},{16,0},{1,17},{17,1},{2,18},{18,2},{3,19},{19,3},{4,20},{20... | collective-permute-start | bytes 442376 | tf_op jit(solution)/shard_map/ppermute | solution.py:29
  37.6 2.9 %collective-permute-start.4 = (bf16[96,768]{0,1:T(8,128)(2,1)S(1)}, bf16[96,768]{0,1:T(8,128)(2,1)S(1)}, u32[]{:S(2)}, u32[]{:S(2)}) collective-permute-start(bf16[96,768]{0,1:T(8,128)(2,1)S(1)} %get-tuple-element.13), channel_id=1, source_target_pairs={{0,16},{16,0},{1,17},{17,1},{2,18},{18,2},{3,19},{19,3},{4,20},{20... | collective-permute-start | bytes 442376 | tf_op jit(solution)/shard_map/ppermute | solution.py:29
  40.6 4.6 %collective-permute-done.2 = bf16[96,768]{0,1:T(8,128)(2,1)S(1)} collective-permute-done((bf16[96,768]{0,1:T(8,128)(2,1)S(1)}, bf16[96,768]{0,1:T(8,128)(2,1)S(1)}, u32[]{:S(2)}, u32[]{:S(2)}) %collective-permute-start.2) | collective-permute-done | bytes 147488 | tf_op jit(solution)/shard_map/ppermute | solution.py:29
  45.1 4.2 %collective-permute-done.3 = bf16[96,768]{0,1:T(8,128)(2,1)S(1)} collective-permute-done((bf16[96,768]{0,1:T(8,128)(2,1)S(1)}, bf16[96,768]{0,1:T(8,128)(2,1)S(1)}, u32[]{:S(2)}, u32[]{:S(2)}) %collective-permute-start.3) | collective-permute-done | bytes 147488 | tf_op jit(solution)/shard_map/ppermute | solution.py:29
  49.3 4.2 %collective-permute-done.4 = bf16[96,768]{0,1:T(8,128)(2,1)S(1)} collective-permute-done((bf16[96,768]{0,1:T(8,128)(2,1)S(1)}, bf16[96,768]{0,1:T(8,128)(2,1)S(1)}, u32[]{:S(2)}, u32[]{:S(2)}) %collective-permute-start.4) | collective-permute-done | bytes 147488 | tf_op jit(solution)/shard_map/ppermute | solution.py:29
  53.5 8.1 %collective-permute-done.5 = bf16[96,768]{0,1:T(8,128)(2,1)S(1)} collective-permute-done((bf16[96,768]{0,1:T(8,128)(2,1)S(1)}, bf16[96,768]{0,1:T(8,128)(2,1)S(1)}, u32[]{:S(2)}, u32[]{:S(2)}) %collective-permute-start.5) | collective-permute-done | bytes 147488 | tf_op jit(solution)/shard_map/ppermute | solution.py:29
  62.0 4.7 %constant_dynamic-update-slice_fusion = (bf16[384,6144]{0,1:T(8,128)(2,1)S(1)}, bf16[384,1536]{0,1:T(8,128)(2,1)S(1)}) fusion(bf16[384,6144]{0,1:T(8,128)(2,1)S(1)} %broadcast_in_dim.37, s32[]{:T(128)S(6)} %select_n.108, bf16[384,768]{0,1:T(8,128)(2,1)S(1)} %bitcast.16, bf16[96,768]{0,1:T(8,128)(2,1)S(1)} %collective-permute-done.5, ...), kind=kLoop, calls=%fused_computation.21 | loop fusion | flops 12386304 | bytes 3735557 | tf_op jit(solution)/shard_map/dynamic_update_slice | solution.py:47
  67.2 1.8 copy-done.2
  69.0 14.5 %collective-permute-start.6 = (bf16[96,1536]{0,1:T(8,128)(2,1)S(1)}, bf16[96,1536]{0,1:T(8,128)(2,1)S(1)}, u32[]{:S(2)}, u32[]{:S(2)}) collective-permute-start(bf16[96,1536]{0,1:T(8,128)(2,1)S(1)} %get-tuple-element.7), channel_id=1, source_target_pairs={{0,32},{32,64},{64,96},{96,0},{1,33},{33,65},{65,97},{97,1},{2,34}... | collective-permute-start | bytes 884744 | tf_op jit(solution)/shard_map/ppermute | solution.py:29
  83.4 2.6 %collective-permute-start.8 = (bf16[96,1536]{0,1:T(8,128)(2,1)S(1)}, bf16[96,1536]{0,1:T(8,128)(2,1)S(1)}, u32[]{:S(2)}, u32[]{:S(2)}) collective-permute-start(bf16[96,1536]{0,1:T(8,128)(2,1)S(1)} %get-tuple-element.8), channel_id=1, source_target_pairs={{0,32},{32,64},{64,96},{96,0},{1,33},{33,65},{65,97},{97,1},{2,34}... | collective-permute-start | bytes 884744 | tf_op jit(solution)/shard_map/ppermute | solution.py:29
  86.1 5.7 %collective-permute-done.6 = bf16[96,1536]{0,1:T(8,128)(2,1)S(1)} collective-permute-done((bf16[96,1536]{0,1:T(8,128)(2,1)S(1)}, bf16[96,1536]{0,1:T(8,128)(2,1)S(1)}, u32[]{:S(2)}, u32[]{:S(2)}) %collective-permute-start.6) | collective-permute-done | bytes 294944 | tf_op jit(solution)/shard_map/ppermute | solution.py:29
  91.8 8.4 %collective-permute-done.7 = bf16[96,1536]{0,1:T(8,128)(2,1)S(1)} collective-permute-done((bf16[96,1536]{0,1:T(8,128)(2,1)S(1)}, bf16[96,1536]{0,1:T(8,128)(2,1)S(1)}, u32[]{:S(2)}, u32[]{:S(2)}) %collective-permute-start.7) | collective-permute-done | bytes 294944 | tf_op jit(solution)/shard_map/ppermute | solution.py:29
  100.2 8.4 %collective-permute-done.8 = bf16[96,1536]{0,1:T(8,128)(2,1)S(1)} collective-permute-done((bf16[96,1536]{0,1:T(8,128)(2,1)S(1)}, bf16[96,1536]{0,1:T(8,128)(2,1)S(1)}, u32[]{:S(2)}, u32[]{:S(2)}) %collective-permute-start.8) | collective-permute-done | bytes 294944 | tf_op jit(solution)/shard_map/ppermute | solution.py:29
  108.6 8.5 %collective-permute-done.9 = bf16[96,1536]{0,1:T(8,128)(2,1)} collective-permute-done((bf16[96,1536]{0,1:T(8,128)(2,1)S(1)}, bf16[96,1536]{0,1:T(8,128)(2,1)}, u32[]{:S(2)}, u32[]{:S(2)}) %collective-permute-start.9) | collective-permute-done | bytes 294944 | tf_op jit(solution)/shard_map/ppermute | solution.py:29
  117.8 2.7 %collective-permute-start.14 = (bf16[96,1536]{0,1:T(8,128)(2,1)S(1)}, bf16[96,1536]{0,1:T(8,128)(2,1)S(1)}, u32[]{:S(2)}, u32[]{:S(2)}) collective-permute-start(bf16[96,1536]{0,1:T(8,128)(2,1)S(1)} %get-tuple-element.7), channel_id=1, source_target_pairs={{0,96},{32,0},{64,32},{96,64},{1,97},{33,1},{65,33},{97,65},{2,98}... | collective-permute-start | bytes 884744 | tf_op jit(solution)/shard_map/ppermute | solution.py:29
  120.6 5.0 %collective-permute-done.10 = bf16[96,1536]{0,1:T(8,128)(2,1)} collective-permute-done((bf16[96,1536]{0,1:T(8,128)(2,1)S(1)}, bf16[96,1536]{0,1:T(8,128)(2,1)}, u32[]{:S(2)}, u32[]{:S(2)}) %collective-permute-start.10) | collective-permute-done | bytes 294944 | tf_op jit(solution)/shard_map/ppermute | solution.py:29
  125.6 1.2 collective-permute-start.15
  126.8 7.2 %collective-permute-done.11 = bf16[96,1536]{0,1:T(8,128)(2,1)} collective-permute-done((bf16[96,1536]{0,1:T(8,128)(2,1)S(1)}, bf16[96,1536]{0,1:T(8,128)(2,1)}, u32[]{:S(2)}, u32[]{:S(2)}) %collective-permute-start.11) | collective-permute-done | bytes 294944 | tf_op jit(solution)/shard_map/ppermute | solution.py:29
  134.0 1.2 collective-permute-start.16
  135.2 7.2 %collective-permute-done.12 = bf16[96,1536]{0,1:T(8,128)(2,1)} collective-permute-done((bf16[96,1536]{0,1:T(8,128)(2,1)S(1)}, bf16[96,1536]{0,1:T(8,128)(2,1)}, u32[]{:S(2)}, u32[]{:S(2)}) %collective-permute-start.12) | collective-permute-done | bytes 294944 | tf_op jit(solution)/shard_map/ppermute | solution.py:29
  142.4 1.2 collective-permute-start.17
  143.6 2.7 %maximum_dynamic-update-slice_fusion = bf16[384,6144]{0,1:T(8,128)(2,1)} fusion(bf16[384,6144]{0,1:T(8,128)(2,1)} %copy-done.2, s32[]{:T(128)S(6)} %select_n.110, bf16[96,1536]{0,1:T(8,128)(2,1)} %collective-permute-done.9, bf16[96,1536]{0,1:T(8,128)(2,1)S(1)} %collective-permute-done.8, bf16[96,1536]{0,1:T(8,128)(2,1)S(1)} %collective-permute-done.7, ...), kind=kLoop, calls=%fused_computation.6 | loop fusion | flops 4718592 | bytes 2457604 | tf_op jit(solution)/shard_map/dynamic_update_slice | solution.py:47
  146.3 4.5 %collective-permute-done.13 = bf16[96,1536]{0,1:T(8,128)(2,1)} collective-permute-done((bf16[96,1536]{0,1:T(8,128)(2,1)}, bf16[96,1536]{0,1:T(8,128)(2,1)}, u32[]{:S(2)}, u32[]{:S(2)}) %collective-permute-start.13) | collective-permute-done | bytes 294944 | tf_op jit(solution)/shard_map/ppermute | solution.py:29
  150.8 3.2 %maximum_dynamic-update-slice_fusion.1 = bf16[384,6144]{0,1:T(8,128)(2,1)} fusion(bf16[384,6144]{0,1:T(8,128)(2,1)} %maximum_dynamic-update-slice_fusion, s32[]{:T(128)S(6)} %select_n.112, bf16[96,1536]{0,1:T(8,128)(2,1)} %collective-permute-done.13, bf16[96,1536]{0,1:T(8,128)(2,1)} %collective-permute-done.12, bf16[96,1536]{0,1:T(8,128)(2,1)} %collective-permute-done.11, ...), kind=kLoop, calls=%fused_computation.7 | loop fusion | flops 4718592 | bytes 2752516 | tf_op jit(solution)/shard_map/dynamic_update_slice | solution.py:47
  154.0 1.7 maximum_dynamic-update-slice_fusion.2
  155.8 9.7 %fusion.7 = (bf16[768,384]{1,0:T(8,128)(2,1)}, f32[768,384]{1,0:T(8,128)S(1)}) fusion(pred[768,384]{1,0:T(32,128)(4,1)S(1)} %copy.17, bf16[768,6144]{1,0:T(8,128)(2,1)} %all-gather.3.cloned.1.call-done, bf16[384,6144]{0,1:T(8,128)(2,1)} %maximum_dynamic-update-slice_fusion.2), kind=kOutput, calls=%fused_computation.28 | convolution fusion | flops 3624468480 | bytes 16220160 | tf_op jit(solution)/shard_map/dot_general | solution.py:71
  165.5 65.2 %all-gather.5.cloned.1.call-done = bf16[768,6144]{1,0:T(8,128)(2,1)} async-done(((bf16[768,384]{1,0:T(8,128)(2,1)}), bf16[768,6144]{1,0:T(8,128)(2,1)}) %all-gather.5.cloned.1.call-update) | async-done | bytes 9437200 | tf_op jit(solution)/shard_map/all_gather | solution.py:101
  230.7 9.7 %fusion.2 = bf16[768,384]{1,0:T(8,128)(2,1)} fusion(pred[768,384]{1,0:T(32,128)(4,1)S(1)} %copy.18, bf16[768,6144]{1,0:T(8,128)(2,1)} %all-gather.5.cloned.1.call-done, bf16[384,6144]{0,1:T(8,128)(2,1)} %maximum_dynamic-update-slice_fusion.2, f32[768,384]{1,0:T(8,128)S(1)} %get-tuple-element.22), kind=kOutput, calls=%fused_computation.4 | convolution fusion | flops 3625353216 | bytes 16220160 | tf_op jit(solution)/shard_map/dot_general | solution.py:71
  (46 shorter events, 4.1 us)
Async XLA Ops:
  6.5 3.8 %copy-start = (s32[96,3]{0,1:T(4,128)S(1)}, s32[96,3]{0,1:T(4,128)}, u32[]{:S(2)}) copy-start(s32[96,3]{0,1:T(4,128)} %param.3) | copy-start | bytes 3460
  6.5 5.1 %copy-start.3 = (bf16[768,384]{1,0:T(8,128)(2,1)S(1)}, bf16[768,384]{1,0:T(8,128)(2,1)}, u32[]{:S(2)}) copy-start(bf16[768,384]{1,0:T(8,128)(2,1)} %param.2) | copy-start | bytes 1769476
  6.5 149.2 %all-gather.3.cloned.1.call-start = ((), (), s32[]{:S(2)}) async-start(), calls=%async_computation | async-start | bytes 10027008 | tf_op jit(solution)/shard_map/all_gather | solution.py:97
  7.9 3.3 %collective-permute-start = (bf16[384,384]{0,1:T(8,128)(2,1)S(1)}, bf16[384,384]{0,1:T(8,128)(2,1)S(1)}, u32[]{:S(2)}, u32[]{:S(2)}) collective-permute-start(bf16[384,384]{0,1:T(8,128)(2,1)S(1)} %copy.19), channel_id=1, source_target_pairs={{0,0},{1,1},{2,16},{3,17},{4,32},{5,33},{6,48},{7,49},{8,64},{9,65... | collective-permute-start | bytes 884744 | tf_op jit(solution)/shard_map/ppermute | solution.py:63
  8.9 2.7 %collective-permute-start.1 = (bf16[384,384]{0,1:T(8,128)(2,1)S(1)}, bf16[384,384]{0,1:T(8,128)(2,1)S(1)}, u32[]{:S(2)}, u32[]{:S(2)}) collective-permute-start(bf16[384,384]{0,1:T(8,128)(2,1)S(1)} %copy.20), channel_id=1, source_target_pairs={{0,1},{1,0},{2,17},{3,16},{4,33},{5,32},{6,49},{7,48},{8,65},{9,64... | collective-permute-start | bytes 884744 | tf_op jit(solution)/shard_map/ppermute | solution.py:63
  13.0 217.7 %all-gather.5.cloned.1.call-start = ((), (), s32[]{:S(2)}) async-start(), calls=%async_computation.1 | async-start | bytes 10027008 | tf_op jit(solution)/shard_map/all_gather | solution.py:101
  14.6 30.6 %collective-permute-start.2 = (bf16[96,768]{0,1:T(8,128)(2,1)S(1)}, bf16[96,768]{0,1:T(8,128)(2,1)S(1)}, u32[]{:S(2)}, u32[]{:S(2)}) collective-permute-start(bf16[96,768]{0,1:T(8,128)(2,1)S(1)} %get-tuple-element.11), channel_id=1, source_target_pairs={{0,16},{16,0},{1,17},{17,1},{2,18},{18,2},{3,19},{19,3},{4,20},{20... | collective-permute-start | bytes 442376 | tf_op jit(solution)/shard_map/ppermute | solution.py:29
  37.5 11.8 %collective-permute-start.3 = (bf16[96,768]{0,1:T(8,128)(2,1)S(1)}, bf16[96,768]{0,1:T(8,128)(2,1)S(1)}, u32[]{:S(2)}, u32[]{:S(2)}) collective-permute-start(bf16[96,768]{0,1:T(8,128)(2,1)S(1)} %get-tuple-element.14), channel_id=1, source_target_pairs={{0,16},{16,0},{1,17},{17,1},{2,18},{18,2},{3,19},{19,3},{4,20},{20... | collective-permute-start | bytes 442376 | tf_op jit(solution)/shard_map/ppermute | solution.py:29
  37.6 16.0 %collective-permute-start.4 = (bf16[96,768]{0,1:T(8,128)(2,1)S(1)}, bf16[96,768]{0,1:T(8,128)(2,1)S(1)}, u32[]{:S(2)}, u32[]{:S(2)}) collective-permute-start(bf16[96,768]{0,1:T(8,128)(2,1)S(1)} %get-tuple-element.13), channel_id=1, source_target_pairs={{0,16},{16,0},{1,17},{17,1},{2,18},{18,2},{3,19},{19,3},{4,20},{20... | collective-permute-start | bytes 442376 | tf_op jit(solution)/shard_map/ppermute | solution.py:29
  40.5 21.2 %collective-permute-start.5 = (bf16[96,768]{0,1:T(8,128)(2,1)S(1)}, bf16[96,768]{0,1:T(8,128)(2,1)S(1)}, u32[]{:S(2)}, u32[]{:S(2)}) collective-permute-start(bf16[96,768]{0,1:T(8,128)(2,1)S(1)} %get-tuple-element.12), channel_id=1, source_target_pairs={{0,16},{16,0},{1,17},{17,1},{2,18},{18,2},{3,19},{19,3},{4,20},{20... | collective-permute-start | bytes 442376 | tf_op jit(solution)/shard_map/ppermute | solution.py:29
  40.6 21.5 %copy-start.1 = (bf16[768,384]{1,0:T(8,128)(2,1)S(1)}, bf16[768,384]{1,0:T(8,128)(2,1)}, u32[]{:S(2)}) copy-start(bf16[768,384]{1,0:T(8,128)(2,1)} %select_convert_fusion) | copy-start | bytes 1769476
  66.7 2.2 copy-start.2
  69.0 22.8 %collective-permute-start.6 = (bf16[96,1536]{0,1:T(8,128)(2,1)S(1)}, bf16[96,1536]{0,1:T(8,128)(2,1)S(1)}, u32[]{:S(2)}, u32[]{:S(2)}) collective-permute-start(bf16[96,1536]{0,1:T(8,128)(2,1)S(1)} %get-tuple-element.7), channel_id=1, source_target_pairs={{0,32},{32,64},{64,96},{96,0},{1,33},{33,65},{65,97},{97,1},{2,34}... | collective-permute-start | bytes 884744 | tf_op jit(solution)/shard_map/ppermute | solution.py:29
  83.4 16.8 %collective-permute-start.7 = (bf16[96,1536]{0,1:T(8,128)(2,1)S(1)}, bf16[96,1536]{0,1:T(8,128)(2,1)S(1)}, u32[]{:S(2)}, u32[]{:S(2)}) collective-permute-start(bf16[96,1536]{0,1:T(8,128)(2,1)S(1)} %get-tuple-element.9), channel_id=1, source_target_pairs={{0,32},{32,64},{64,96},{96,0},{1,33},{33,65},{65,97},{97,1},{2,34}... | collective-permute-start | bytes 884744 | tf_op jit(solution)/shard_map/ppermute | solution.py:29
  83.4 25.2 %collective-permute-start.8 = (bf16[96,1536]{0,1:T(8,128)(2,1)S(1)}, bf16[96,1536]{0,1:T(8,128)(2,1)S(1)}, u32[]{:S(2)}, u32[]{:S(2)}) collective-permute-start(bf16[96,1536]{0,1:T(8,128)(2,1)S(1)} %get-tuple-element.8), channel_id=1, source_target_pairs={{0,32},{32,64},{64,96},{96,0},{1,33},{33,65},{65,97},{97,1},{2,34}... | collective-permute-start | bytes 884744 | tf_op jit(solution)/shard_map/ppermute | solution.py:29
  86.1 31.1 %collective-permute-start.9 = (bf16[96,1536]{0,1:T(8,128)(2,1)S(1)}, bf16[96,1536]{0,1:T(8,128)(2,1)}, u32[]{:S(2)}, u32[]{:S(2)}) collective-permute-start(bf16[96,1536]{0,1:T(8,128)(2,1)S(1)} %get-tuple-element.10), channel_id=1, source_target_pairs={{0,32},{32,64},{64,96},{96,0},{1,33},{33,65},{65,97},{97,1},{2,34}... | collective-permute-start | bytes 884744 | tf_op jit(solution)/shard_map/ppermute | solution.py:29
  91.8 33.8 %collective-permute-start.10 = (bf16[96,1536]{0,1:T(8,128)(2,1)S(1)}, bf16[96,1536]{0,1:T(8,128)(2,1)}, u32[]{:S(2)}, u32[]{:S(2)}) collective-permute-start(bf16[96,1536]{0,1:T(8,128)(2,1)S(1)} %collective-permute-done.6), channel_id=1, source_target_pairs={{0,32},{32,64},{64,96},{96,0},{1,33},{33,65},{65,97},{97,1},{2,34}... | collective-permute-start | bytes 884744 | tf_op jit(solution)/shard_map/ppermute | solution.py:29
  100.2 33.8 %collective-permute-start.11 = (bf16[96,1536]{0,1:T(8,128)(2,1)S(1)}, bf16[96,1536]{0,1:T(8,128)(2,1)}, u32[]{:S(2)}, u32[]{:S(2)}) collective-permute-start(bf16[96,1536]{0,1:T(8,128)(2,1)S(1)} %collective-permute-done.7), channel_id=1, source_target_pairs={{0,32},{32,64},{64,96},{96,0},{1,33},{33,65},{65,97},{97,1},{2,34}... | collective-permute-start | bytes 884744 | tf_op jit(solution)/shard_map/ppermute | solution.py:29
  108.6 33.8 %collective-permute-start.12 = (bf16[96,1536]{0,1:T(8,128)(2,1)S(1)}, bf16[96,1536]{0,1:T(8,128)(2,1)}, u32[]{:S(2)}, u32[]{:S(2)}) collective-permute-start(bf16[96,1536]{0,1:T(8,128)(2,1)S(1)} %collective-permute-done.8), channel_id=1, source_target_pairs={{0,32},{32,64},{64,96},{96,0},{1,33},{33,65},{65,97},{97,1},{2,34}... | collective-permute-start | bytes 884744 | tf_op jit(solution)/shard_map/ppermute | solution.py:29
  117.1 33.7 %collective-permute-start.13 = (bf16[96,1536]{0,1:T(8,128)(2,1)}, bf16[96,1536]{0,1:T(8,128)(2,1)}, u32[]{:S(2)}, u32[]{:S(2)}) collective-permute-start(bf16[96,1536]{0,1:T(8,128)(2,1)} %collective-permute-done.9), channel_id=1, source_target_pairs={{0,32},{32,64},{64,96},{96,0},{1,33},{33,65},{65,97},{97,1},{2,34}... | collective-permute-start | bytes 884744 | tf_op jit(solution)/shard_map/ppermute | solution.py:29
  117.8 36.2 %collective-permute-start.14 = (bf16[96,1536]{0,1:T(8,128)(2,1)S(1)}, bf16[96,1536]{0,1:T(8,128)(2,1)S(1)}, u32[]{:S(2)}, u32[]{:S(2)}) collective-permute-start(bf16[96,1536]{0,1:T(8,128)(2,1)S(1)} %get-tuple-element.7), channel_id=1, source_target_pairs={{0,96},{32,0},{64,32},{96,64},{1,97},{33,1},{65,33},{97,65},{2,98}... | collective-permute-start | bytes 884744 | tf_op jit(solution)/shard_map/ppermute | solution.py:29
  125.6 28.4 %collective-permute-start.15 = (bf16[96,1536]{0,1:T(8,128)(2,1)S(1)}, bf16[96,1536]{0,1:T(8,128)(2,1)S(1)}, u32[]{:S(2)}, u32[]{:S(2)}) collective-permute-start(bf16[96,1536]{0,1:T(8,128)(2,1)S(1)} %get-tuple-element.9), channel_id=1, source_target_pairs={{0,96},{32,0},{64,32},{96,64},{1,97},{33,1},{65,33},{97,65},{2,98}... | collective-permute-start | bytes 884744 | tf_op jit(solution)/shard_map/ppermute | solution.py:29
  134.0 20.0 %collective-permute-start.16 = (bf16[96,1536]{0,1:T(8,128)(2,1)S(1)}, bf16[96,1536]{0,1:T(8,128)(2,1)S(1)}, u32[]{:S(2)}, u32[]{:S(2)}) collective-permute-start(bf16[96,1536]{0,1:T(8,128)(2,1)S(1)} %get-tuple-element.8), channel_id=1, source_target_pairs={{0,96},{32,0},{64,32},{96,64},{1,97},{33,1},{65,33},{97,65},{2,98}... | collective-permute-start | bytes 884744 | tf_op jit(solution)/shard_map/ppermute | solution.py:29
  142.4 11.6 %collective-permute-start.17 = (bf16[96,1536]{0,1:T(8,128)(2,1)S(1)}, bf16[96,1536]{0,1:T(8,128)(2,1)S(1)}, u32[]{:S(2)}, u32[]{:S(2)}) collective-permute-start(bf16[96,1536]{0,1:T(8,128)(2,1)S(1)} %get-tuple-element.10), channel_id=1, source_target_pairs={{0,96},{32,0},{64,32},{96,64},{1,97},{33,1},{65,33},{97,65},{2,98}... | collective-permute-start | bytes 884744 | tf_op jit(solution)/shard_map/ppermute | solution.py:29
Sparse Core Ops, SparseCore 0:
  13.1 96.7 all-gather.2
  165.6 65.0 all-gather.4

commit v4 on v3

--- a/solution.py
+++ b/solution.py
@@ -12,7 +12,7 @@
 FAR = 90
 ROW = ("y", "zh")
 COL = ("zl", "x", "core")
-CHUNKS = 4
+CHUNKS = 1
 
 
 def cell_mask(block_cells, row_start, row_count, col_start, col_count, bound_sq):

time: 247 us -> 215 us (0.87)
  waiting for transfers between devices: 142 us -> 129 us
  starting transfers between devices: 51.6 us -> 39.2 us
  other arithmetic: 13.8 us -> 3.07 us
  local copies, waits for them, and re-layouts: 7.21 us -> 10.4 us
    ppermute x16 -> x4, starting transfers between devices: 49.4 us -> 37 us  [chunked_shift(): lax.ppermute(value[i * step:(i + 1) * step], axis, pairs)]
    ppermute x16 -> x4, waiting for transfers between devices: 76.1 us -> 63.9 us  [chunked_shift(): lax.ppermute(value[i * step:(i + 1) * step], axis, pairs)]
    dynamic_update_slice x4 -> x1, other arithmetic: 12.3 us -> 1.56 us  [column_panel_t(): lax.dynamic_update_slice_in_dim(panel, part, (y_id + offset) % ring * wid...]
    dynamic_update_slice x0 -> x3, local copies, waits for them, and re-layouts: none -> 4.74 us  [column_panel_t(): lax.dynamic_update_slice_in_dim(panel, part, (y_id + offset) % ring * wid...]
  transfers between devices with their start and end apart: 20 -> 8, of which waited for: 14 -> 5; matrix products, arithmetic and copies ran while one was open for 7% -> 4% of each run, Pallas kernels for 0% -> 0%
where the time goes in v4:
time: 215 us
  waiting for transfers between devices  129 us (60%)
  starting transfers between devices  39.2 us (18%)
  matrix products  19.4 us (9%)
  between operations  13.6 us (6%)
  local copies, waits for them, and re-layouts  10.4 us (5%)
  other arithmetic  3.07 us (1%)
    all_gather x1, waiting for transfers between devices, per_device(): low_panel = lax.all_gather(square_low, COL, axis=1, tiled=True)  65.3 us
    ppermute x4, waiting for transfers between devices, chunked_shift(): lax.ppermute(value[i * step:(i + 1) * step], axis, pairs)  63.9 us
    ppermute x4, starting transfers between devices, chunked_shift(): lax.ppermute(value[i * step:(i + 1) * step], axis, pairs)  37 us
    dot_general x2, matrix products, dot_t(): lax.dot_general(left, right_t, (((1,), (1,)), ((), ())), preferred_elemen...  19.4 us
    dynamic_update_slice x3, local copies, waits for them, and re-layouts, column_panel_t(): lax.dynamic_update_slice_in_dim(panel, part, (y_id + offset) % ring * wid...  4.74 us
  transfers between devices with their start and end apart: 8, of which 5 were waited for; matrix products, arithmetic and copies ran while one was open for 4% of the time, Pallas kernels for 0%

profile of v4, /device:TPU:1, one launch (start us, length us, event | category | flops | bytes accessed | tf_op | source)
XLA Modules:
  0.0 215.1 jit_solution(3671756206877655461)
XLA Ops:
  6.5 1.1 constant_dynamic-slice_fusion.1
  7.7 0.2 copy.19
  7.9 0.7 collective-permute-start
  8.6 0.2 copy.20
  8.8 1.5 collective-permute-start.1
  10.3 0.1 constant_dynamic-slice_fusion.2
  10.4 0.1 fusion.1
  10.5 0.1 broadcast_in_dim.31
  10.6 0.1 reshape.14
  10.7 0.1 broadcast_in_dim.32
  10.8 0.4 copy.18
  11.2 0.3 collective-permute-done.1
  11.6 1.3 select_convert_fusion.1
  13.0 22.9 %collective-permute-start.2 = (bf16[384,768]{0,1:T(8,128)(2,1)}, bf16[384,768]{0,1:T(8,128)(2,1)S(1)}, u32[]{:S(2)}, u32[]{:S(2)}) collective-permute-start(bf16[384,768]{0,1:T(8,128)(2,1)} %bitcast.15), channel_id=1, source_target_pairs={{0,16},{16,0},{1,17},{17,1},{2,18},{18,2},{3,19},{19,3},{4,20},{20... | collective-permute-start | bytes 1769480 | tf_op jit(solution)/shard_map/ppermute | solution.py:29
  35.9 17.7 %collective-permute-done.2 = bf16[384,768]{0,1:T(8,128)(2,1)S(1)} collective-permute-done((bf16[384,768]{0,1:T(8,128)(2,1)}, bf16[384,768]{0,1:T(8,128)(2,1)S(1)}, u32[]{:S(2)}, u32[]{:S(2)}) %collective-permute-start.2) | collective-permute-done | bytes 589856 | tf_op jit(solution)/shard_map/ppermute | solution.py:29
  53.6 0.4 broadcast_in_dim.37
  54.0 1.6 constant_dynamic-update-slice_fusion.3
  55.6 2.2 %copy-done.2 = bf16[384,6144]{0,1:T(8,128)(2,1)} copy-done((bf16[384,6144]{0,1:T(8,128)(2,1)}, bf16[384,6144]{0,1:T(8,128)(2,1)S(1)}, u32[]{:S(2)}) %copy-start.2) | copy-done | bytes 4718616
  57.8 11.4 %collective-permute-start.3 = (bf16[384,1536]{0,1:T(8,128)(2,1)}, bf16[384,1536]{0,1:T(8,128)(2,1)S(1)}, u32[]{:S(2)}, u32[]{:S(2)}) collective-permute-start(bf16[384,1536]{0,1:T(8,128)(2,1)} %get-tuple-element.6), channel_id=1, source_target_pairs={{0,32},{32,64},{64,96},{96,0},{1,33},{33,65},{65,97},{97,1},{2,34}... | collective-permute-start | bytes 3538952 | tf_op jit(solution)/shard_map/ppermute | solution.py:29
  69.3 25.4 %collective-permute-done.3 = bf16[384,1536]{0,1:T(8,128)(2,1)S(1)} collective-permute-done((bf16[384,1536]{0,1:T(8,128)(2,1)}, bf16[384,1536]{0,1:T(8,128)(2,1)S(1)}, u32[]{:S(2)}, u32[]{:S(2)}) %collective-permute-start.3) | collective-permute-done | bytes 1179680 | tf_op jit(solution)/shard_map/ppermute | solution.py:29
  94.7 2.7 %collective-permute-start.5 = (bf16[384,1536]{0,1:T(8,128)(2,1)}, bf16[384,1536]{0,1:T(8,128)(2,1)S(1)}, u32[]{:S(2)}, u32[]{:S(2)}) collective-permute-start(bf16[384,1536]{0,1:T(8,128)(2,1)} %get-tuple-element.6), channel_id=1, source_target_pairs={{0,96},{32,0},{64,32},{96,64},{1,97},{33,1},{65,33},{97,65},{2,98}... | collective-permute-start | bytes 3538952 | tf_op jit(solution)/shard_map/ppermute | solution.py:29
  97.3 0.1 broadcast_in_dim.33
  97.4 0.1 reshape.16
  97.5 0.1 broadcast_in_dim.34
  97.6 0.4 copy.17
  98.0 1.1 constant_dynamic-update-slice_fusion.2
  99.1 20.8 %collective-permute-done.4 = bf16[384,1536]{0,1:T(8,128)(2,1)} collective-permute-done((bf16[384,1536]{0,1:T(8,128)(2,1)S(1)}, bf16[384,1536]{0,1:T(8,128)(2,1)}, u32[]{:S(2)}, u32[]{:S(2)}) %collective-permute-start.4) | collective-permute-done | bytes 1179680 | tf_op jit(solution)/shard_map/ppermute | solution.py:29
  120.0 2.5 %constant_dynamic-update-slice_fusion.1 = bf16[384,6144]{0,1:T(8,128)(2,1)} fusion(bf16[384,6144]{0,1:T(8,128)(2,1)} %constant_dynamic-update-slice_fusion.2, bf16[384,1536]{0,1:T(8,128)(2,1)} %collective-permute-done.4, s32[]{:T(128)S(6)} %select_n.112), kind=kLoop, calls=%fused_computation.17 | loop fusion | bytes 2359300 | tf_op jit(solution)/shard_map/dynamic_update_slice | solution.py:47
  122.4 1.1 constant_dynamic-update-slice_fusion
  123.6 9.7 %fusion.2 = (bf16[768,384]{1,0:T(8,128)(2,1)}, f32[768,384]{1,0:T(8,128)S(1)}) fusion(pred[768,384]{1,0:T(32,128)(4,1)S(1)} %copy.17, bf16[768,6144]{1,0:T(8,128)(2,1)} %all-gather.3.cloned.1.call-done, bf16[384,6144]{0,1:T(8,128)(2,1)} %constant_dynamic-update-slice_fusion), kind=kOutput, calls=%fused_computation.24 | convolution fusion | flops 3624468480 | bytes 16220160 | tf_op jit(solution)/shard_map/dot_general | solution.py:71
  133.3 65.3 %all-gather.5.cloned.1.call-done = bf16[768,6144]{1,0:T(8,128)(2,1)} async-done(((bf16[768,384]{1,0:T(8,128)(2,1)}), bf16[768,6144]{1,0:T(8,128)(2,1)}) %all-gather.5.cloned.1.call-update) | async-done | bytes 9437200 | tf_op jit(solution)/shard_map/all_gather | solution.py:101
  198.5 9.7 %select_convert_fusion = bf16[768,384]{1,0:T(8,128)(2,1)} fusion(pred[768,384]{1,0:T(32,128)(4,1)S(1)} %copy.18, f32[768,384]{1,0:T(8,128)S(1)} %get-tuple-element.14, bf16[768,6144]{1,0:T(8,128)(2,1)} %all-gather.5.cloned.1.call-done, bf16[384,6144]{0,1:T(8,128)(2,1)} %constant_dynamic-update-slice_fusion), kind=kOutput, calls=%fused_computation.3 | convolution fusion | flops 3625353216 | bytes 16220160 | tf_op jit(solution)/shard_map/dot_general | solution.py:71
  (20 shorter events, 0.3 us)
Async XLA Ops:
  6.5 3.7 %copy-start = (s32[96,3]{0,1:T(4,128)S(1)}, s32[96,3]{0,1:T(4,128)}, u32[]{:S(2)}) copy-start(s32[96,3]{0,1:T(4,128)} %param.3) | copy-start | bytes 3460
  6.5 117.0 %all-gather.3.cloned.1.call-start = ((), (), s32[]{:S(2)}) async-start(), calls=%async_computation | async-start | bytes 10027008 | tf_op jit(solution)/shard_map/all_gather | solution.py:97
  7.9 3.3 %collective-permute-start = (bf16[384,384]{0,1:T(8,128)(2,1)S(1)}, bf16[384,384]{0,1:T(8,128)(2,1)S(1)}, u32[]{:S(2)}, u32[]{:S(2)}) collective-permute-start(bf16[384,384]{0,1:T(8,128)(2,1)S(1)} %copy.19), channel_id=1, source_target_pairs={{0,0},{1,1},{2,16},{3,17},{4,32},{5,33},{6,48},{7,49},{8,64},{9,65... | collective-permute-start | bytes 884744 | tf_op jit(solution)/shard_map/ppermute | solution.py:63
  8.8 2.7 %copy-start.3 = (bf16[768,384]{1,0:T(8,128)(2,1)S(1)}, bf16[768,384]{1,0:T(8,128)(2,1)}, u32[]{:S(2)}) copy-start(bf16[768,384]{1,0:T(8,128)(2,1)} %param.2) | copy-start | bytes 1769476
  8.8 2.7 %collective-permute-start.1 = (bf16[384,384]{0,1:T(8,128)(2,1)S(1)}, bf16[384,384]{0,1:T(8,128)(2,1)S(1)}, u32[]{:S(2)}, u32[]{:S(2)}) collective-permute-start(bf16[384,384]{0,1:T(8,128)(2,1)S(1)} %copy.20), channel_id=1, source_target_pairs={{0,1},{1,0},{2,17},{3,16},{4,33},{5,32},{6,49},{7,48},{8,65},{9,64... | collective-permute-start | bytes 884744 | tf_op jit(solution)/shard_map/ppermute | solution.py:63
  12.9 185.6 %all-gather.5.cloned.1.call-start = ((), (), s32[]{:S(2)}) async-start(), calls=%async_computation.1 | async-start | bytes 10027008 | tf_op jit(solution)/shard_map/all_gather | solution.py:101
  13.0 40.6 %collective-permute-start.2 = (bf16[384,768]{0,1:T(8,128)(2,1)}, bf16[384,768]{0,1:T(8,128)(2,1)S(1)}, u32[]{:S(2)}, u32[]{:S(2)}) collective-permute-start(bf16[384,768]{0,1:T(8,128)(2,1)} %bitcast.15), channel_id=1, source_target_pairs={{0,16},{16,0},{1,17},{17,1},{2,18},{18,2},{3,19},{19,3},{4,20},{20... | collective-permute-start | bytes 1769480 | tf_op jit(solution)/shard_map/ppermute | solution.py:29
  35.9 18.1 %copy-start.1 = (bf16[768,384]{1,0:T(8,128)(2,1)S(1)}, bf16[768,384]{1,0:T(8,128)(2,1)}, u32[]{:S(2)}) copy-start(bf16[768,384]{1,0:T(8,128)(2,1)} %select_convert_fusion.1) | copy-start | bytes 1769476
  55.6 2.3 %copy-start.2 = (bf16[384,6144]{0,1:T(8,128)(2,1)}, bf16[384,6144]{0,1:T(8,128)(2,1)S(1)}, u32[]{:S(2)}) copy-start(bf16[384,6144]{0,1:T(8,128)(2,1)S(1)} %get-tuple-element.5) | copy-start | bytes 14155780
  57.8 36.8 %collective-permute-start.3 = (bf16[384,1536]{0,1:T(8,128)(2,1)}, bf16[384,1536]{0,1:T(8,128)(2,1)S(1)}, u32[]{:S(2)}, u32[]{:S(2)}) collective-permute-start(bf16[384,1536]{0,1:T(8,128)(2,1)} %get-tuple-element.6), channel_id=1, source_target_pairs={{0,32},{32,64},{64,96},{96,0},{1,33},{33,65},{65,97},{97,1},{2,34}... | collective-permute-start | bytes 3538952 | tf_op jit(solution)/shard_map/ppermute | solution.py:29
  94.7 25.3 %collective-permute-start.4 = (bf16[384,1536]{0,1:T(8,128)(2,1)S(1)}, bf16[384,1536]{0,1:T(8,128)(2,1)}, u32[]{:S(2)}, u32[]{:S(2)}) collective-permute-start(bf16[384,1536]{0,1:T(8,128)(2,1)S(1)} %collective-permute-done.3), channel_id=1, source_target_pairs={{0,32},{32,64},{64,96},{96,0},{1,33},{33,65},{65,97},{97,1},{2,34}... | collective-permute-start | bytes 3538952 | tf_op jit(solution)/shard_map/ppermute | solution.py:29
  94.7 27.8 %collective-permute-start.5 = (bf16[384,1536]{0,1:T(8,128)(2,1)}, bf16[384,1536]{0,1:T(8,128)(2,1)S(1)}, u32[]{:S(2)}, u32[]{:S(2)}) collective-permute-start(bf16[384,1536]{0,1:T(8,128)(2,1)} %get-tuple-element.6), channel_id=1, source_target_pairs={{0,96},{32,0},{64,32},{96,64},{1,97},{33,1},{65,33},{97,65},{2,98}... | collective-permute-start | bytes 3538952 | tf_op jit(solution)/shard_map/ppermute | solution.py:29
Sparse Core Ops, SparseCore 0:
  13.0 91.1 all-gather.2
  133.4 65.1 all-gather.4

commit v5 on v4

--- a/solution.py
+++ b/solution.py
@@ -30,10 +30,9 @@
     return jnp.concatenate(parts, 0)
 
 
-def column_panel_t(tile_t):
-    partner = chunked_shift(tile_t, "zh", [(0, 1), (1, 0)])
+def column_panel_t(tile_t, partner_t):
     zh_id = lax.axis_index("zh")
-    pair = jnp.where(zh_id == 0, jnp.concatenate([tile_t, partner], 1), jnp.concatenate([partner, tile_t], 1))
+    pair = jnp.where(zh_id == 0, jnp.concatenate([tile_t, partner_t], 1), jnp.concatenate([partner_t, tile_t], 1))
     ring = lax.axis_size("y")
     up = [(i, (i + 1) % ring) for i in range(ring)]
     down = [(i, (i - 1) % ring) for i in range(ring)]
@@ -48,23 +47,41 @@
     return panel
 
 
-def mirror_tile(upper_stored, rows, cols):
+def mirror_tiles(upper_stored, rows, cols):
+    half_width = upper_stored.shape[1]
+    col_id = lax.axis_index(COL)
+    h_own = col_id % 2
+    mirrors = []
+    for row_flip in range(2):
+        pieces = []
+        for k in range(2):
+            half = (col_id + k) % 2
+            piece = lax.dynamic_slice_in_dim(upper_stored, half * half_width, half_width, 0)
+            pairs = []
+            for a in range(rows):
+                for b in range(cols):
+                    h = (b + k) % 2
+                    pairs.append((a * cols + b, ((b // 2) ^ row_flip) * cols + 2 * a + h))
+            pieces.append(lax.ppermute(piece, ROW + COL, pairs))
+        first = jnp.where(h_own == 0, pieces[0], pieces[1])
+        second = jnp.where(h_own == 0, pieces[1], pieces[0])
+        mirrors.append(jnp.concatenate([first, second], 1).T)
+    return mirrors
+
+
+def density_tile(upper_stored, mirrored, block_cells, row_id, col_id, order_total):
     tile_side, half_width = upper_stored.shape
-    col_id = lax.axis_index(COL)
-    pieces = []
-    for k in range(2):
-        half = (col_id + k) % 2
-        piece = lax.dynamic_slice_in_dim(upper_stored, half * half_width, half_width, 0)
-        pairs = []
-        for a in range(rows):
-            for b in range(cols):
-                h = (b + k) % 2
-                pairs.append((a * cols + b, (b // 2) * cols + 2 * a + h))
-        pieces.append(lax.ppermute(piece, ROW + COL, pairs))
-    h_own = col_id % 2
-    first = jnp.where(h_own == 0, pieces[0], pieces[1])
-    second = jnp.where(h_own == 0, pieces[1], pieces[0])
-    return jnp.concatenate([first, second], 1).T
+    global_rows = row_id * tile_side + lax.broadcasted_iota(jnp.int32, (tile_side, half_width), 0)
+    global_cols = col_id * half_width + lax.broadcasted_iota(jnp.int32, (tile_side, half_width), 1)
+    symmetric = jnp.where(global_rows <= global_cols, upper_stored, mirrored)
+    near = cell_mask(
+        block_cells, row_id * (tile_side // BLK), tile_side // BLK,
+        col_id * (half_width // BLK), half_width // BLK, NEAR
+    )
+    diagonal = jnp.where(global_rows == global_cols, 0.5, 0.0).astype(jnp.float32)
+    value_scale = 2.0 / math.sqrt(order_total)
+    density_full = diagonal + value_scale * symmetric.astype(jnp.float32)
+    return jnp.where(near, density_full, 0.0).astype(jnp.bfloat16), near
 
 
 def dot_t(left, right_t):
@@ -78,24 +95,18 @@
     col_id = lax.axis_index(COL)
     tile_side, half_width = upper_stored.shape
     order_total = tile_side * rows
-    tile_blocks = tile_side // BLK
-    half_blocks = half_width // BLK
-    mirrored = mirror_tile(upper_stored, rows, cols)
-    global_rows = row_id * tile_side + lax.broadcasted_iota(jnp.int32, (tile_side, half_width), 0)
-    global_cols = col_id * half_width + lax.broadcasted_iota(jnp.int32, (tile_side, half_width), 1)
-    symmetric = jnp.where(global_rows <= global_cols, upper_stored, mirrored)
-    near_own = cell_mask(
-        block_cells, row_id * tile_blocks, tile_blocks, col_id * half_blocks, half_blocks, NEAR
+    partner_upper = lax.ppermute(upper_stored, "zh", [(0, 1), (1, 0)])
+    mirrored, partner_mirrored = mirror_tiles(upper_stored, rows, cols)
+    density, near_own = density_tile(upper_stored, mirrored, block_cells, row_id, col_id, order_total)
+    partner_density, _ = density_tile(
+        partner_upper, partner_mirrored, block_cells, row_id ^ 1, col_id, order_total
     )
     far_own = cell_mask(
-        block_cells, row_id * tile_blocks, tile_blocks, col_id * half_blocks, half_blocks, FAR
+        block_cells, row_id * (tile_side // BLK), tile_side // BLK,
+        col_id * (half_width // BLK), half_width // BLK, FAR
     )
-    diagonal = jnp.where(global_rows == global_cols, 0.5, 0.0).astype(jnp.float32)
-    value_scale = 2.0 / math.sqrt(order_total)
-    density_full = diagonal + value_scale * symmetric.astype(jnp.float32)
-    density = jnp.where(near_own, density_full, 0.0).astype(jnp.bfloat16)
     row_panel = lax.all_gather(density, COL, axis=1, tiled=True)
-    col_panel_t = column_panel_t(density.T)
+    col_panel_t = column_panel_t(density.T, partner_density.T)
     square = jnp.where(far_own, dot_t(row_panel, col_panel_t), 0.0)
     square_low = square.astype(jnp.bfloat16)
     low_panel = lax.all_gather(square_low, COL, axis=1, tiled=True)

time: 215 us -> 233 us (1.084)
  waiting for transfers between devices: 129 us -> 166 us
  starting transfers between devices: 39.2 us -> 16.8 us
    ppermute x2 -> x5, waiting for transfers between devices: 0.27 us -> 55.4 us  [the longest x4 42.9 us: mirror_tiles(): pieces.append(lax.ppermute(piece, ROW + COL, pairs))]
    ppermute x4 -> x3, starting transfers between devices: 37 us -> 4.98 us  [chunked_shift(): lax.ppermute(value[i * step:(i + 1) * step], axis, pairs)]
    ppermute x4 -> x3, waiting for transfers between devices: 63.9 us -> 49.1 us  [chunked_shift(): lax.ppermute(value[i * step:(i + 1) * step], axis, pairs)]
    ppermute x2 -> x5, starting transfers between devices: 2.14 us -> 11.8 us  [the longest x4 10.6 us: mirror_tiles(): pieces.append(lax.ppermute(piece, ROW + COL, pairs))]
    all_gather x1, waiting for transfers between devices: 65.3 us -> 61.1 us  [per_device(): low_panel = lax.all_gather(square_low, COL, axis=1, tiled=True)]
  transfers between devices with their start and end apart: 8 -> 10, of which waited for: 5 -> 6; matrix products, arithmetic and copies ran while one was open for 4% -> 4% of each run, Pallas kernels for 0% -> 0%
where the time goes in v5:
time: 233 us; the launch traced here: 232 us
  waiting for transfers between devices  166 us (71%)
  matrix products  19.4 us (8%)
  starting transfers between devices  16.8 us (7%)
  between operations  13.6 us (6%)
  local copies, waits for them, and re-layouts  11.8 us (5%)
  other arithmetic  5.04 us (2%)
    all_gather x1, waiting for transfers between devices, per_device(): low_panel = lax.all_gather(square_low, COL, axis=1, tiled=True)  61.1 us
    ppermute x3, waiting for transfers between devices, chunked_shift(): lax.ppermute(value[i * step:(i + 1) * step], axis, pairs)  49.1 us
    ppermute x4, waiting for transfers between devices, mirror_tiles(): pieces.append(lax.ppermute(piece, ROW + COL, pairs))  42.9 us
    dot_general x2, matrix products, dot_t(): lax.dot_general(left, right_t, (((1,), (1,)), ((), ())), preferred_elemen...  19.4 us
    ppermute x1, waiting for transfers between devices, per_device(): partner_upper = lax.ppermute(upper_stored, 'zh', [(0, 1), (1, 0)])  12.6 us
    ppermute x4, starting transfers between devices, mirror_tiles(): pieces.append(lax.ppermute(piece, ROW + COL, pairs))  10.6 us
    ppermute x3, starting transfers between devices, chunked_shift(): lax.ppermute(value[i * step:(i + 1) * step], axis, pairs)  4.98 us
    dynamic_update_slice x3, local copies, waits for them, and re-layouts, column_panel_t(): lax.dynamic_update_slice_in_dim(panel, part, (y_id + offset) % ring * wid...  4.75 us
  transfers between devices with their start and end apart: 10, of which 6 were waited for; matrix products, arithmetic and copies ran while one was open for 4% of the time, Pallas kernels for 0%

profile of v5, /device:TPU:1, one launch (start us, length us, event | category | flops | bytes accessed | tf_op | source)
XLA Modules:
  0.0 232.3 jit_solution(7418913905646673901)
XLA Ops:
  6.5 1.2 constant_dynamic-slice_fusion.2
  7.7 0.2 copy.23
  7.9 0.7 collective-permute-start
  8.6 6.0 %collective-permute-start.3 = (bf16[384,384]{0,1:T(8,128)(2,1)S(1)}, bf16[384,384]{0,1:T(8,128)(2,1)S(1)}, u32[]{:S(2)}, u32[]{:S(2)}) collective-permute-start(bf16[384,384]{0,1:T(8,128)(2,1)S(1)} %copy.23), channel_id=1, source_target_pairs={{0,16},{1,17},{2,0},{3,1},{4,48},{5,49},{6,32},{7,33},{8,80},{9,81... | collective-permute-start | bytes 884744 | tf_op jit(solution)/shard_map/ppermute | solution.py:65
  14.6 0.2 copy.24
  14.9 1.3 collective-permute-start.1
  16.2 2.6 %collective-permute-start.4 = (bf16[384,384]{0,1:T(8,128)(2,1)S(1)}, bf16[384,384]{0,1:T(8,128)(2,1)S(1)}, u32[]{:S(2)}, u32[]{:S(2)}) collective-permute-start(bf16[384,384]{0,1:T(8,128)(2,1)S(1)} %copy.24), channel_id=1, source_target_pairs={{0,17},{1,16},{2,1},{3,0},{4,49},{5,48},{6,33},{7,32},{8,81},{9,80... | collective-permute-start | bytes 884744 | tf_op jit(solution)/shard_map/ppermute | solution.py:65
  18.8 1.2 collective-permute-start.2
  20.4 0.1 reshape.25
  20.5 0.5 copy.20
  21.3 0.4 copy.22
  21.7 1.0 broadcast_select_fusion.3
  22.7 30.2 %collective-permute-done.3 = bf16[384,384]{0,1:T(8,128)(2,1)S(1)} collective-permute-done((bf16[384,384]{0,1:T(8,128)(2,1)S(1)}, bf16[384,384]{0,1:T(8,128)(2,1)S(1)}, u32[]{:S(2)}, u32[]{:S(2)}) %collective-permute-start.3) | collective-permute-done | bytes 294944 | tf_op jit(solution)/shard_map/ppermute | solution.py:65
  52.9 12.6 %collective-permute-done.4 = bf16[384,384]{0,1:T(8,128)(2,1)S(1)} collective-permute-done((bf16[384,384]{0,1:T(8,128)(2,1)S(1)}, bf16[384,384]{0,1:T(8,128)(2,1)S(1)}, u32[]{:S(2)}, u32[]{:S(2)}) %collective-permute-start.4) | collective-permute-done | bytes 294944 | tf_op jit(solution)/shard_map/ppermute | solution.py:65
  65.6 12.6 %collective-permute-done.2 = bf16[768,384]{1,0:T(8,128)(2,1)S(1)} collective-permute-done((bf16[768,384]{1,0:T(8,128)(2,1)S(1)}, bf16[768,384]{1,0:T(8,128)(2,1)S(1)}, u32[]{:S(2)}, u32[]{:S(2)}) %collective-permute-start.2) | collective-permute-done | bytes 589856 | tf_op jit(solution)/shard_map/ppermute | solution.py:98
  78.2 2.3 fusion
  80.6 0.4 broadcast_in_dim.48
  81.0 0.6 copy-done
  81.6 1.6 constant_dynamic-update-slice_fusion.3
  83.2 2.2 copy-done.1
  85.5 2.3 collective-permute-start.5
  87.8 26.1 %collective-permute-done.5 = bf16[384,1536]{0,1:T(8,128)(2,1)S(1)} collective-permute-done((bf16[384,1536]{0,1:T(8,128)(2,1)}, bf16[384,1536]{0,1:T(8,128)(2,1)S(1)}, u32[]{:S(2)}, u32[]{:S(2)}) %collective-permute-start.5) | collective-permute-done | bytes 1179680 | tf_op jit(solution)/shard_map/ppermute | solution.py:29
  113.9 1.3 collective-permute-start.6
  115.1 1.4 collective-permute-start.7
  116.8 0.4 copy.21
  117.2 1.1 constant_dynamic-update-slice_fusion.2
  118.3 23.0 %collective-permute-done.6 = bf16[384,1536]{0,1:T(8,128)(2,1)} collective-permute-done((bf16[384,1536]{0,1:T(8,128)(2,1)S(1)}, bf16[384,1536]{0,1:T(8,128)(2,1)}, u32[]{:S(2)}, u32[]{:S(2)}) %collective-permute-start.6) | collective-permute-done | bytes 1179680 | tf_op jit(solution)/shard_map/ppermute | solution.py:29
  141.3 2.5 %constant_dynamic-update-slice_fusion.1 = bf16[384,6144]{0,1:T(8,128)(2,1)} fusion(bf16[384,6144]{0,1:T(8,128)(2,1)} %constant_dynamic-update-slice_fusion.2, bf16[384,1536]{0,1:T(8,128)(2,1)} %collective-permute-done.6, s32[]{:T(128)S(6)} %select_n.145), kind=kLoop, calls=%fused_computation.24 | loop fusion | bytes 2359300 | tf_op jit(solution)/shard_map/dynamic_update_slice | solution.py:46
  143.8 1.1 constant_dynamic-update-slice_fusion
  144.9 9.7 %fusion.5 = (bf16[768,384]{1,0:T(8,128)(2,1)}, f32[768,384]{1,0:T(8,128)S(1)}) fusion(pred[768,384]{1,0:T(32,128)(4,1)S(1)} %copy.21, bf16[768,6144]{1,0:T(8,128)(2,1)} %all-gather.3.cloned.1.call-done, bf16[384,6144]{0,1:T(8,128)(2,1)} %constant_dynamic-update-slice_fusion), kind=kOutput, calls=%fused_computation.36 | convolution fusion | flops 3624468480 | bytes 16220160 | tf_op jit(solution)/shard_map/dot_general | solution.py:88
  154.6 61.1 %all-gather.5.cloned.1.call-done = bf16[768,6144]{1,0:T(8,128)(2,1)} async-done(((bf16[768,384]{1,0:T(8,128)(2,1)}), bf16[768,6144]{1,0:T(8,128)(2,1)}) %all-gather.5.cloned.1.call-update) | async-done | bytes 9437200 | tf_op jit(solution)/shard_map/all_gather | solution.py:112
  215.7 9.7 %select_convert_fusion = bf16[768,384]{1,0:T(8,128)(2,1)} fusion(pred[768,384]{1,0:T(32,128)(4,1)S(1)} %copy.22, f32[768,384]{1,0:T(8,128)S(1)} %get-tuple-element.22, bf16[768,6144]{1,0:T(8,128)(2,1)} %all-gather.5.cloned.1.call-done, bf16[384,6144]{0,1:T(8,128)(2,1)} %constant_dynamic-update-slice_fusion), kind=kOutput, calls=%fused_computation.3 | convolution fusion | flops 3625353216 | bytes 16220160 | tf_op jit(solution)/shard_map/dot_general | solution.py:88
  (29 shorter events, 1.1 us)
Async XLA Ops:
  6.5 138.4 %all-gather.3.cloned.1.call-start = ((), (), s32[]{:S(2)}) async-start(), calls=%async_computation | async-start | bytes 10027008 | tf_op jit(solution)/shard_map/all_gather | solution.py:108
  6.5 12.3 %copy-start.2 = (bf16[768,384]{1,0:T(8,128)(2,1)S(1)}, bf16[768,384]{1,0:T(8,128)(2,1)}, u32[]{:S(2)}) copy-start(bf16[768,384]{1,0:T(8,128)(2,1)} %param.2) | copy-start | bytes 1769476
  6.5 13.5 %copy-start.3 = (s32[96,3]{0,1:T(4,128)S(1)}, s32[96,3]{0,1:T(4,128)}, u32[]{:S(2)}) copy-start(s32[96,3]{0,1:T(4,128)} %param.3) | copy-start | bytes 3460
  7.9 13.7 %collective-permute-start = (bf16[384,384]{0,1:T(8,128)(2,1)S(1)}, bf16[384,384]{0,1:T(8,128)(2,1)S(1)}, u32[]{:S(2)}, u32[]{:S(2)}) collective-permute-start(bf16[384,384]{0,1:T(8,128)(2,1)S(1)} %copy.23), channel_id=1, source_target_pairs={{0,0},{1,1},{2,16},{3,17},{4,32},{5,33},{6,48},{7,49},{8,64},{9,65... | collective-permute-start | bytes 884744 | tf_op jit(solution)/shard_map/ppermute | solution.py:65
  8.6 44.3 %collective-permute-start.3 = (bf16[384,384]{0,1:T(8,128)(2,1)S(1)}, bf16[384,384]{0,1:T(8,128)(2,1)S(1)}, u32[]{:S(2)}, u32[]{:S(2)}) collective-permute-start(bf16[384,384]{0,1:T(8,128)(2,1)S(1)} %copy.23), channel_id=1, source_target_pairs={{0,16},{1,17},{2,0},{3,1},{4,48},{5,49},{6,32},{7,33},{8,80},{9,81... | collective-permute-start | bytes 884744 | tf_op jit(solution)/shard_map/ppermute | solution.py:65
  14.9 6.8 %collective-permute-start.1 = (bf16[384,384]{0,1:T(8,128)(2,1)S(1)}, bf16[384,384]{0,1:T(8,128)(2,1)}, u32[]{:S(2)}, u32[]{:S(2)}) collective-permute-start(bf16[384,384]{0,1:T(8,128)(2,1)S(1)} %copy.24), channel_id=1, source_target_pairs={{0,1},{1,0},{2,17},{3,16},{4,33},{5,32},{6,49},{7,48},{8,65},{9,64... | collective-permute-start | bytes 884744 | tf_op jit(solution)/shard_map/ppermute | solution.py:65
  16.2 49.4 %collective-permute-start.4 = (bf16[384,384]{0,1:T(8,128)(2,1)S(1)}, bf16[384,384]{0,1:T(8,128)(2,1)S(1)}, u32[]{:S(2)}, u32[]{:S(2)}) collective-permute-start(bf16[384,384]{0,1:T(8,128)(2,1)S(1)} %copy.24), channel_id=1, source_target_pairs={{0,17},{1,16},{2,1},{3,0},{4,49},{5,48},{6,33},{7,32},{8,81},{9,80... | collective-permute-start | bytes 884744 | tf_op jit(solution)/shard_map/ppermute | solution.py:65
  18.8 59.4 %collective-permute-start.2 = (bf16[768,384]{1,0:T(8,128)(2,1)S(1)}, bf16[768,384]{1,0:T(8,128)(2,1)S(1)}, u32[]{:S(2)}, u32[]{:S(2)}) collective-permute-start(bf16[768,384]{1,0:T(8,128)(2,1)S(1)} %copy-done.2), channel_id=1, source_target_pairs={{0,16},{16,0},{1,17},{17,1},{2,18},{18,2},{3,19},{19,3},{4,20},{20... | collective-permute-start | bytes 1769480 | tf_op jit(solution)/shard_map/ppermute | solution.py:98
  80.5 135.3 %all-gather.5.cloned.1.call-start = ((), (), s32[]{:S(2)}) async-start(), calls=%async_computation.1 | async-start | bytes 10027008 | tf_op jit(solution)/shard_map/all_gather | solution.py:112
  80.6 1.1 copy-start
  83.2 2.2 copy-start.1
  85.5 28.4 %collective-permute-start.5 = (bf16[384,1536]{0,1:T(8,128)(2,1)}, bf16[384,1536]{0,1:T(8,128)(2,1)S(1)}, u32[]{:S(2)}, u32[]{:S(2)}) collective-permute-start(bf16[384,1536]{0,1:T(8,128)(2,1)} %get-tuple-element.8), channel_id=1, source_target_pairs={{0,32},{32,64},{64,96},{96,0},{1,33},{33,65},{65,97},{97,1},{2,34}... | collective-permute-start | bytes 3538952 | tf_op jit(solution)/shard_map/ppermute | solution.py:29
  113.9 27.4 %collective-permute-start.6 = (bf16[384,1536]{0,1:T(8,128)(2,1)S(1)}, bf16[384,1536]{0,1:T(8,128)(2,1)}, u32[]{:S(2)}, u32[]{:S(2)}) collective-permute-start(bf16[384,1536]{0,1:T(8,128)(2,1)S(1)} %collective-permute-done.5), channel_id=1, source_target_pairs={{0,32},{32,64},{64,96},{96,0},{1,33},{33,65},{65,97},{97,1},{2,34}... | collective-permute-start | bytes 3538952 | tf_op jit(solution)/shard_map/ppermute | solution.py:29
  115.1 28.7 %collective-permute-start.7 = (bf16[384,1536]{0,1:T(8,128)(2,1)}, bf16[384,1536]{0,1:T(8,128)(2,1)S(1)}, u32[]{:S(2)}, u32[]{:S(2)}) collective-permute-start(bf16[384,1536]{0,1:T(8,128)(2,1)} %get-tuple-element.8), channel_id=1, source_target_pairs={{0,96},{32,0},{64,32},{96,64},{1,97},{33,1},{65,33},{97,65},{2,98}... | collective-permute-start | bytes 3538952 | tf_op jit(solution)/shard_map/ppermute | solution.py:29
Sparse Core Ops, SparseCore 0:
  80.6 60.2 all-gather.2
  154.7 60.9 all-gather.4

commit v6 on v4

--- a/solution.py
+++ b/solution.py
@@ -30,22 +30,28 @@
     return jnp.concatenate(parts, 0)
 
 
+def ring_gather(tile_t, panel, plane):
+    ring = lax.axis_size("y")
+    up = [(i, (i + 1) % ring) for i in range(ring)]
+    down = [(i, (i - 1) % ring) for i in range(ring)]
+    from_below = chunked_shift(tile_t, "y", up)
+    from_above = chunked_shift(tile_t, "y", down)
+    from_two_below = chunked_shift(from_below, "y", up)
+    y_id = lax.axis_index("y")
+    width = tile_t.shape[1]
+    for offset, part in ((0, tile_t), (-1, from_below), (-2, from_two_below), (1, from_above)):
+        position = ((y_id + offset) % ring) * 2 + plane
+        panel = lax.dynamic_update_slice_in_dim(panel, part, position * width, 1)
+    return panel
+
+
 def column_panel_t(tile_t):
     partner = chunked_shift(tile_t, "zh", [(0, 1), (1, 0)])
     zh_id = lax.axis_index("zh")
-    pair = jnp.where(zh_id == 0, jnp.concatenate([tile_t, partner], 1), jnp.concatenate([partner, tile_t], 1))
     ring = lax.axis_size("y")
-    up = [(i, (i + 1) % ring) for i in range(ring)]
-    down = [(i, (i - 1) % ring) for i in range(ring)]
-    from_below = chunked_shift(pair, "y", up)
-    from_above = chunked_shift(pair, "y", down)
-    from_two_below = chunked_shift(from_below, "y", up)
-    y_id = lax.axis_index("y")
-    width = pair.shape[1]
-    panel = jnp.zeros((pair.shape[0], ring * width), pair.dtype)
-    for offset, part in ((0, pair), (-1, from_below), (-2, from_two_below), (1, from_above)):
-        panel = lax.dynamic_update_slice_in_dim(panel, part, ((y_id + offset) % ring) * width, 1)
-    return panel
+    panel = jnp.zeros((tile_t.shape[0], 2 * ring * tile_t.shape[1]), tile_t.dtype)
+    panel = ring_gather(tile_t, panel, zh_id)
+    return ring_gather(partner, panel, 1 - zh_id)
 
 
 def mirror_tile(upper_stored, rows, cols):

time: 215 us -> 196 us (0.912)
  waiting for transfers between devices: 129 us -> 93.6 us
  starting transfers between devices: 39.2 us -> 54.6 us
  local copies, waits for them, and re-layouts: 10.4 us -> 13 us
    ppermute x4 -> x7, waiting for transfers between devices: 63.9 us -> 31.3 us  [chunked_shift(): lax.ppermute(value[i * step:(i + 1) * step], axis, pairs)]
    ppermute x4 -> x7, starting transfers between devices: 37 us -> 52.4 us  [chunked_shift(): lax.ppermute(value[i * step:(i + 1) * step], axis, pairs)]
    all_gather x1, waiting for transfers between devices: 65.3 us -> 62 us  [per_device(): low_panel = lax.all_gather(square_low, COL, axis=1, tiled=True)]
    dynamic_update_slice x3 -> x7, local copies, waits for them, and re-layouts: 4.74 us -> 7.31 us  [ring_gather(): panel = lax.dynamic_update_slice_in_dim(panel, part, position * width, 1)]
    unnamed x10 -> x6, local copies, waits for them, and re-layouts: 2.7 us -> 0.44 us
    broadcast_in_dim x1, local copies, waits for them, and re-layouts: 0.41 us -> 2.66 us  [column_panel_t(): jnp.zeros((tile_t.shape[0], 2 * ring * tile_t.shape[1]), tile_t.dtype)]
  transfers between devices with their start and end apart: 8 -> 11, of which waited for: 5 -> 6; matrix products, arithmetic and copies ran while one was open for 4% -> 5% of each run, Pallas kernels for 0% -> 0%
where the time goes in v6:
time: 196 us
  waiting for transfers between devices  93.6 us (48%)
  starting transfers between devices  54.6 us (28%)
  matrix products  19.4 us (10%)
  between operations  13.6 us (7%)
  local copies, waits for them, and re-layouts  13 us (7%)
    all_gather x1, waiting for transfers between devices, per_device(): low_panel = lax.all_gather(square_low, COL, axis=1, tiled=True)  62 us
    ppermute x7, starting transfers between devices, chunked_shift(): lax.ppermute(value[i * step:(i + 1) * step], axis, pairs)  52.4 us
    ppermute x7, waiting for transfers between devices, chunked_shift(): lax.ppermute(value[i * step:(i + 1) * step], axis, pairs)  31.3 us
    dot_general x2, matrix products, dot_t(): lax.dot_general(left, right_t, (((1,), (1,)), ((), ())), preferred_elemen...  19.4 us
    dynamic_update_slice x7, local copies, waits for them, and re-layouts, ring_gather(): panel = lax.dynamic_update_slice_in_dim(panel, part, position * width, 1)  7.31 us
  transfers between devices with their start and end apart: 11, of which 6 were waited for; matrix products, arithmetic and copies ran while one was open for 5% of the time, Pallas kernels for 0%

profile of v6, /device:TPU:1, one launch (start us, length us, event | category | flops | bytes accessed | tf_op | source)
XLA Modules:
  0.0 195.9 jit_solution(17529377519830692849)
XLA Ops:
  6.5 1.2 constant_dynamic-slice_fusion.1
  7.7 0.2 copy.19
  7.9 0.7 collective-permute-start
  8.6 0.2 copy.20
  8.9 1.5 collective-permute-start.1
  10.5 0.1 fusion.1
  10.7 0.1 reshape.14
  10.8 0.4 copy.18
  11.3 0.2 collective-permute-done.1
  11.6 2.7 %broadcast_in_dim.37 = bf16[384,6144]{0,1:T(8,128)(2,1)} broadcast(bf16[]{:T(256)} %constant.98.clone.1), dimensions={} | broadcast | bytes 4718594 | tf_op jit(solution)/shard_map/broadcast_in_dim | solution.py:52
  14.2 1.5 constant_dynamic-update-slice_fusion.7
  15.9 23.0 %collective-permute-start.5 = (bf16[384,768]{0,1:T(8,128)(2,1)}, bf16[384,768]{0,1:T(8,128)(2,1)S(1)}, u32[]{:S(2)}, u32[]{:S(2)}) collective-permute-start(bf16[384,768]{0,1:T(8,128)(2,1)} %bitcast.17), channel_id=1, source_target_pairs={{0,16},{16,0},{1,17},{17,1},{2,18},{18,2},{3,19},{19,3},{4,20},{20... | collective-permute-start | bytes 1769480 | tf_op jit(solution)/shard_map/ppermute | solution.py:29
  38.8 11.8 %collective-permute-start.2 = (bf16[384,768]{0,1:T(8,128)(2,1)}, bf16[384,768]{0,1:T(8,128)(2,1)S(1)}, u32[]{:S(2)}, u32[]{:S(2)}) collective-permute-start(bf16[384,768]{0,1:T(8,128)(2,1)} %bitcast.18), channel_id=1, source_target_pairs={{0,32},{32,64},{64,96},{96,0},{1,33},{33,65},{65,97},{97,1},{2,34}... | collective-permute-start | bytes 1769480 | tf_op jit(solution)/shard_map/ppermute | solution.py:29
  50.6 3.1 %collective-permute-done.5 = bf16[384,768]{0,1:T(8,128)(2,1)S(1)} collective-permute-done((bf16[384,768]{0,1:T(8,128)(2,1)}, bf16[384,768]{0,1:T(8,128)(2,1)S(1)}, u32[]{:S(2)}, u32[]{:S(2)}) %collective-permute-start.5) | collective-permute-done | bytes 589856 | tf_op jit(solution)/shard_map/ppermute | solution.py:29
  53.7 14.3 %collective-permute-start.6 = (bf16[384,768]{0,1:T(8,128)(2,1)S(1)}, bf16[384,768]{0,1:T(8,128)(2,1)S(1)}, u32[]{:S(2)}, u32[]{:S(2)}) collective-permute-start(bf16[384,768]{0,1:T(8,128)(2,1)S(1)} %collective-permute-done.5), channel_id=1, source_target_pairs={{0,32},{32,64},{64,96},{96,0},{1,33},{33,65},{65,97},{97,1},{2,34}... | collective-permute-start | bytes 1769480 | tf_op jit(solution)/shard_map/ppermute | solution.py:29
  67.9 2.7 %collective-permute-start.4 = (bf16[384,768]{0,1:T(8,128)(2,1)}, bf16[384,768]{0,1:T(8,128)(2,1)S(1)}, u32[]{:S(2)}, u32[]{:S(2)}) collective-permute-start(bf16[384,768]{0,1:T(8,128)(2,1)} %bitcast.19), channel_id=1, source_target_pairs={{0,96},{32,0},{64,32},{96,64},{1,97},{33,1},{65,33},{97,65},{2,98}... | collective-permute-start | bytes 1769480 | tf_op jit(solution)/shard_map/ppermute | solution.py:29
  70.7 0.1 reshape.16
  70.9 0.4 copy.17
  71.3 0.7 collective-permute-start.8
  72.0 8.5 %collective-permute-done.6 = bf16[384,768]{0,1:T(8,128)(2,1)S(1)} collective-permute-done((bf16[384,768]{0,1:T(8,128)(2,1)S(1)}, bf16[384,768]{0,1:T(8,128)(2,1)S(1)}, u32[]{:S(2)}, u32[]{:S(2)}) %collective-permute-start.6) | collective-permute-done | bytes 589856 | tf_op jit(solution)/shard_map/ppermute | solution.py:29
  80.5 0.9 constant_dynamic-update-slice_fusion.6
  81.4 11.9 %collective-permute-done.3 = bf16[384,768]{0,1:T(8,128)(2,1)} collective-permute-done((bf16[384,768]{0,1:T(8,128)(2,1)S(1)}, bf16[384,768]{0,1:T(8,128)(2,1)}, u32[]{:S(2)}, u32[]{:S(2)}) %collective-permute-start.3) | collective-permute-done | bytes 589856 | tf_op jit(solution)/shard_map/ppermute | solution.py:29
  93.3 2.0 constant_dynamic-update-slice_fusion.5
  95.2 0.9 constant_dynamic-update-slice_fusion.4
  96.1 0.9 constant_dynamic-update-slice_fusion.3
  97.0 0.9 constant_dynamic-update-slice_fusion.2
  97.9 7.9 %collective-permute-done.7 = bf16[384,768]{0,1:T(8,128)(2,1)S(1)} collective-permute-done((bf16[384,768]{0,1:T(8,128)(2,1)S(1)}, bf16[384,768]{0,1:T(8,128)(2,1)S(1)}, u32[]{:S(2)}, u32[]{:S(2)}) %collective-permute-start.7) | collective-permute-done | bytes 589856 | tf_op jit(solution)/shard_map/ppermute | solution.py:29
  105.8 0.9 constant_dynamic-update-slice_fusion.1
  106.7 0.9 constant_dynamic-update-slice_fusion
  107.6 9.7 %fusion.2 = (bf16[768,384]{1,0:T(8,128)(2,1)}, f32[768,384]{1,0:T(8,128)S(1)}) fusion(pred[768,384]{1,0:T(32,128)(4,1)S(1)} %copy.17, bf16[768,6144]{1,0:T(8,128)(2,1)} %all-gather.3.cloned.1.call-done, bf16[384,6144]{0,1:T(8,128)(2,1)} %constant_dynamic-update-slice_fusion), kind=kOutput, calls=%fused_computation.27 | convolution fusion | flops 3624468480 | bytes 16220160 | tf_op jit(solution)/shard_map/dot_general | solution.py:77
  117.3 62.0 %all-gather.5.cloned.1.call-done = bf16[768,6144]{1,0:T(8,128)(2,1)} async-done(((bf16[768,384]{1,0:T(8,128)(2,1)}), bf16[768,6144]{1,0:T(8,128)(2,1)}) %all-gather.5.cloned.1.call-update) | async-done | bytes 9437200 | tf_op jit(solution)/shard_map/all_gather | solution.py:107
  179.3 9.7 %select_convert_fusion = bf16[768,384]{1,0:T(8,128)(2,1)} fusion(pred[768,384]{1,0:T(32,128)(4,1)S(1)} %copy.18, f32[768,384]{1,0:T(8,128)S(1)} %get-tuple-element.14, bf16[768,6144]{1,0:T(8,128)(2,1)} %all-gather.5.cloned.1.call-done, bf16[384,6144]{0,1:T(8,128)(2,1)} %constant_dynamic-update-slice_fusion), kind=kOutput, calls=%fused_computation.2 | convolution fusion | flops 3625353216 | bytes 16220160 | tf_op jit(solution)/shard_map/dot_general | solution.py:77
  (25 shorter events, 0.7 us)
Async XLA Ops:
  6.5 3.8 %copy-start = (s32[96,3]{0,1:T(4,128)S(1)}, s32[96,3]{0,1:T(4,128)}, u32[]{:S(2)}) copy-start(s32[96,3]{0,1:T(4,128)} %param.3) | copy-start | bytes 3460
  6.5 7.7 %copy-start.1 = (bf16[768,384]{1,0:T(8,128)(2,1)S(1)}, bf16[768,384]{1,0:T(8,128)(2,1)}, u32[]{:S(2)}) copy-start(bf16[768,384]{1,0:T(8,128)(2,1)} %param.2) | copy-start | bytes 1769476
  6.5 101.0 %all-gather.3.cloned.1.call-start = ((), (), s32[]{:S(2)}) async-start(), calls=%async_computation | async-start | bytes 10027008 | tf_op jit(solution)/shard_map/all_gather | solution.py:103
  7.9 3.3 %collective-permute-start = (bf16[384,384]{0,1:T(8,128)(2,1)S(1)}, bf16[384,384]{0,1:T(8,128)(2,1)S(1)}, u32[]{:S(2)}, u32[]{:S(2)}) collective-permute-start(bf16[384,384]{0,1:T(8,128)(2,1)S(1)} %copy.19), channel_id=1, source_target_pairs={{0,0},{1,1},{2,16},{3,17},{4,32},{5,33},{6,48},{7,49},{8,64},{9,65... | collective-permute-start | bytes 884744 | tf_op jit(solution)/shard_map/ppermute | solution.py:69
  8.9 2.7 %collective-permute-start.1 = (bf16[384,384]{0,1:T(8,128)(2,1)S(1)}, bf16[384,384]{0,1:T(8,128)(2,1)S(1)}, u32[]{:S(2)}, u32[]{:S(2)}) collective-permute-start(bf16[384,384]{0,1:T(8,128)(2,1)S(1)} %copy.20), channel_id=1, source_target_pairs={{0,1},{1,0},{2,17},{3,16},{4,33},{5,32},{6,49},{7,48},{8,65},{9,64... | collective-permute-start | bytes 884744 | tf_op jit(solution)/shard_map/ppermute | solution.py:69
  15.8 163.5 %all-gather.5.cloned.1.call-start = ((), (), s32[]{:S(2)}) async-start(), calls=%async_computation.1 | async-start | bytes 10027008 | tf_op jit(solution)/shard_map/all_gather | solution.py:107
  15.9 37.8 %collective-permute-start.5 = (bf16[384,768]{0,1:T(8,128)(2,1)}, bf16[384,768]{0,1:T(8,128)(2,1)S(1)}, u32[]{:S(2)}, u32[]{:S(2)}) collective-permute-start(bf16[384,768]{0,1:T(8,128)(2,1)} %bitcast.17), channel_id=1, source_target_pairs={{0,16},{16,0},{1,17},{17,1},{2,18},{18,2},{3,19},{19,3},{4,20},{20... | collective-permute-start | bytes 1769480 | tf_op jit(solution)/shard_map/ppermute | solution.py:29
  38.8 29.1 %collective-permute-start.2 = (bf16[384,768]{0,1:T(8,128)(2,1)}, bf16[384,768]{0,1:T(8,128)(2,1)S(1)}, u32[]{:S(2)}, u32[]{:S(2)}) collective-permute-start(bf16[384,768]{0,1:T(8,128)(2,1)} %bitcast.18), channel_id=1, source_target_pairs={{0,32},{32,64},{64,96},{96,0},{1,33},{33,65},{65,97},{97,1},{2,34}... | collective-permute-start | bytes 1769480 | tf_op jit(solution)/shard_map/ppermute | solution.py:29
  53.7 26.9 %collective-permute-start.6 = (bf16[384,768]{0,1:T(8,128)(2,1)S(1)}, bf16[384,768]{0,1:T(8,128)(2,1)S(1)}, u32[]{:S(2)}, u32[]{:S(2)}) collective-permute-start(bf16[384,768]{0,1:T(8,128)(2,1)S(1)} %collective-permute-done.5), channel_id=1, source_target_pairs={{0,32},{32,64},{64,96},{96,0},{1,33},{33,65},{65,97},{97,1},{2,34}... | collective-permute-start | bytes 1769480 | tf_op jit(solution)/shard_map/ppermute | solution.py:29
  67.9 25.4 %collective-permute-start.3 = (bf16[384,768]{0,1:T(8,128)(2,1)S(1)}, bf16[384,768]{0,1:T(8,128)(2,1)}, u32[]{:S(2)}, u32[]{:S(2)}) collective-permute-start(bf16[384,768]{0,1:T(8,128)(2,1)S(1)} %collective-permute-done.2), channel_id=1, source_target_pairs={{0,32},{32,64},{64,96},{96,0},{1,33},{33,65},{65,97},{97,1},{2,34}... | collective-permute-start | bytes 1769480 | tf_op jit(solution)/shard_map/ppermute | solution.py:29
  67.9 27.3 %collective-permute-start.4 = (bf16[384,768]{0,1:T(8,128)(2,1)}, bf16[384,768]{0,1:T(8,128)(2,1)S(1)}, u32[]{:S(2)}, u32[]{:S(2)}) collective-permute-start(bf16[384,768]{0,1:T(8,128)(2,1)} %bitcast.19), channel_id=1, source_target_pairs={{0,96},{32,0},{64,32},{96,64},{1,97},{33,1},{65,33},{97,65},{2,98}... | collective-permute-start | bytes 1769480 | tf_op jit(solution)/shard_map/ppermute | solution.py:29
  71.3 35.4 %collective-permute-start.8 = (bf16[384,768]{0,1:T(8,128)(2,1)S(1)}, bf16[384,768]{0,1:T(8,128)(2,1)S(1)}, u32[]{:S(2)}, u32[]{:S(2)}) collective-permute-start(bf16[384,768]{0,1:T(8,128)(2,1)S(1)} %collective-permute-done.5), channel_id=1, source_target_pairs={{0,96},{32,0},{64,32},{96,64},{1,97},{33,1},{65,33},{97,65},{2,98}... | collective-permute-start | bytes 1769480 | tf_op jit(solution)/shard_map/ppermute | solution.py:29
  80.5 25.3 %collective-permute-start.7 = (bf16[384,768]{0,1:T(8,128)(2,1)S(1)}, bf16[384,768]{0,1:T(8,128)(2,1)S(1)}, u32[]{:S(2)}, u32[]{:S(2)}) collective-permute-start(bf16[384,768]{0,1:T(8,128)(2,1)S(1)} %collective-permute-done.6), channel_id=1, source_target_pairs={{0,32},{32,64},{64,96},{96,0},{1,33},{33,65},{65,97},{97,1},{2,34}... | collective-permute-start | bytes 1769480 | tf_op jit(solution)/shard_map/ppermute | solution.py:29
Sparse Core Ops, SparseCore 0:
  15.9 91.1 all-gather.2
  117.4 61.8 all-gather.4

commit v7 on v6

--- a/solution.py
+++ b/solution.py
@@ -102,11 +102,20 @@
     density = jnp.where(near_own, density_full, 0.0).astype(jnp.bfloat16)
     row_panel = lax.all_gather(density, COL, axis=1, tiled=True)
     col_panel_t = column_panel_t(density.T)
-    square = jnp.where(far_own, dot_t(row_panel, col_panel_t), 0.0)
-    square_low = square.astype(jnp.bfloat16)
-    low_panel = lax.all_gather(square_low, COL, axis=1, tiled=True)
-    cubic = dot_t(low_panel, col_panel_t)
-    return jnp.where(near_own, 3.0 * square - 2.0 * cubic, 0.0).astype(jnp.bfloat16)
+    half = tile_side // 2
+    results = []
+    squares = []
+    for part in range(2):
+        rows_part = slice(part * half, (part + 1) * half)
+        squares.append(jnp.where(far_own[rows_part], dot_t(row_panel[rows_part], col_panel_t), 0.0))
+    for part in range(2):
+        rows_part = slice(part * half, (part + 1) * half)
+        low_panel = lax.all_gather(squares[part].astype(jnp.bfloat16), COL, axis=1, tiled=True)
+        cubic = dot_t(low_panel, col_panel_t)
+        results.append(
+            jnp.where(near_own[rows_part], 3.0 * squares[part] - 2.0 * cubic, 0.0).astype(jnp.bfloat16)
+        )
+    return jnp.concatenate(results, 0)
 
 
 def solution(mesh):

time: 196 us -> 213 us (1.087)
  waiting for transfers between devices: 93.6 us -> 102 us
  matrix products: 19.4 us -> 27.1 us
    dot_general x2 -> x4, matrix products: 19.4 us -> 27.1 us  [dot_t(): lax.dot_general(left, right_t, (((1,), (1,)), ((), ())), preferred_elemen...]
    all_gather x1 -> x2, waiting for transfers between devices: 62 us -> 69.3 us  [per_device(): lax.all_gather(squares[part].astype(jnp.bfloat16), COL, axis=1, tiled=True)]
  transfers between devices with their start and end apart: 11 -> 12, of which waited for: 6 -> 6; matrix products, arithmetic and copies ran while one was open for 5% -> 11% of each run, Pallas kernels for 0% -> 0%
where the time goes in v7:
time: 213 us
  waiting for transfers between devices  102 us (48%)
  starting transfers between devices  54.4 us (26%)
  matrix products  27.1 us (13%)
  local copies, waits for them, and re-layouts  13.7 us (6%)
  between operations  13.3 us (6%)
  other arithmetic  2.53 us (1%)
    all_gather x2, waiting for transfers between devices, per_device(): lax.all_gather(squares[part].astype(jnp.bfloat16), COL, axis=1, tiled=True)  69.3 us
    ppermute x7, starting transfers between devices, chunked_shift(): lax.ppermute(value[i * step:(i + 1) * step], axis, pairs)  52 us
    ppermute x7, waiting for transfers between devices, chunked_shift(): lax.ppermute(value[i * step:(i + 1) * step], axis, pairs)  32.4 us
    dot_general x4, matrix products, dot_t(): lax.dot_general(left, right_t, (((1,), (1,)), ((), ())), preferred_elemen...  27.1 us
    dynamic_update_slice x7, local copies, waits for them, and re-layouts, ring_gather(): panel = lax.dynamic_update_slice_in_dim(panel, part, position * width, 1)  6.36 us
  transfers between devices with their start and end apart: 12, of which 6 were waited for; matrix products, arithmetic and copies ran while one was open for 11% of the time, Pallas kernels for 0%

profile of v7, /device:TPU:1, one launch (start us, length us, event | category | flops | bytes accessed | tf_op | source)
XLA Modules:
  0.0 212.8 jit_solution(15498410968157300717)
XLA Ops:
  6.5 1.1 constant_dynamic-slice_fusion.1
  7.7 0.7 collective-permute-start
  8.4 1.5 collective-permute-start.1
  10.1 1.3 copy.14
  11.7 2.7 %broadcast_in_dim.56 = bf16[384,6144]{1,0:T(8,128)(2,1)} broadcast(bf16[]{:T(256)} %constant.98.clone.1), dimensions={} | broadcast | bytes 4718594 | tf_op jit(solution)/shard_map/broadcast_in_dim | solution.py:52
  14.4 1.5 constant_dynamic-update-slice_fusion.7
  15.9 22.6 %collective-permute-start.5 = (bf16[384,768]{1,0:T(8,128)(2,1)}, bf16[384,768]{1,0:T(8,128)(2,1)S(1)}, u32[]{:S(2)}, u32[]{:S(2)}) collective-permute-start(bf16[384,768]{1,0:T(8,128)(2,1)} %bitcast.28), channel_id=1, source_target_pairs={{0,16},{16,0},{1,17},{17,1},{2,18},{18,2},{3,19},{19,3},{4,20},{20... | collective-permute-start | bytes 1769480 | tf_op jit(solution)/shard_map/ppermute | solution.py:29
  38.5 11.8 %collective-permute-start.2 = (bf16[384,768]{1,0:T(8,128)(2,1)}, bf16[384,768]{1,0:T(8,128)(2,1)S(1)}, u32[]{:S(2)}, u32[]{:S(2)}) collective-permute-start(bf16[384,768]{1,0:T(8,128)(2,1)} %bitcast.29), channel_id=1, source_target_pairs={{0,32},{32,64},{64,96},{96,0},{1,33},{33,65},{65,97},{97,1},{2,34}... | collective-permute-start | bytes 1769480 | tf_op jit(solution)/shard_map/ppermute | solution.py:29
  50.3 3.1 %collective-permute-done.5 = bf16[384,768]{1,0:T(8,128)(2,1)S(1)} collective-permute-done((bf16[384,768]{1,0:T(8,128)(2,1)}, bf16[384,768]{1,0:T(8,128)(2,1)S(1)}, u32[]{:S(2)}, u32[]{:S(2)}) %collective-permute-start.5) | collective-permute-done | bytes 589856 | tf_op jit(solution)/shard_map/ppermute | solution.py:29
  53.4 14.3 %collective-permute-start.6 = (bf16[384,768]{1,0:T(8,128)(2,1)S(1)}, bf16[384,768]{1,0:T(8,128)(2,1)S(1)}, u32[]{:S(2)}, u32[]{:S(2)}) collective-permute-start(bf16[384,768]{1,0:T(8,128)(2,1)S(1)} %collective-permute-done.5), channel_id=1, source_target_pairs={{0,32},{32,64},{64,96},{96,0},{1,33},{33,65},{65,97},{97,1},{2,34}... | collective-permute-start | bytes 1769480 | tf_op jit(solution)/shard_map/ppermute | solution.py:29
  67.7 2.7 %collective-permute-start.4 = (bf16[384,768]{1,0:T(8,128)(2,1)}, bf16[384,768]{1,0:T(8,128)(2,1)S(1)}, u32[]{:S(2)}, u32[]{:S(2)}) collective-permute-start(bf16[384,768]{1,0:T(8,128)(2,1)} %bitcast.30), channel_id=1, source_target_pairs={{0,96},{32,0},{64,32},{96,64},{1,97},{33,1},{65,33},{97,65},{2,98}... | collective-permute-start | bytes 1769480 | tf_op jit(solution)/shard_map/ppermute | solution.py:29
  70.6 0.2 copy.15
  70.9 0.7 collective-permute-start.8
  71.6 8.6 %collective-permute-done.6 = bf16[384,768]{1,0:T(8,128)(2,1)S(1)} collective-permute-done((bf16[384,768]{1,0:T(8,128)(2,1)S(1)}, bf16[384,768]{1,0:T(8,128)(2,1)S(1)}, u32[]{:S(2)}, u32[]{:S(2)}) %collective-permute-start.6) | collective-permute-done | bytes 589856 | tf_op jit(solution)/shard_map/ppermute | solution.py:29
  80.2 0.9 constant_dynamic-update-slice_fusion.6
  81.1 11.7 %collective-permute-done.3 = bf16[384,768]{1,0:T(8,128)(2,1)S(1)} collective-permute-done((bf16[384,768]{1,0:T(8,128)(2,1)S(1)}, bf16[384,768]{1,0:T(8,128)(2,1)S(1)}, u32[]{:S(2)}, u32[]{:S(2)}) %collective-permute-start.3) | collective-permute-done | bytes 589856 | tf_op jit(solution)/shard_map/ppermute | solution.py:29
  92.8 0.9 constant_dynamic-update-slice_fusion.5
  93.7 0.9 constant_dynamic-update-slice_fusion.4
  94.6 0.9 constant_dynamic-update-slice_fusion.3
  95.6 0.9 constant_dynamic-update-slice_fusion.2
  96.5 9.0 %collective-permute-done.7 = bf16[384,768]{1,0:T(8,128)(2,1)S(1)} collective-permute-done((bf16[384,768]{1,0:T(8,128)(2,1)S(1)}, bf16[384,768]{1,0:T(8,128)(2,1)S(1)}, u32[]{:S(2)}, u32[]{:S(2)}) %collective-permute-start.7) | collective-permute-done | bytes 589856 | tf_op jit(solution)/shard_map/ppermute | solution.py:29
  105.5 0.9 constant_dynamic-update-slice_fusion.1
  106.4 0.9 constant_dynamic-update-slice_fusion
  107.3 7.1 %fusion.15 = (bf16[384,384]{1,0:T(8,128)(2,1)}, f32[384,384]{1,0:T(8,128)S(1)}) fusion(pred[384,384]{1,0:T(32,128)(4,1)S(1)} %copy.15, bf16[384,6144]{1,0:T(8,128)(2,1)} %constant_dynamic-update-slice_fusion, bf16[768,6144]{0,1:T(8,128)(2,1)} %all-gather.4.cloned.1.call-done), kind=kOutput, calls=%fused_computation.38 | convolution fusion | flops 1812234240 | bytes 10469376 | tf_op jit(solution)/shard_map/dot_general | solution.py:77
  114.9 0.2 copy.17
  115.1 7.1 %fusion.14 = (bf16[384,384]{1,0:T(8,128)(2,1)}, f32[384,384]{1,0:T(8,128)S(1)}) fusion(pred[384,384]{1,0:T(32,128)(4,1)S(1)} %copy.17, bf16[384,6144]{1,0:T(8,128)(2,1)} %constant_dynamic-update-slice_fusion, bf16[768,6144]{0,1:T(8,128)(2,1)} %all-gather.4.cloned.1.call-done), kind=kOutput, calls=%fused_computation.37 | convolution fusion | flops 1812234240 | bytes 10469376 | tf_op jit(solution)/shard_map/dot_general | solution.py:77
  122.5 0.2 copy.16
  123.2 35.1 %all-gather.6.cloned.1.call-done = bf16[384,6144]{1,0:T(8,128)(2,1)} async-done(((bf16[384,384]{1,0:T(8,128)(2,1)}), bf16[384,6144]{1,0:T(8,128)(2,1)}) %all-gather.6.cloned.1.call-update) | async-done | bytes 4718608 | tf_op jit(solution)/shard_map/all_gather | solution.py:113
  158.3 6.4 %select_convert_fusion.2 = bf16[384,384]{1,0:T(8,128)(2,1)S(1)} fusion(pred[384,384]{1,0:T(32,128)(4,1)S(1)} %copy.16, f32[384,384]{1,0:T(8,128)S(1)} %get-tuple-element.20, bf16[384,6144]{1,0:T(8,128)(2,1)} %all-gather.6.cloned.1.call-done, bf16[384,6144]{1,0:T(8,128)(2,1)} %constant_dynamic-update-slice_fusion), kind=kOutput, calls=%fused_computation.13 | convolution fusion | flops 1812676608 | bytes 10469376 | tf_op jit(solution)/shard_map/dot_general | solution.py:77
  164.7 34.3 %all-gather.8.cloned.1.call-done = bf16[384,6144]{1,0:T(8,128)(2,1)} async-done(((bf16[384,384]{1,0:T(8,128)(2,1)}), bf16[384,6144]{1,0:T(8,128)(2,1)}) %all-gather.8.cloned.1.call-update) | async-done | bytes 4718608 | tf_op jit(solution)/shard_map/all_gather | solution.py:113
  199.0 6.4 %select_convert_fusion.1 = bf16[384,384]{1,0:T(8,128)(2,1)S(1)} fusion(pred[384,384]{1,0:T(32,128)(4,1)S(1)} %copy.18, f32[384,384]{1,0:T(8,128)S(1)} %get-tuple-element.18, bf16[384,6144]{1,0:T(8,128)(2,1)} %all-gather.8.cloned.1.call-done, bf16[384,6144]{1,0:T(8,128)(2,1)} %constant_dynamic-update-slice_fusion), kind=kOutput, calls=%fused_computation.12 | convolution fusion | flops 1812676608 | bytes 10469376 | tf_op jit(solution)/shard_map/dot_general | solution.py:77
  205.4 0.9 pad_maximum_fusion
  (39 shorter events, 2.0 us)
Async XLA Ops:
  6.5 3.3 %copy-start = (s32[96,3]{0,1:T(4,128)S(1)}, s32[96,3]{0,1:T(4,128)}, u32[]{:S(2)}) copy-start(s32[96,3]{0,1:T(4,128)} %param.3) | copy-start | bytes 3460
  6.5 100.8 %all-gather.4.cloned.1.call-start = ((), (), s32[]{:S(2)}) async-start(), calls=%async_computation | async-start | bytes 10027008 | tf_op jit(solution)/shard_map/all_gather | solution.py:103
  7.7 3.9 %collective-permute-start = (bf16[384,384]{1,0:T(8,128)(2,1)S(1)}, bf16[384,384]{1,0:T(8,128)(2,1)S(1)}, u32[]{:S(2)}, u32[]{:S(2)}) collective-permute-start(bf16[384,384]{1,0:T(8,128)(2,1)S(1)} %get-tuple-element.7), channel_id=1, source_target_pairs={{0,0},{1,1},{2,16},{3,17},{4,32},{5,33},{6,48},{7,49},{8,64},{9,65... | collective-permute-start | bytes 884744 | tf_op jit(solution)/shard_map/ppermute | solution.py:69
  8.4 3.3 %collective-permute-start.1 = (bf16[384,384]{1,0:T(8,128)(2,1)S(1)}, bf16[384,384]{1,0:T(8,128)(2,1)S(1)}, u32[]{:S(2)}, u32[]{:S(2)}) collective-permute-start(bf16[384,384]{1,0:T(8,128)(2,1)S(1)} %get-tuple-element.8), channel_id=1, source_target_pairs={{0,1},{1,0},{2,17},{3,16},{4,33},{5,32},{6,49},{7,48},{8,65},{9,64... | collective-permute-start | bytes 884744 | tf_op jit(solution)/shard_map/ppermute | solution.py:69
  15.9 142.4 %all-gather.6.cloned.1.call-start = ((), (), s32[]{:S(2)}) async-start(), calls=%async_computation.1 | async-start | bytes 5013504 | tf_op jit(solution)/shard_map/all_gather | solution.py:113
  15.9 37.4 %collective-permute-start.5 = (bf16[384,768]{1,0:T(8,128)(2,1)}, bf16[384,768]{1,0:T(8,128)(2,1)S(1)}, u32[]{:S(2)}, u32[]{:S(2)}) collective-permute-start(bf16[384,768]{1,0:T(8,128)(2,1)} %bitcast.28), channel_id=1, source_target_pairs={{0,16},{16,0},{1,17},{17,1},{2,18},{18,2},{3,19},{19,3},{4,20},{20... | collective-permute-start | bytes 1769480 | tf_op jit(solution)/shard_map/ppermute | solution.py:29
  38.5 29.1 %collective-permute-start.2 = (bf16[384,768]{1,0:T(8,128)(2,1)}, bf16[384,768]{1,0:T(8,128)(2,1)S(1)}, u32[]{:S(2)}, u32[]{:S(2)}) collective-permute-start(bf16[384,768]{1,0:T(8,128)(2,1)} %bitcast.29), channel_id=1, source_target_pairs={{0,32},{32,64},{64,96},{96,0},{1,33},{33,65},{65,97},{97,1},{2,34}... | collective-permute-start | bytes 1769480 | tf_op jit(solution)/shard_map/ppermute | solution.py:29
  53.4 26.8 %collective-permute-start.6 = (bf16[384,768]{1,0:T(8,128)(2,1)S(1)}, bf16[384,768]{1,0:T(8,128)(2,1)S(1)}, u32[]{:S(2)}, u32[]{:S(2)}) collective-permute-start(bf16[384,768]{1,0:T(8,128)(2,1)S(1)} %collective-permute-done.5), channel_id=1, source_target_pairs={{0,32},{32,64},{64,96},{96,0},{1,33},{33,65},{65,97},{97,1},{2,34}... | collective-permute-start | bytes 1769480 | tf_op jit(solution)/shard_map/ppermute | solution.py:29
  67.7 25.2 %collective-permute-start.3 = (bf16[384,768]{1,0:T(8,128)(2,1)S(1)}, bf16[384,768]{1,0:T(8,128)(2,1)S(1)}, u32[]{:S(2)}, u32[]{:S(2)}) collective-permute-start(bf16[384,768]{1,0:T(8,128)(2,1)S(1)} %collective-permute-done.2), channel_id=1, source_target_pairs={{0,32},{32,64},{64,96},{96,0},{1,33},{33,65},{65,97},{97,1},{2,34}... | collective-permute-start | bytes 1769480 | tf_op jit(solution)/shard_map/ppermute | solution.py:29
  67.7 26.0 %collective-permute-start.4 = (bf16[384,768]{1,0:T(8,128)(2,1)}, bf16[384,768]{1,0:T(8,128)(2,1)S(1)}, u32[]{:S(2)}, u32[]{:S(2)}) collective-permute-start(bf16[384,768]{1,0:T(8,128)(2,1)} %bitcast.30), channel_id=1, source_target_pairs={{0,96},{32,0},{64,32},{96,64},{1,97},{33,1},{65,33},{97,65},{2,98}... | collective-permute-start | bytes 1769480 | tf_op jit(solution)/shard_map/ppermute | solution.py:29
  70.9 35.5 %collective-permute-start.8 = (bf16[384,768]{1,0:T(8,128)(2,1)S(1)}, bf16[384,768]{1,0:T(8,128)(2,1)S(1)}, u32[]{:S(2)}, u32[]{:S(2)}) collective-permute-start(bf16[384,768]{1,0:T(8,128)(2,1)S(1)} %collective-permute-done.5), channel_id=1, source_target_pairs={{0,96},{32,0},{64,32},{96,64},{1,97},{33,1},{65,33},{97,65},{2,98}... | collective-permute-start | bytes 1769480 | tf_op jit(solution)/shard_map/ppermute | solution.py:29
  80.2 25.3 %collective-permute-start.7 = (bf16[384,768]{1,0:T(8,128)(2,1)S(1)}, bf16[384,768]{1,0:T(8,128)(2,1)S(1)}, u32[]{:S(2)}, u32[]{:S(2)}) collective-permute-start(bf16[384,768]{1,0:T(8,128)(2,1)S(1)} %collective-permute-done.6), channel_id=1, source_target_pairs={{0,32},{32,64},{64,96},{96,0},{1,33},{33,65},{65,97},{97,1},{2,34}... | collective-permute-start | bytes 1769480 | tf_op jit(solution)/shard_map/ppermute | solution.py:29
  114.4 84.5 %all-gather.8.cloned.1.call-start = ((), (), s32[]{:S(2)}) async-start(), calls=%async_computation.2 | async-start | bytes 5013504 | tf_op jit(solution)/shard_map/all_gather | solution.py:113
Sparse Core Ops, SparseCore 0:
  16.0 90.8 all-gather.3
  114.6 43.6 all-gather.5
  160.0 38.9 all-gather.7

commit v8 on v6

--- a/solution.py
+++ b/solution.py
@@ -73,6 +73,20 @@
     return jnp.concatenate([first, second], 1).T
 
 
+def plane_panel(tile):
+    partner = lax.ppermute(tile, "zl", [(0, 1), (1, 0)])
+    zl_id = lax.axis_index("zl")
+    pair = jnp.where(zl_id == 0, jnp.concatenate([tile, partner], 1), jnp.concatenate([partner, tile], 1))
+    return lax.all_gather(pair, ("x", "core"), axis=1, tiled=True)
+
+
+def to_plane_order(panel_t, tile_width):
+    rows, width = panel_t.shape
+    planes = lax.axis_size("zl")
+    shaped = panel_t.reshape(rows, planes, width // (planes * tile_width), tile_width)
+    return shaped.transpose(0, 2, 1, 3).reshape(rows, width)
+
+
 def dot_t(left, right_t):
     return lax.dot_general(left, right_t, (((1,), (1,)), ((), ())), preferred_element_type=jnp.float32)
 
@@ -100,11 +114,11 @@
     value_scale = 2.0 / math.sqrt(order_total)
     density_full = diagonal + value_scale * symmetric.astype(jnp.float32)
     density = jnp.where(near_own, density_full, 0.0).astype(jnp.bfloat16)
-    row_panel = lax.all_gather(density, COL, axis=1, tiled=True)
-    col_panel_t = column_panel_t(density.T)
+    row_panel = plane_panel(density)
+    col_panel_t = to_plane_order(column_panel_t(density.T), half_width)
     square = jnp.where(far_own, dot_t(row_panel, col_panel_t), 0.0)
     square_low = square.astype(jnp.bfloat16)
-    low_panel = lax.all_gather(square_low, COL, axis=1, tiled=True)
+    low_panel = plane_panel(square_low)
     cubic = dot_t(low_panel, col_panel_t)
     return jnp.where(near_own, 3.0 * square - 2.0 * cubic, 0.0).astype(jnp.bfloat16)
 

time: 196 us -> 221 us (1.13)
  waiting for transfers between devices: 93.6 us -> 115 us
  local copies, waits for them, and re-layouts: 13 us -> 26.3 us
  starting transfers between devices: 54.6 us -> 45.2 us
    ppermute x7, starting transfers between devices: 52.4 us -> 9.95 us  [chunked_shift(): lax.ppermute(value[i * step:(i + 1) * step], axis, pairs)]
    ppermute x0 -> x2, starting transfers between devices: none -> 33 us  [plane_panel(): partner = lax.ppermute(tile, 'zl', [(0, 1), (1, 0)])]
    ppermute x0 -> x2, waiting for transfers between devices: none -> 24.8 us  [plane_panel(): partner = lax.ppermute(tile, 'zl', [(0, 1), (1, 0)])]
    ppermute x0 -> x7, local copies, waits for them, and re-layouts: none -> 6.44 us  [chunked_shift(): lax.ppermute(value[i * step:(i + 1) * step], axis, pairs)]
    transpose x0 -> x2, local copies, waits for them, and re-layouts: none -> 5.51 us  [the longest x1 5.21 us: to_plane_order(): return shaped.transpose(0, 2, 1, 3).reshape(rows, width)]
    all_gather x2, waiting for transfers between devices: 62 us -> 56.9 us  [plane_panel(): return lax.all_gather(pair, ('x', 'core'), axis=1, tiled=True)]
    select_n x0 -> x2, other arithmetic: none -> 2.97 us  [plane_panel(): jnp.where(zl_id == 0, jnp.concatenate([tile, partner], 1), jnp.concatenat...]
    dynamic_update_slice x7 -> x8, local copies, waits for them, and re-layouts: 7.31 us -> 7.14 us  [ring_gather(): panel = lax.dynamic_update_slice_in_dim(panel, part, position * width, 1)]
  transfers between devices with their start and end apart: 11 -> 13, of which waited for: 6 -> 8; matrix products, arithmetic and copies ran while one was open for 5% -> 11% of each run, Pallas kernels for 0% -> 0%
where the time goes in v8:
time: 221 us
  waiting for transfers between devices  115 us (52%)
  starting transfers between devices  45.2 us (20%)
  local copies, waits for them, and re-layouts  26.3 us (12%)
  matrix products  17.7 us (8%)
  between operations  13.6 us (6%)
  other arithmetic  3.58 us (2%)
    all_gather x2, waiting for transfers between devices, plane_panel(): return lax.all_gather(pair, ('x', 'core'), axis=1, tiled=True)  56.9 us
    ppermute x2, starting transfers between devices, plane_panel(): partner = lax.ppermute(tile, 'zl', [(0, 1), (1, 0)])  33 us
    ppermute x7, waiting for transfers between devices, chunked_shift(): lax.ppermute(value[i * step:(i + 1) * step], axis, pairs)  32.8 us
    ppermute x2, waiting for transfers between devices, plane_panel(): partner = lax.ppermute(tile, 'zl', [(0, 1), (1, 0)])  24.8 us
    dot_general x2, matrix products, dot_t(): lax.dot_general(left, right_t, (((1,), (1,)), ((), ())), preferred_elemen...  17.7 us
    ppermute x7, starting transfers between devices, chunked_shift(): lax.ppermute(value[i * step:(i + 1) * step], axis, pairs)  9.95 us
    dynamic_update_slice x8, local copies, waits for them, and re-layouts, ring_gather(): panel = lax.dynamic_update_slice_in_dim(panel, part, position * width, 1)  7.14 us
    ppermute x7, local copies, waits for them, and re-layouts, chunked_shift(): lax.ppermute(value[i * step:(i + 1) * step], axis, pairs)  6.44 us
  transfers between devices with their start and end apart: 13, of which 8 were waited for; matrix products, arithmetic and copies ran while one was open for 11% of the time, Pallas kernels for 0%

profile of v8, /device:TPU:1, one launch (start us, length us, event | category | flops | bytes accessed | tf_op | source)
XLA Modules:
  0.0 220.8 jit_solution(7795175546034125253)
XLA Ops:
  6.5 1.1 constant_dynamic-slice_fusion.1
  8.4 1.5 collective-permute-start.1
  10.1 1.3 copy.27
  12.1 31.0 %collective-permute-start.2 = (bf16[768,384]{0,1:T(8,128)(2,1)S(1)}, bf16[768,384]{0,1:T(8,128)(2,1)S(1)}, u32[]{:S(2)}, u32[]{:S(2)}) collective-permute-start(bf16[768,384]{0,1:T(8,128)(2,1)S(1)} %fusion.2), channel_id=1, source_target_pairs={{0,8},{8,0},{1,9},{9,1},{2,10},{10,2},{3,11},{11,3},{4,12},{12,4},... | collective-permute-start | bytes 1769480 | tf_op jit(solution)/shard_map/ppermute | solution.py:77
  43.1 13.4 %collective-permute-done.2 = bf16[768,384]{0,1:T(8,128)(2,1)S(1)} collective-permute-done((bf16[768,384]{0,1:T(8,128)(2,1)S(1)}, bf16[768,384]{0,1:T(8,128)(2,1)S(1)}, u32[]{:S(2)}, u32[]{:S(2)}) %collective-permute-start.2) | collective-permute-done | bytes 589856 | tf_op jit(solution)/shard_map/ppermute | solution.py:77
  56.5 1.5 maximum_select_fusion
  58.2 4.5 %collective-permute-start.3 = (bf16[384,768]{1,0:T(8,128)(2,1)S(1)}, bf16[384,768]{1,0:T(8,128)(2,1)S(1)}, u32[]{:S(2)}, u32[]{:S(2)}) collective-permute-start(bf16[384,768]{1,0:T(8,128)(2,1)S(1)} %bitcast.28), channel_id=1, source_target_pairs={{0,32},{32,64},{64,96},{96,0},{1,33},{33,65},{65,97},{97,1},{2,34}... | collective-permute-start | bytes 1769480 | tf_op jit(solution)/shard_map/ppermute | solution.py:29
  62.6 1.9 collective-permute-start.5
  64.5 9.7 %collective-permute-done.6 = bf16[384,768]{1,0:T(8,128)(2,1)} collective-permute-done((bf16[384,768]{1,0:T(8,128)(2,1)S(1)}, bf16[384,768]{1,0:T(8,128)(2,1)}, u32[]{:S(2)}, u32[]{:S(2)}) %collective-permute-start.6) | collective-permute-done | bytes 589856 | tf_op jit(solution)/shard_map/ppermute | solution.py:29
  75.1 1.9 collective-permute-done.3
  77.2 2.5 %collective-permute-start.9 = (bf16[384,768]{1,0:T(8,128)(2,1)}, bf16[384,768]{1,0:T(8,128)(2,1)}, u32[]{:S(2)}, u32[]{:S(2)}) collective-permute-start(bf16[384,768]{1,0:T(8,128)(2,1)} %collective-permute-done.6), channel_id=1, source_target_pairs={{0,96},{32,0},{64,32},{96,64},{1,97},{33,1},{65,33},{97,65},{2,98}... | collective-permute-start | bytes 1769480 | tf_op jit(solution)/shard_map/ppermute | solution.py:29
  80.7 2.5 %broadcast_in_dim.37 = bf16[384,6144]{0,1:T(8,128)(2,1)} broadcast(bf16[]{:T(256)} %constant.98.clone.1), dimensions={} | broadcast | bytes 4718594 | tf_op jit(solution)/shard_map/broadcast_in_dim | solution.py:52
  83.3 0.9 constant_dynamic-update-slice_fusion.7
  84.5 1.4 copy.32
  86.2 3.4 %collective-permute-done.7 = bf16[384,768]{1,0:T(8,128)(2,1)S(1)} collective-permute-done((bf16[384,768]{1,0:T(8,128)(2,1)}, bf16[384,768]{1,0:T(8,128)(2,1)S(1)}, u32[]{:S(2)}, u32[]{:S(2)}) %collective-permute-start.7) | collective-permute-done | bytes 589856 | tf_op jit(solution)/shard_map/ppermute | solution.py:29
  89.6 0.9 constant_dynamic-update-slice_fusion.6
  90.8 11.4 %collective-permute-done.4 = bf16[384,768]{1,0:T(8,128)(2,1)} collective-permute-done((bf16[384,768]{1,0:T(8,128)(2,1)S(1)}, bf16[384,768]{1,0:T(8,128)(2,1)}, u32[]{:S(2)}, u32[]{:S(2)}) %collective-permute-start.4) | collective-permute-done | bytes 589856 | tf_op jit(solution)/shard_map/ppermute | solution.py:29
  102.2 1.4 copy.30
  103.6 1.4 copy.35
  105.0 0.9 constant_dynamic-update-slice_fusion.5
  108.5 6.3 %collective-permute-done.8 = bf16[384,768]{1,0:T(8,128)(2,1)} collective-permute-done((bf16[384,768]{1,0:T(8,128)(2,1)S(1)}, bf16[384,768]{1,0:T(8,128)(2,1)}, u32[]{:S(2)}, u32[]{:S(2)}) %collective-permute-start.8) | collective-permute-done | bytes 589856 | tf_op jit(solution)/shard_map/ppermute | solution.py:29
  114.9 1.4 copy.34
  116.3 0.9 constant_dynamic-update-slice_fusion.1
  117.1 0.9 constant_dynamic-update-slice_fusion
  118.0 5.2 %copy.36 = bf16[384,8,2,384]{0,3,2,1:T(8,128)(2,1)} copy(bf16[384,8,2,384]{0,3,1,2:T(8,128)(2,1)} %bitcast.5) | data formatting | bytes 9437184 | tf_op jit(solution)/shard_map/transpose | solution.py:87
  123.3 8.8 %fusion.5 = (bf16[768,384]{0,1:T(8,128)(2,1)S(1)}, f32[768,384]{0,1:T(8,128)S(1)}) fusion(pred[768,384]{0,1:T(32,128)(4,1)S(1)} %bitcast.31, bf16[768,6144]{0,1:T(8,128)(2,1)} %all-gather.3.cloned.1.call-done, bf16[384,6144]{0,1:T(8,128)(2,1)} %bitcast.25), kind=kOutput, calls=%fused_computation.32 | convolution fusion | flops 3624468480 | bytes 16220160 | tf_op jit(solution)/shard_map/dot_general | solution.py:91
  132.1 2.0 collective-permute-start.10
  134.1 11.5 %collective-permute-done.10 = bf16[768,384]{0,1:T(8,128)(2,1)S(1)} collective-permute-done((bf16[768,384]{0,1:T(8,128)(2,1)S(1)}, bf16[768,384]{0,1:T(8,128)(2,1)S(1)}, u32[]{:S(2)}, u32[]{:S(2)}) %collective-permute-start.10) | collective-permute-done | bytes 589856 | tf_op jit(solution)/shard_map/ppermute | solution.py:77
  145.6 1.5 maximum_select_fusion.1
  147.1 56.9 %all-gather.5.cloned.1.call-done = bf16[768,6144]{0,1:T(8,128)(2,1)} async-done(((bf16[768,768]{0,1:T(8,128)(2,1)}), bf16[768,6144]{0,1:T(8,128)(2,1)}) %all-gather.5.cloned.1.call-update) | async-done | bytes 9437200 | tf_op jit(solution)/shard_map/all_gather | solution.py:80
  204.0 8.9 %fusion.1 = bf16[768,384]{0,1:T(8,128)(2,1)S(1)} fusion(bf16[768,6144]{0,1:T(8,128)(2,1)} %all-gather.5.cloned.1.call-done, bf16[384,6144]{0,1:T(8,128)(2,1)} %bitcast.26, f32[768,384]{0,1:T(8,128)S(1)} %get-tuple-element.12, pred[768,6]{0,1:T(8,128)(4,1)S(1)} %reshape.20), kind=kOutput, calls=%fused_computation.5 | convolution fusion | flops 3625353216 | bytes 15929856 | tf_op jit(solution)/shard_map/dot_general | solution.py:91
  212.9 1.1 copy.38
  (38 shorter events, 7.5 us)
Async XLA Ops:
  6.5 3.3 %copy-start = (s32[96,3]{0,1:T(4,128)S(1)}, s32[96,3]{0,1:T(4,128)}, u32[]{:S(2)}) copy-start(s32[96,3]{0,1:T(4,128)} %param.3) | copy-start | bytes 3460
  6.5 116.7 %all-gather.3.cloned.1.call-start = ((), (), s32[]{:S(2)}) async-start(), calls=%async_computation | async-start | bytes 10616832 | tf_op jit(solution)/shard_map/all_gather | solution.py:80
  7.7 3.9 %collective-permute-start = (bf16[384,384]{1,0:T(8,128)(2,1)S(1)}, bf16[384,384]{1,0:T(8,128)(2,1)S(1)}, u32[]{:S(2)}, u32[]{:S(2)}) collective-permute-start(bf16[384,384]{1,0:T(8,128)(2,1)S(1)} %get-tuple-element.7), channel_id=1, source_target_pairs={{0,0},{1,1},{2,16},{3,17},{4,32},{5,33},{6,48},{7,49},{8,64},{9,65... | collective-permute-start | bytes 884744 | tf_op jit(solution)/shard_map/ppermute | solution.py:69
  8.4 3.2 %collective-permute-start.1 = (bf16[384,384]{1,0:T(8,128)(2,1)S(1)}, bf16[384,384]{1,0:T(8,128)(2,1)S(1)}, u32[]{:S(2)}, u32[]{:S(2)}) collective-permute-start(bf16[384,384]{1,0:T(8,128)(2,1)S(1)} %get-tuple-element.8), channel_id=1, source_target_pairs={{0,1},{1,0},{2,17},{3,16},{4,33},{5,32},{6,49},{7,48},{8,65},{9,64... | collective-permute-start | bytes 884744 | tf_op jit(solution)/shard_map/ppermute | solution.py:69
  12.1 44.4 %collective-permute-start.2 = (bf16[768,384]{0,1:T(8,128)(2,1)S(1)}, bf16[768,384]{0,1:T(8,128)(2,1)S(1)}, u32[]{:S(2)}, u32[]{:S(2)}) collective-permute-start(bf16[768,384]{0,1:T(8,128)(2,1)S(1)} %fusion.2), channel_id=1, source_target_pairs={{0,8},{8,0},{1,9},{9,1},{2,10},{10,2},{3,11},{11,3},{4,12},{12,4},... | collective-permute-start | bytes 1769480 | tf_op jit(solution)/shard_map/ppermute | solution.py:77
  58.0 146.0 %all-gather.5.cloned.1.call-start = ((), (), s32[]{:S(2)}) async-start(), calls=%async_computation.1 | async-start | bytes 10616832 | tf_op jit(solution)/shard_map/all_gather | solution.py:80
  58.1 16.2 %collective-permute-start.6 = (bf16[384,768]{1,0:T(8,128)(2,1)S(1)}, bf16[384,768]{1,0:T(8,128)(2,1)}, u32[]{:S(2)}, u32[]{:S(2)}) collective-permute-start(bf16[384,768]{1,0:T(8,128)(2,1)S(1)} %bitcast.27), channel_id=1, source_target_pairs={{0,16},{16,0},{1,17},{17,1},{2,18},{18,2},{3,19},{19,3},{4,20},{20... | collective-permute-start | bytes 1769480 | tf_op jit(solution)/shard_map/ppermute | solution.py:29
  58.2 18.8 %collective-permute-start.3 = (bf16[384,768]{1,0:T(8,128)(2,1)S(1)}, bf16[384,768]{1,0:T(8,128)(2,1)S(1)}, u32[]{:S(2)}, u32[]{:S(2)}) collective-permute-start(bf16[384,768]{1,0:T(8,128)(2,1)S(1)} %bitcast.28), channel_id=1, source_target_pairs={{0,32},{32,64},{64,96},{96,0},{1,33},{33,65},{65,97},{97,1},{2,34}... | collective-permute-start | bytes 1769480 | tf_op jit(solution)/shard_map/ppermute | solution.py:29
  62.6 23.3 %collective-permute-start.5 = (bf16[384,768]{1,0:T(8,128)(2,1)S(1)}, bf16[384,768]{1,0:T(8,128)(2,1)S(1)}, u32[]{:S(2)}, u32[]{:S(2)}) collective-permute-start(bf16[384,768]{1,0:T(8,128)(2,1)S(1)} %bitcast.29), channel_id=1, source_target_pairs={{0,96},{32,0},{64,32},{96,64},{1,97},{33,1},{65,33},{97,65},{2,98}... | collective-permute-start | bytes 1769480 | tf_op jit(solution)/shard_map/ppermute | solution.py:29
  74.2 15.4 %collective-permute-start.7 = (bf16[384,768]{1,0:T(8,128)(2,1)}, bf16[384,768]{1,0:T(8,128)(2,1)S(1)}, u32[]{:S(2)}, u32[]{:S(2)}) collective-permute-start(bf16[384,768]{1,0:T(8,128)(2,1)} %collective-permute-done.6), channel_id=1, source_target_pairs={{0,32},{32,64},{64,96},{96,0},{1,33},{33,65},{65,97},{97,1},{2,34}... | collective-permute-start | bytes 1769480 | tf_op jit(solution)/shard_map/ppermute | solution.py:29
  77.0 25.3 %collective-permute-start.4 = (bf16[384,768]{1,0:T(8,128)(2,1)S(1)}, bf16[384,768]{1,0:T(8,128)(2,1)}, u32[]{:S(2)}, u32[]{:S(2)}) collective-permute-start(bf16[384,768]{1,0:T(8,128)(2,1)S(1)} %collective-permute-done.3), channel_id=1, source_target_pairs={{0,32},{32,64},{64,96},{96,0},{1,33},{33,65},{65,97},{97,1},{2,34}... | collective-permute-start | bytes 1769480 | tf_op jit(solution)/shard_map/ppermute | solution.py:29
  77.2 26.5 %collective-permute-start.9 = (bf16[384,768]{1,0:T(8,128)(2,1)}, bf16[384,768]{1,0:T(8,128)(2,1)}, u32[]{:S(2)}, u32[]{:S(2)}) collective-permute-start(bf16[384,768]{1,0:T(8,128)(2,1)} %collective-permute-done.6), channel_id=1, source_target_pairs={{0,96},{32,0},{64,32},{96,64},{1,97},{33,1},{65,33},{97,65},{2,98}... | collective-permute-start | bytes 1769480 | tf_op jit(solution)/shard_map/ppermute | solution.py:29
  89.6 25.3 %collective-permute-start.8 = (bf16[384,768]{1,0:T(8,128)(2,1)S(1)}, bf16[384,768]{1,0:T(8,128)(2,1)}, u32[]{:S(2)}, u32[]{:S(2)}) collective-permute-start(bf16[384,768]{1,0:T(8,128)(2,1)S(1)} %collective-permute-done.7), channel_id=1, source_target_pairs={{0,32},{32,64},{64,96},{96,0},{1,33},{33,65},{65,97},{97,1},{2,34}... | collective-permute-start | bytes 1769480 | tf_op jit(solution)/shard_map/ppermute | solution.py:29
  118.0 5.2 %copy-start.1 = (pred[768,6]{0,1:T(8,128)(4,1)S(1)}, pred[768,6]{0,1:T(8,128)(4,1)}, u32[]{:S(2)}) copy-start(pred[768,6]{0,1:T(8,128)(4,1)} %reshape.22) | copy-start | bytes 13828
  132.1 13.5 %collective-permute-start.10 = (bf16[768,384]{0,1:T(8,128)(2,1)S(1)}, bf16[768,384]{0,1:T(8,128)(2,1)S(1)}, u32[]{:S(2)}, u32[]{:S(2)}) collective-permute-start(bf16[768,384]{0,1:T(8,128)(2,1)S(1)} %get-tuple-element.11), channel_id=1, source_target_pairs={{0,8},{8,0},{1,9},{9,1},{2,10},{10,2},{3,11},{11,3},{4,12},{12,4},... | collective-permute-start | bytes 1769480 | tf_op jit(solution)/shard_map/ppermute | solution.py:77
Sparse Core Ops, SparseCore 0:
  58.1 56.6 all-gather.2
  147.2 56.7 all-gather.4

commit v9 on v6

--- a/solution.py
+++ b/solution.py
@@ -100,12 +100,29 @@
     value_scale = 2.0 / math.sqrt(order_total)
     density_full = diagonal + value_scale * symmetric.astype(jnp.float32)
     density = jnp.where(near_own, density_full, 0.0).astype(jnp.bfloat16)
-    row_panel = lax.all_gather(density, COL, axis=1, tiled=True)
+    core_id = lax.axis_index("core")
+    group = ("zl", "x")
     col_panel_t = column_panel_t(density.T)
-    square = jnp.where(far_own, dot_t(row_panel, col_panel_t), 0.0)
+    by_core = col_panel_t.reshape(half_width, cols // 2, 2, half_width)
+    mine = lax.dynamic_index_in_dim(by_core, core_id, 2, keepdims=False).reshape(half_width, -1)
+    for_partner = lax.dynamic_index_in_dim(by_core, 1 - core_id, 2, keepdims=False).reshape(half_width, -1)
+    from_partner = lax.ppermute(for_partner, "core", [(0, 1), (1, 0)])
+    chip_panel_t = jnp.where(
+        core_id == 0,
+        jnp.concatenate([mine, from_partner], 0),
+        jnp.concatenate([from_partner, mine], 0),
+    )
+
+    def chip_product(left_tile):
+        left = lax.all_gather(left_tile, group, axis=1, tiled=True)
+        partial = dot_t(left, chip_panel_t)
+        own = jnp.where(core_id == 0, partial[:, :half_width], partial[:, half_width:])
+        other = jnp.where(core_id == 0, partial[:, half_width:], partial[:, :half_width])
+        return own + lax.ppermute(other, "core", [(0, 1), (1, 0)])
+
+    square = jnp.where(far_own, chip_product(density), 0.0)
     square_low = square.astype(jnp.bfloat16)
-    low_panel = lax.all_gather(square_low, COL, axis=1, tiled=True)
-    cubic = dot_t(low_panel, col_panel_t)
+    cubic = chip_product(square_low)
     return jnp.where(near_own, 3.0 * square - 2.0 * cubic, 0.0).astype(jnp.bfloat16)
 
 

time: 196 us -> 253 us (1.29)
  starting transfers between devices: 54.6 us -> 97.3 us
  waiting for transfers between devices: 93.6 us -> 101 us
  other arithmetic: 1.7 us -> 6.87 us
  local copies, waits for them, and re-layouts: 13 us -> 17 us
    ppermute x7, starting transfers between devices: 52.4 us -> 92.3 us  [chunked_shift(): lax.ppermute(value[i * step:(i + 1) * step], axis, pairs)]
    ppermute x0 -> x3, waiting for transfers between devices: none -> 8.23 us  [the longest x1 4.29 us: per_device(): from_partner = lax.ppermute(for_partner, 'core', [(0, 1), (1, 0)])]
    all_gather x2, waiting for transfers between devices: 62 us -> 56.9 us  [chip_product(): left = lax.all_gather(left_tile, group, axis=1, tiled=True)]
    dynamic_slice x0 -> x1, local copies, waits for them, and re-layouts: none -> 4.38 us  [per_device(): lax.dynamic_index_in_dim(by_core, core_id, 2, keepdims=False)]
    ppermute x7, waiting for transfers between devices: 31.3 us -> 35.2 us  [chunked_shift(): lax.ppermute(value[i * step:(i + 1) * step], axis, pairs)]
    convert_element_type x0 -> x2, other arithmetic: none -> 3.85 us  [the longest x1 2.53 us: per_device(): square_low = square.astype(jnp.bfloat16)]
    ppermute x0 -> x3, starting transfers between devices: none -> 2.83 us  [the longest x1 1.55 us: per_device(): from_partner = lax.ppermute(for_partner, 'core', [(0, 1), (1, 0)])]
  transfers between devices with their start and end apart: 11 -> 14, of which waited for: 6 -> 9; matrix products, arithmetic and copies ran while one was open for 5% -> 5% of each run, Pallas kernels for 0% -> 0%
where the time goes in v9:
time: 253 us
  waiting for transfers between devices  101 us (40%)
  starting transfers between devices  97.3 us (38%)
  matrix products  17.9 us (7%)
  local copies, waits for them, and re-layouts  17 us (7%)
  between operations  13.6 us (5%)
  other arithmetic  6.87 us (3%)
    ppermute x7, starting transfers between devices, chunked_shift(): lax.ppermute(value[i * step:(i + 1) * step], axis, pairs)  92.3 us
    all_gather x2, waiting for transfers between devices, chip_product(): left = lax.all_gather(left_tile, group, axis=1, tiled=True)  56.9 us
    ppermute x7, waiting for transfers between devices, chunked_shift(): lax.ppermute(value[i * step:(i + 1) * step], axis, pairs)  35.2 us
    dot_general x2, matrix products, dot_t(): lax.dot_general(left, right_t, (((1,), (1,)), ((), ())), preferred_elemen...  17.9 us
    dynamic_update_slice x7, local copies, waits for them, and re-layouts, ring_gather(): panel = lax.dynamic_update_slice_in_dim(panel, part, position * width, 1)  6.25 us
  transfers between devices with their start and end apart: 14, of which 9 were waited for; matrix products, arithmetic and copies ran while one was open for 5% of the time, Pallas kernels for 0%

profile of v9, /device:TPU:1, one launch (start us, length us, event | category | flops | bytes accessed | tf_op | source)
XLA Modules:
  0.0 253.2 jit_solution(2531246164265867346)
XLA Ops:
  6.5 1.1 constant_dynamic-slice_fusion.3
  8.8 1.5 collective-permute-start.1
  11.5 2.6 %broadcast_in_dim.37 = bf16[384,6144]{0,1:T(8,128)(2,1)} broadcast(bf16[]{:T(256)} %constant.105.clone.1), dimensions={} | broadcast | bytes 4718594 | tf_op jit(solution)/shard_map/broadcast_in_dim | solution.py:52
  14.2 1.5 constant_dynamic-update-slice_fusion.7
  15.8 22.9 %collective-permute-start.5 = (bf16[384,768]{0,1:T(8,128)(2,1)}, bf16[384,768]{0,1:T(8,128)(2,1)S(1)}, u32[]{:S(2)}, u32[]{:S(2)}) collective-permute-start(bf16[384,768]{0,1:T(8,128)(2,1)} %bitcast.21), channel_id=1, source_target_pairs={{0,16},{16,0},{1,17},{17,1},{2,18},{18,2},{3,19},{19,3},{4,20},{20... | collective-permute-start | bytes 1769480 | tf_op jit(solution)/shard_map/ppermute | solution.py:29
  38.7 11.8 %collective-permute-start.2 = (bf16[384,768]{0,1:T(8,128)(2,1)}, bf16[384,768]{0,1:T(8,128)(2,1)S(1)}, u32[]{:S(2)}, u32[]{:S(2)}) collective-permute-start(bf16[384,768]{0,1:T(8,128)(2,1)} %bitcast.22), channel_id=1, source_target_pairs={{0,32},{32,64},{64,96},{96,0},{1,33},{33,65},{65,97},{97,1},{2,34}... | collective-permute-start | bytes 1769480 | tf_op jit(solution)/shard_map/ppermute | solution.py:29
  50.5 3.1 %collective-permute-done.5 = bf16[384,768]{0,1:T(8,128)(2,1)S(1)} collective-permute-done((bf16[384,768]{0,1:T(8,128)(2,1)}, bf16[384,768]{0,1:T(8,128)(2,1)S(1)}, u32[]{:S(2)}, u32[]{:S(2)}) %collective-permute-start.5) | collective-permute-done | bytes 589856 | tf_op jit(solution)/shard_map/ppermute | solution.py:29
  53.6 54.5 %collective-permute-start.6 = (bf16[384,768]{0,1:T(8,128)(2,1)S(1)}, bf16[384,768]{0,1:T(8,128)(2,1)S(1)}, u32[]{:S(2)}, u32[]{:S(2)}) collective-permute-start(bf16[384,768]{0,1:T(8,128)(2,1)S(1)} %collective-permute-done.5), channel_id=1, source_target_pairs={{0,32},{32,64},{64,96},{96,0},{1,33},{33,65},{65,97},{97,1},{2,34}... | collective-permute-start | bytes 1769480 | tf_op jit(solution)/shard_map/ppermute | solution.py:29
  108.1 1.3 collective-permute-start.3
  109.4 1.4 collective-permute-start.4
  111.2 11.2 %collective-permute-done.6 = bf16[384,768]{0,1:T(8,128)(2,1)S(1)} collective-permute-done((bf16[384,768]{0,1:T(8,128)(2,1)S(1)}, bf16[384,768]{0,1:T(8,128)(2,1)S(1)}, u32[]{:S(2)}, u32[]{:S(2)}) %collective-permute-start.6) | collective-permute-done | bytes 589856 | tf_op jit(solution)/shard_map/ppermute | solution.py:29
  122.4 0.9 constant_dynamic-update-slice_fusion.6
  123.3 11.7 %collective-permute-done.3 = bf16[384,768]{0,1:T(8,128)(2,1)S(1)} collective-permute-done((bf16[384,768]{0,1:T(8,128)(2,1)S(1)}, bf16[384,768]{0,1:T(8,128)(2,1)S(1)}, u32[]{:S(2)}, u32[]{:S(2)}) %collective-permute-start.3) | collective-permute-done | bytes 589856 | tf_op jit(solution)/shard_map/ppermute | solution.py:29
  135.9 0.9 constant_dynamic-update-slice_fusion.4
  136.8 0.9 constant_dynamic-update-slice_fusion.3
  137.7 0.9 constant_dynamic-update-slice_fusion.2
  138.6 9.1 %collective-permute-done.7 = bf16[384,768]{0,1:T(8,128)(2,1)S(1)} collective-permute-done((bf16[384,768]{0,1:T(8,128)(2,1)S(1)}, bf16[384,768]{0,1:T(8,128)(2,1)S(1)}, u32[]{:S(2)}, u32[]{:S(2)}) %collective-permute-start.7) | collective-permute-done | bytes 589856 | tf_op jit(solution)/shard_map/ppermute | solution.py:29
  147.7 0.9 constant_dynamic-update-slice_fusion.1
  148.6 0.9 constant_dynamic-update-slice_fusion
  149.5 4.4 %constant_dynamic-slice_fusion.1 = (bf16[384,8,1,384]{0,3,2,1:T(8,128)(2,1)}, bf16[384,8,1,384]{0,3,2,1:T(8,128)(2,1)S(1)}) fusion(bf16[384,8,2,384]{0,3,2,1:T(8,128)(2,1)} %bitcast.4, s32[]{:T(128)S(6)} %select_n.166, s32[]{:T(128)S(6)} %select_n.167), kind=kLoop, calls=%fused_computation.17 | loop fusion | bytes 9437192 | tf_op jit(solution)/shard_map/jit(dynamic_index_in_dim)/dynamic_slice | solution.py:107
  153.9 1.5 collective-permute-start.9
  155.4 4.3 %collective-permute-done.9 = bf16[384,3072]{0,1:T(8,128)(2,1)} collective-permute-done((bf16[384,3072]{0,1:T(8,128)(2,1)S(1)}, bf16[384,3072]{0,1:T(8,128)(2,1)}, u32[]{:S(2)}, u32[]{:S(2)}) %collective-permute-start.9) | collective-permute-done | bytes 2359328 | tf_op jit(solution)/shard_map/ppermute | solution.py:109
  159.7 9.0 %fusion.1 = f32[768,768]{1,0:T(8,128)S(1)} fusion(bf16[768,3072]{1,0:T(8,128)(2,1)} %all-gather.3.cloned.1.call-done, bf16[384,3072]{0,1:T(8,128)(2,1)} %collective-permute-done.9, bf16[384,3072]{0,1:T(8,128)(2,1)} %bitcast.18, pred[]{:T(512)S(6)} %eq.26), kind=kOutput, calls=%fused_computation.8 | convolution fusion | flops 3645112320 | bytes 11796481 | tf_op jit(solution)/shard_map/dot_general | solution.py:77
  168.7 1.2 slice_select_fusion.1
  170.5 1.1 copy.17
  171.6 1.5 collective-permute-done.10
  173.1 2.5 fusion.6
  175.6 56.9 %all-gather.5.cloned.1.call-done = bf16[768,3072]{1,0:T(8,128)(2,1)} async-done(((bf16[768,384]{1,0:T(8,128)(2,1)}), bf16[768,3072]{1,0:T(8,128)(2,1)}) %all-gather.5.cloned.1.call-update) | async-done | bytes 4718608 | tf_op jit(solution)/shard_map/all_gather | solution.py:117
  232.6 9.0 %fusion = f32[768,768]{1,0:T(8,128)S(1)} fusion(bf16[768,3072]{1,0:T(8,128)(2,1)} %all-gather.5.cloned.1.call-done, bf16[384,3072]{0,1:T(8,128)(2,1)} %collective-permute-done.9, bf16[384,3072]{0,1:T(8,128)(2,1)} %bitcast.19, pred[]{:T(512)S(6)} %eq.26), kind=kOutput, calls=%fused_computation.7 | convolution fusion | flops 3645112320 | bytes 11796481 | tf_op jit(solution)/shard_map/dot_general | solution.py:77
  241.7 0.9 collective-permute-start.11
  242.6 2.5 collective-permute-done.11
  245.0 1.3 select_convert_fusion
  (40 shorter events, 4.4 us)
Async XLA Ops:
  6.5 3.7 %copy-start = (s32[96,3]{0,1:T(4,128)S(1)}, s32[96,3]{0,1:T(4,128)}, u32[]{:S(2)}) copy-start(s32[96,3]{0,1:T(4,128)} %param.3) | copy-start | bytes 3460
  6.5 153.2 %all-gather.3.cloned.1.call-start = ((), (), s32[]{:S(2)}) async-start(), calls=%async_computation | async-start | bytes 5308416 | tf_op jit(solution)/shard_map/all_gather | solution.py:117
  7.9 3.4 %collective-permute-start = (bf16[384,384]{0,1:T(8,128)(2,1)S(1)}, bf16[384,384]{0,1:T(8,128)(2,1)S(1)}, u32[]{:S(2)}, u32[]{:S(2)}) collective-permute-start(bf16[384,384]{0,1:T(8,128)(2,1)S(1)} %copy.19), channel_id=1, source_target_pairs={{0,0},{1,1},{2,16},{3,17},{4,32},{5,33},{6,48},{7,49},{8,64},{9,65... | collective-permute-start | bytes 884744 | tf_op jit(solution)/shard_map/ppermute | solution.py:69
  8.8 2.7 %collective-permute-start.1 = (bf16[384,384]{0,1:T(8,128)(2,1)S(1)}, bf16[384,384]{0,1:T(8,128)(2,1)S(1)}, u32[]{:S(2)}, u32[]{:S(2)}) collective-permute-start(bf16[384,384]{0,1:T(8,128)(2,1)S(1)} %copy.20), channel_id=1, source_target_pairs={{0,1},{1,0},{2,17},{3,16},{4,33},{5,32},{6,49},{7,48},{8,65},{9,64... | collective-permute-start | bytes 884744 | tf_op jit(solution)/shard_map/ppermute | solution.py:69
  11.2 2.9 %copy-start.1 = (pred[768,384]{1,0:T(8,128)(4,1)}, pred[768,384]{1,0:T(8,128)(4,1)S(1)}, u32[]{:S(2)}) copy-start(pred[768,384]{1,0:T(8,128)(4,1)S(1)} %copy.18) | copy-start | bytes 884740
  11.5 2.6 %copy-start.3 = (bf16[768,384]{1,0:T(8,128)(2,1)S(1)}, bf16[768,384]{1,0:T(8,128)(2,1)}, u32[]{:S(2)}) copy-start(bf16[768,384]{1,0:T(8,128)(2,1)} %param.2) | copy-start | bytes 1769476
  15.7 216.8 %all-gather.5.cloned.1.call-start = ((), (), s32[]{:S(2)}) async-start(), calls=%async_computation.1 | async-start | bytes 5308416 | tf_op jit(solution)/shard_map/all_gather | solution.py:117
  15.8 37.8 %collective-permute-start.5 = (bf16[384,768]{0,1:T(8,128)(2,1)}, bf16[384,768]{0,1:T(8,128)(2,1)S(1)}, u32[]{:S(2)}, u32[]{:S(2)}) collective-permute-start(bf16[384,768]{0,1:T(8,128)(2,1)} %bitcast.21), channel_id=1, source_target_pairs={{0,16},{16,0},{1,17},{17,1},{2,18},{18,2},{3,19},{19,3},{4,20},{20... | collective-permute-start | bytes 1769480 | tf_op jit(solution)/shard_map/ppermute | solution.py:29
  38.7 69.4 %collective-permute-start.2 = (bf16[384,768]{0,1:T(8,128)(2,1)}, bf16[384,768]{0,1:T(8,128)(2,1)S(1)}, u32[]{:S(2)}, u32[]{:S(2)}) collective-permute-start(bf16[384,768]{0,1:T(8,128)(2,1)} %bitcast.22), channel_id=1, source_target_pairs={{0,32},{32,64},{64,96},{96,0},{1,33},{33,65},{65,97},{97,1},{2,34}... | collective-permute-start | bytes 1769480 | tf_op jit(solution)/shard_map/ppermute | solution.py:29
  53.6 68.8 %collective-permute-start.6 = (bf16[384,768]{0,1:T(8,128)(2,1)S(1)}, bf16[384,768]{0,1:T(8,128)(2,1)S(1)}, u32[]{:S(2)}, u32[]{:S(2)}) collective-permute-start(bf16[384,768]{0,1:T(8,128)(2,1)S(1)} %collective-permute-done.5), channel_id=1, source_target_pairs={{0,32},{32,64},{64,96},{96,0},{1,33},{33,65},{65,97},{97,1},{2,34}... | collective-permute-start | bytes 1769480 | tf_op jit(solution)/shard_map/ppermute | solution.py:29
  108.1 26.9 %collective-permute-start.3 = (bf16[384,768]{0,1:T(8,128)(2,1)S(1)}, bf16[384,768]{0,1:T(8,128)(2,1)S(1)}, u32[]{:S(2)}, u32[]{:S(2)}) collective-permute-start(bf16[384,768]{0,1:T(8,128)(2,1)S(1)} %collective-permute-done.2), channel_id=1, source_target_pairs={{0,32},{32,64},{64,96},{96,0},{1,33},{33,65},{65,97},{97,1},{2,34}... | collective-permute-start | bytes 1769480 | tf_op jit(solution)/shard_map/ppermute | solution.py:29
  109.4 26.5 %collective-permute-start.4 = (bf16[384,768]{0,1:T(8,128)(2,1)}, bf16[384,768]{0,1:T(8,128)(2,1)S(1)}, u32[]{:S(2)}, u32[]{:S(2)}) collective-permute-start(bf16[384,768]{0,1:T(8,128)(2,1)} %bitcast.23), channel_id=1, source_target_pairs={{0,96},{32,0},{64,32},{96,64},{1,97},{33,1},{65,33},{97,65},{2,98}... | collective-permute-start | bytes 1769480 | tf_op jit(solution)/shard_map/ppermute | solution.py:29
  110.8 37.8 %collective-permute-start.8 = (bf16[384,768]{0,1:T(8,128)(2,1)S(1)}, bf16[384,768]{0,1:T(8,128)(2,1)S(1)}, u32[]{:S(2)}, u32[]{:S(2)}) collective-permute-start(bf16[384,768]{0,1:T(8,128)(2,1)S(1)} %collective-permute-done.5), channel_id=1, source_target_pairs={{0,96},{32,0},{64,32},{96,64},{1,97},{33,1},{65,33},{97,65},{2,98}... | collective-permute-start | bytes 1769480 | tf_op jit(solution)/shard_map/ppermute | solution.py:29
  122.4 25.3 %collective-permute-start.7 = (bf16[384,768]{0,1:T(8,128)(2,1)S(1)}, bf16[384,768]{0,1:T(8,128)(2,1)S(1)}, u32[]{:S(2)}, u32[]{:S(2)}) collective-permute-start(bf16[384,768]{0,1:T(8,128)(2,1)S(1)} %collective-permute-done.6), channel_id=1, source_target_pairs={{0,32},{32,64},{64,96},{96,0},{1,33},{33,65},{65,97},{97,1},{2,34}... | collective-permute-start | bytes 1769480 | tf_op jit(solution)/shard_map/ppermute | solution.py:29
  153.9 5.8 %collective-permute-start.9 = (bf16[384,3072]{0,1:T(8,128)(2,1)S(1)}, bf16[384,3072]{0,1:T(8,128)(2,1)}, u32[]{:S(2)}, u32[]{:S(2)}) collective-permute-start(bf16[384,3072]{0,1:T(8,128)(2,1)S(1)} %bitcast.20), channel_id=1, source_target_pairs={{0,1},{1,0},{2,3},{3,2},{4,5},{5,4},{6,7},{7,6},{8,9},{9,8},{10,11... | collective-permute-start | bytes 7077896 | tf_op jit(solution)/shard_map/ppermute | solution.py:109
  169.9 3.2 %collective-permute-start.10 = (f32[768,384]{1,0:T(8,128)}, f32[768,384]{1,0:T(8,128)}, u32[]{:S(2)}, u32[]{:S(2)}) collective-permute-start(f32[768,384]{1,0:T(8,128)} %slice_select_fusion.1), channel_id=1, source_target_pairs={{0,1},{1,0},{2,3},{3,2},{4,5},{5,4},{6,7},{7,6},{8,9},{9,8},{10,11... | collective-permute-start | bytes 3538952 | tf_op jit(solution)/shard_map/ppermute | solution.py:121
  241.5 3.5 %copy-start.2 = (pred[768,384]{1,0:T(8,128)(4,1)S(1)}, pred[768,384]{1,0:T(8,128)(4,1)}, u32[]{:S(2)}) copy-start(pred[768,384]{1,0:T(8,128)(4,1)} %copy-done.1) | copy-start | bytes 884740
  241.7 3.4 %collective-permute-start.11 = (f32[768,384]{1,0:T(8,128)S(1)}, f32[768,384]{1,0:T(8,128)S(1)}, u32[]{:S(2)}, u32[]{:S(2)}) collective-permute-start(f32[768,384]{1,0:T(8,128)S(1)} %slice_select_fusion), channel_id=1, source_target_pairs={{0,1},{1,0},{2,3},{3,2},{4,5},{5,4},{6,7},{7,6},{8,9},{9,8},{10,11... | collective-permute-start | bytes 3538952 | tf_op jit(solution)/shard_map/ppermute | solution.py:121
Sparse Core Ops, SparseCore 0:
  15.8 88.9 all-gather.2
  175.7 56.7 all-gather.4

commit v10 on v6

--- a/solution.py
+++ b/solution.py
@@ -65,7 +65,8 @@
         for a in range(rows):
             for b in range(cols):
                 h = (b + k) % 2
-                pairs.append((a * cols + b, (b // 2) * cols + 2 * a + h))
+                if a <= b // 2:
+                    pairs.append((a * cols + b, (b // 2) * cols + 2 * a + h))
         pieces.append(lax.ppermute(piece, ROW + COL, pairs))
     h_own = col_id % 2
     first = jnp.where(h_own == 0, pieces[0], pieces[1])

time: 196 us -> 194 us (0.990)
  waiting for transfers between devices: 93.6 us -> 88.4 us
  starting transfers between devices: 54.6 us -> 58.1 us
    ppermute x7, waiting for transfers between devices: 31.3 us -> 28.6 us  [chunked_shift(): lax.ppermute(value[i * step:(i + 1) * step], axis, pairs)]
    all_gather x1, waiting for transfers between devices: 62 us -> 59.6 us  [per_device(): low_panel = lax.all_gather(square_low, COL, axis=1, tiled=True)]
where the time goes in v10:
time: 194 us
  waiting for transfers between devices  88.4 us (46%)
  starting transfers between devices  58.1 us (30%)
  matrix products  19.4 us (10%)
  between operations  13.6 us (7%)
  local copies, waits for them, and re-layouts  13 us (7%)
    all_gather x1, waiting for transfers between devices, per_device(): low_panel = lax.all_gather(square_low, COL, axis=1, tiled=True)  59.6 us
    ppermute x7, starting transfers between devices, chunked_shift(): lax.ppermute(value[i * step:(i + 1) * step], axis, pairs)  54.1 us
    ppermute x7, waiting for transfers between devices, chunked_shift(): lax.ppermute(value[i * step:(i + 1) * step], axis, pairs)  28.6 us
    dot_general x2, matrix products, dot_t(): lax.dot_general(left, right_t, (((1,), (1,)), ((), ())), preferred_elemen...  19.4 us
    dynamic_update_slice x7, local copies, waits for them, and re-layouts, ring_gather(): panel = lax.dynamic_update_slice_in_dim(panel, part, position * width, 1)  7.3 us
    ppermute x2, starting transfers between devices, mirror_tile(): pieces.append(lax.ppermute(piece, ROW + COL, pairs))  3.97 us
  transfers between devices with their start and end apart: 11, of which 6 were waited for; matrix products, arithmetic and copies ran while one was open for 5% of the time, Pallas kernels for 0%

profile of v10, /device:TPU:1, one launch (start us, length us, event | category | flops | bytes accessed | tf_op | source)
XLA Modules:
  0.0 194.2 jit_solution(1421929608432124653)
XLA Ops:
  6.5 1.2 constant_dynamic-slice_fusion.1
  7.7 0.2 copy.19
  7.9 0.7 collective-permute-start
  8.6 0.2 copy.20
  8.9 3.3 %collective-permute-start.1 = (bf16[384,384]{0,1:T(8,128)(2,1)S(1)}, bf16[384,384]{0,1:T(8,128)(2,1)S(1)}, u32[]{:S(2)}, u32[]{:S(2)}) collective-permute-start(bf16[384,384]{0,1:T(8,128)(2,1)S(1)} %copy.20), channel_id=1, source_target_pairs={{0,1},{1,0},{2,17},{3,16},{4,33},{5,32},{6,49},{7,48},{8,65},{9,64... | collective-permute-start | bytes 884744 | tf_op jit(solution)/shard_map/ppermute | solution.py:70
  12.5 0.1 reshape.14
  12.7 0.4 copy.18
  13.1 0.2 collective-permute-done.1
  13.4 2.7 %broadcast_in_dim.37 = bf16[384,6144]{0,1:T(8,128)(2,1)} broadcast(bf16[]{:T(256)} %constant.98.clone.1), dimensions={} | broadcast | bytes 4718594 | tf_op jit(solution)/shard_map/broadcast_in_dim | solution.py:52
  16.1 1.5 constant_dynamic-update-slice_fusion.7
  17.7 18.5 %collective-permute-start.5 = (bf16[384,768]{0,1:T(8,128)(2,1)}, bf16[384,768]{0,1:T(8,128)(2,1)S(1)}, u32[]{:S(2)}, u32[]{:S(2)}) collective-permute-start(bf16[384,768]{0,1:T(8,128)(2,1)} %bitcast.17), channel_id=1, source_target_pairs={{0,16},{16,0},{1,17},{17,1},{2,18},{18,2},{3,19},{19,3},{4,20},{20... | collective-permute-start | bytes 1769480 | tf_op jit(solution)/shard_map/ppermute | solution.py:29
  36.1 13.2 %collective-permute-start.2 = (bf16[384,768]{0,1:T(8,128)(2,1)}, bf16[384,768]{0,1:T(8,128)(2,1)S(1)}, u32[]{:S(2)}, u32[]{:S(2)}) collective-permute-start(bf16[384,768]{0,1:T(8,128)(2,1)} %bitcast.18), channel_id=1, source_target_pairs={{0,32},{32,64},{64,96},{96,0},{1,33},{33,65},{65,97},{97,1},{2,34}... | collective-permute-start | bytes 1769480 | tf_op jit(solution)/shard_map/ppermute | solution.py:29
  49.3 0.4 collective-permute-done.5
  49.7 16.7 %collective-permute-start.6 = (bf16[384,768]{0,1:T(8,128)(2,1)S(1)}, bf16[384,768]{0,1:T(8,128)(2,1)S(1)}, u32[]{:S(2)}, u32[]{:S(2)}) collective-permute-start(bf16[384,768]{0,1:T(8,128)(2,1)S(1)} %collective-permute-done.5), channel_id=1, source_target_pairs={{0,32},{32,64},{64,96},{96,0},{1,33},{33,65},{65,97},{97,1},{2,34}... | collective-permute-start | bytes 1769480 | tf_op jit(solution)/shard_map/ppermute | solution.py:29
  66.4 2.0 %collective-permute-start.3 = (bf16[384,768]{0,1:T(8,128)(2,1)S(1)}, bf16[384,768]{0,1:T(8,128)(2,1)}, u32[]{:S(2)}, u32[]{:S(2)}) collective-permute-start(bf16[384,768]{0,1:T(8,128)(2,1)S(1)} %collective-permute-done.2), channel_id=1, source_target_pairs={{0,32},{32,64},{64,96},{96,0},{1,33},{33,65},{65,97},{97,1},{2,34}... | collective-permute-start | bytes 1769480 | tf_op jit(solution)/shard_map/ppermute | solution.py:29
  68.4 2.2 %collective-permute-start.4 = (bf16[384,768]{0,1:T(8,128)(2,1)}, bf16[384,768]{0,1:T(8,128)(2,1)S(1)}, u32[]{:S(2)}, u32[]{:S(2)}) collective-permute-start(bf16[384,768]{0,1:T(8,128)(2,1)} %bitcast.19), channel_id=1, source_target_pairs={{0,96},{32,0},{64,32},{96,64},{1,97},{33,1},{65,33},{97,65},{2,98}... | collective-permute-start | bytes 1769480 | tf_op jit(solution)/shard_map/ppermute | solution.py:29
  70.7 0.1 reshape.16
  70.9 0.4 copy.17
  71.3 1.5 collective-permute-start.8
  72.8 8.5 %collective-permute-done.6 = bf16[384,768]{0,1:T(8,128)(2,1)S(1)} collective-permute-done((bf16[384,768]{0,1:T(8,128)(2,1)S(1)}, bf16[384,768]{0,1:T(8,128)(2,1)S(1)}, u32[]{:S(2)}, u32[]{:S(2)}) %collective-permute-start.6) | collective-permute-done | bytes 589856 | tf_op jit(solution)/shard_map/ppermute | solution.py:29
  81.3 0.9 constant_dynamic-update-slice_fusion.6
  82.2 11.9 %collective-permute-done.3 = bf16[384,768]{0,1:T(8,128)(2,1)} collective-permute-done((bf16[384,768]{0,1:T(8,128)(2,1)S(1)}, bf16[384,768]{0,1:T(8,128)(2,1)}, u32[]{:S(2)}, u32[]{:S(2)}) %collective-permute-start.3) | collective-permute-done | bytes 589856 | tf_op jit(solution)/shard_map/ppermute | solution.py:29
  94.0 1.9 %constant_dynamic-update-slice_fusion.5 = bf16[384,6144]{0,1:T(8,128)(2,1)} fusion(bf16[384,6144]{0,1:T(8,128)(2,1)} %constant_dynamic-update-slice_fusion.6, bf16[384,768]{0,1:T(8,128)(2,1)} %collective-permute-done.3, s32[]{:T(128)S(6)} %select_n.122), kind=kLoop, calls=%fused_computation.17 | loop fusion | bytes 1179652 | tf_op jit(solution)/shard_map/dynamic_update_slice | solution.py:44
  96.0 0.9 constant_dynamic-update-slice_fusion.4
  96.9 0.9 constant_dynamic-update-slice_fusion.3
  97.8 0.9 constant_dynamic-update-slice_fusion.2
  98.7 7.9 %collective-permute-done.7 = bf16[384,768]{0,1:T(8,128)(2,1)S(1)} collective-permute-done((bf16[384,768]{0,1:T(8,128)(2,1)S(1)}, bf16[384,768]{0,1:T(8,128)(2,1)S(1)}, u32[]{:S(2)}, u32[]{:S(2)}) %collective-permute-start.7) | collective-permute-done | bytes 589856 | tf_op jit(solution)/shard_map/ppermute | solution.py:29
  106.6 0.9 constant_dynamic-update-slice_fusion.1
  107.5 0.9 constant_dynamic-update-slice_fusion
  108.3 9.7 %fusion.2 = (bf16[768,384]{1,0:T(8,128)(2,1)}, f32[768,384]{1,0:T(8,128)S(1)}) fusion(pred[768,384]{1,0:T(32,128)(4,1)S(1)} %copy.17, bf16[768,6144]{1,0:T(8,128)(2,1)} %all-gather.3.cloned.1.call-done, bf16[384,6144]{0,1:T(8,128)(2,1)} %constant_dynamic-update-slice_fusion), kind=kOutput, calls=%fused_computation.27 | convolution fusion | flops 3624468480 | bytes 16220160 | tf_op jit(solution)/shard_map/dot_general | solution.py:78
  118.1 59.6 %all-gather.5.cloned.1.call-done = bf16[768,6144]{1,0:T(8,128)(2,1)} async-done(((bf16[768,384]{1,0:T(8,128)(2,1)}), bf16[768,6144]{1,0:T(8,128)(2,1)}) %all-gather.5.cloned.1.call-update) | async-done | bytes 9437200 | tf_op jit(solution)/shard_map/all_gather | solution.py:108
  177.6 9.7 %select_convert_fusion = bf16[768,384]{1,0:T(8,128)(2,1)} fusion(pred[768,384]{1,0:T(32,128)(4,1)S(1)} %copy.18, f32[768,384]{1,0:T(8,128)S(1)} %get-tuple-element.14, bf16[768,6144]{1,0:T(8,128)(2,1)} %all-gather.5.cloned.1.call-done, bf16[384,6144]{0,1:T(8,128)(2,1)} %constant_dynamic-update-slice_fusion), kind=kOutput, calls=%fused_computation.2 | convolution fusion | flops 3625353216 | bytes 16220160 | tf_op jit(solution)/shard_map/dot_general | solution.py:78
  (25 shorter events, 0.7 us)
Async XLA Ops:
  6.5 5.6 %copy-start = (s32[96,3]{0,1:T(4,128)S(1)}, s32[96,3]{0,1:T(4,128)}, u32[]{:S(2)}) copy-start(s32[96,3]{0,1:T(4,128)} %param.3) | copy-start | bytes 3460
  6.5 9.5 %copy-start.1 = (bf16[768,384]{1,0:T(8,128)(2,1)S(1)}, bf16[768,384]{1,0:T(8,128)(2,1)}, u32[]{:S(2)}) copy-start(bf16[768,384]{1,0:T(8,128)(2,1)} %param.2) | copy-start | bytes 1769476
  6.5 101.8 %all-gather.3.cloned.1.call-start = ((), (), s32[]{:S(2)}) async-start(), calls=%async_computation | async-start | bytes 10027008 | tf_op jit(solution)/shard_map/all_gather | solution.py:104
  7.9 5.2 %collective-permute-start = (bf16[384,384]{0,1:T(8,128)(2,1)S(1)}, bf16[384,384]{0,1:T(8,128)(2,1)S(1)}, u32[]{:S(2)}, u32[]{:S(2)}) collective-permute-start(bf16[384,384]{0,1:T(8,128)(2,1)S(1)} %copy.19), channel_id=1, source_target_pairs={{0,0},{1,1},{2,16},{3,17},{4,32},{5,33},{6,48},{7,49},{8,64},{9,65... | collective-permute-start | bytes 884744 | tf_op jit(solution)/shard_map/ppermute | solution.py:70
  8.9 4.5 %collective-permute-start.1 = (bf16[384,384]{0,1:T(8,128)(2,1)S(1)}, bf16[384,384]{0,1:T(8,128)(2,1)S(1)}, u32[]{:S(2)}, u32[]{:S(2)}) collective-permute-start(bf16[384,384]{0,1:T(8,128)(2,1)S(1)} %copy.20), channel_id=1, source_target_pairs={{0,1},{1,0},{2,17},{3,16},{4,33},{5,32},{6,49},{7,48},{8,65},{9,64... | collective-permute-start | bytes 884744 | tf_op jit(solution)/shard_map/ppermute | solution.py:70
  17.6 160.0 %all-gather.5.cloned.1.call-start = ((), (), s32[]{:S(2)}) async-start(), calls=%async_computation.1 | async-start | bytes 10027008 | tf_op jit(solution)/shard_map/all_gather | solution.py:108
  17.7 32.0 %collective-permute-start.5 = (bf16[384,768]{0,1:T(8,128)(2,1)}, bf16[384,768]{0,1:T(8,128)(2,1)S(1)}, u32[]{:S(2)}, u32[]{:S(2)}) collective-permute-start(bf16[384,768]{0,1:T(8,128)(2,1)} %bitcast.17), channel_id=1, source_target_pairs={{0,16},{16,0},{1,17},{17,1},{2,18},{18,2},{3,19},{19,3},{4,20},{20... | collective-permute-start | bytes 1769480 | tf_op jit(solution)/shard_map/ppermute | solution.py:29
  36.1 30.3 %collective-permute-start.2 = (bf16[384,768]{0,1:T(8,128)(2,1)}, bf16[384,768]{0,1:T(8,128)(2,1)S(1)}, u32[]{:S(2)}, u32[]{:S(2)}) collective-permute-start(bf16[384,768]{0,1:T(8,128)(2,1)} %bitcast.18), channel_id=1, source_target_pairs={{0,32},{32,64},{64,96},{96,0},{1,33},{33,65},{65,97},{97,1},{2,34}... | collective-permute-start | bytes 1769480 | tf_op jit(solution)/shard_map/ppermute | solution.py:29
  49.7 31.6 %collective-permute-start.6 = (bf16[384,768]{0,1:T(8,128)(2,1)S(1)}, bf16[384,768]{0,1:T(8,128)(2,1)S(1)}, u32[]{:S(2)}, u32[]{:S(2)}) collective-permute-start(bf16[384,768]{0,1:T(8,128)(2,1)S(1)} %collective-permute-done.5), channel_id=1, source_target_pairs={{0,32},{32,64},{64,96},{96,0},{1,33},{33,65},{65,97},{97,1},{2,34}... | collective-permute-start | bytes 1769480 | tf_op jit(solution)/shard_map/ppermute | solution.py:29
  66.4 27.6 %collective-permute-start.3 = (bf16[384,768]{0,1:T(8,128)(2,1)S(1)}, bf16[384,768]{0,1:T(8,128)(2,1)}, u32[]{:S(2)}, u32[]{:S(2)}) collective-permute-start(bf16[384,768]{0,1:T(8,128)(2,1)S(1)} %collective-permute-done.2), channel_id=1, source_target_pairs={{0,32},{32,64},{64,96},{96,0},{1,33},{33,65},{65,97},{97,1},{2,34}... | collective-permute-start | bytes 1769480 | tf_op jit(solution)/shard_map/ppermute | solution.py:29
  68.4 27.5 %collective-permute-start.4 = (bf16[384,768]{0,1:T(8,128)(2,1)}, bf16[384,768]{0,1:T(8,128)(2,1)S(1)}, u32[]{:S(2)}, u32[]{:S(2)}) collective-permute-start(bf16[384,768]{0,1:T(8,128)(2,1)} %bitcast.19), channel_id=1, source_target_pairs={{0,96},{32,0},{64,32},{96,64},{1,97},{33,1},{65,33},{97,65},{2,98}... | collective-permute-start | bytes 1769480 | tf_op jit(solution)/shard_map/ppermute | solution.py:29
  71.3 36.1 %collective-permute-start.8 = (bf16[384,768]{0,1:T(8,128)(2,1)S(1)}, bf16[384,768]{0,1:T(8,128)(2,1)S(1)}, u32[]{:S(2)}, u32[]{:S(2)}) collective-permute-start(bf16[384,768]{0,1:T(8,128)(2,1)S(1)} %collective-permute-done.5), channel_id=1, source_target_pairs={{0,96},{32,0},{64,32},{96,64},{1,97},{33,1},{65,33},{97,65},{2,98}... | collective-permute-start | bytes 1769480 | tf_op jit(solution)/shard_map/ppermute | solution.py:29
  81.3 25.3 %collective-permute-start.7 = (bf16[384,768]{0,1:T(8,128)(2,1)S(1)}, bf16[384,768]{0,1:T(8,128)(2,1)S(1)}, u32[]{:S(2)}, u32[]{:S(2)}) collective-permute-start(bf16[384,768]{0,1:T(8,128)(2,1)S(1)} %collective-permute-done.6), channel_id=1, source_target_pairs={{0,32},{32,64},{64,96},{96,0},{1,33},{33,65},{65,97},{97,1},{2,34}... | collective-permute-start | bytes 1769480 | tf_op jit(solution)/shard_map/ppermute | solution.py:29
Sparse Core Ops, SparseCore 0:
  17.7 86.4 all-gather.2
  118.2 59.4 all-gather.4

commit v11 on v10

--- a/solution.py
+++ b/solution.py
@@ -30,28 +30,24 @@
     return jnp.concatenate(parts, 0)
 
 
-def ring_gather(tile_t, panel, plane):
+def column_panel_t(tile_t):
     ring = lax.axis_size("y")
-    up = [(i, (i + 1) % ring) for i in range(ring)]
-    down = [(i, (i - 1) % ring) for i in range(ring)]
-    from_below = chunked_shift(tile_t, "y", up)
-    from_above = chunked_shift(tile_t, "y", down)
-    from_two_below = chunked_shift(from_below, "y", up)
     y_id = lax.axis_index("y")
+    zh_id = lax.axis_index("zh")
     width = tile_t.shape[1]
-    for offset, part in ((0, tile_t), (-1, from_below), (-2, from_two_below), (1, from_above)):
-        position = ((y_id + offset) % ring) * 2 + plane
-        panel = lax.dynamic_update_slice_in_dim(panel, part, position * width, 1)
+    panel = jnp.zeros((tile_t.shape[0], 2 * ring * width), tile_t.dtype)
+    panel = lax.dynamic_update_slice_in_dim(panel, tile_t, (y_id * 2 + zh_id) * width, 1)
+    for dy in range(ring):
+        for dz in range(2):
+            if dy == 0 and dz == 0:
+                continue
+            pairs = [
+                (y * 2 + z, ((y + dy) % ring) * 2 + (z ^ dz)) for y in range(ring) for z in range(2)
+            ]
+            part = lax.ppermute(tile_t, ROW, pairs)
+            source = ((y_id - dy) % ring) * 2 + (zh_id ^ dz)
+            panel = lax.dynamic_update_slice_in_dim(panel, part, source * width, 1)
     return panel
-
-
-def column_panel_t(tile_t):
-    partner = chunked_shift(tile_t, "zh", [(0, 1), (1, 0)])
-    zh_id = lax.axis_index("zh")
-    ring = lax.axis_size("y")
-    panel = jnp.zeros((tile_t.shape[0], 2 * ring * tile_t.shape[1]), tile_t.dtype)
-    panel = ring_gather(tile_t, panel, zh_id)
-    return ring_gather(partner, panel, 1 - zh_id)
 
 
 def mirror_tile(upper_stored, rows, cols):

time: 194 us -> 234 us (1.21)
  starting transfers between devices: 58.1 us -> 84.9 us
  waiting for transfers between devices: 88.4 us -> 101 us
    ppermute x7, starting transfers between devices: 54.1 us -> 80.9 us  [column_panel_t(): part = lax.ppermute(tile_t, ROW, pairs)]
    all_gather x1, waiting for transfers between devices: 0.01 us -> 15.1 us  [per_device(): row_panel = lax.all_gather(density, COL, axis=1, tiled=True)]
    ppermute x7, waiting for transfers between devices: 28.6 us -> 20.5 us  [column_panel_t(): part = lax.ppermute(tile_t, ROW, pairs)]
    all_gather x1, waiting for transfers between devices: 59.6 us -> 65.2 us  [per_device(): low_panel = lax.all_gather(square_low, COL, axis=1, tiled=True)]
  transfers between devices with their start and end apart: 11 -> 11, of which waited for: 6 -> 6; matrix products, arithmetic and copies ran while one was open for 5% -> 4% of each run, Pallas kernels for 0% -> 0%
where the time goes in v11:
time: 234 us
  waiting for transfers between devices  101 us (43%)
  starting transfers between devices  84.9 us (36%)
  matrix products  19.4 us (8%)
  between operations  13.6 us (6%)
  local copies, waits for them, and re-layouts  13 us (6%)
    ppermute x7, starting transfers between devices, column_panel_t(): part = lax.ppermute(tile_t, ROW, pairs)  80.9 us
    all_gather x1, waiting for transfers between devices, per_device(): low_panel = lax.all_gather(square_low, COL, axis=1, tiled=True)  65.2 us
    ppermute x7, waiting for transfers between devices, column_panel_t(): part = lax.ppermute(tile_t, ROW, pairs)  20.5 us
    dot_general x2, matrix products, dot_t(): lax.dot_general(left, right_t, (((1,), (1,)), ((), ())), preferred_elemen...  19.4 us
    all_gather x1, waiting for transfers between devices, per_device(): row_panel = lax.all_gather(density, COL, axis=1, tiled=True)  15.1 us
    dynamic_update_slice x7, local copies, waits for them, and re-layouts, column_panel_t(): panel = lax.dynamic_update_slice_in_dim(panel, part, source * width, 1)  7.3 us
  transfers between devices with their start and end apart: 11, of which 6 were waited for; matrix products, arithmetic and copies ran while one was open for 4% of the time, Pallas kernels for 0%

profile of v11, /device:TPU:1, one launch (start us, length us, event | category | flops | bytes accessed | tf_op | source)
XLA Modules:
  0.0 233.7 jit_solution(6369445750035507419)
XLA Ops:
  6.5 1.2 constant_dynamic-slice_fusion.1
  7.7 0.2 copy.19
  7.9 0.7 collective-permute-start
  8.6 0.2 copy.20
  8.9 3.3 %collective-permute-start.1 = (bf16[384,384]{0,1:T(8,128)(2,1)S(1)}, bf16[384,384]{0,1:T(8,128)(2,1)S(1)}, u32[]{:S(2)}, u32[]{:S(2)}) collective-permute-start(bf16[384,384]{0,1:T(8,128)(2,1)S(1)} %copy.20), channel_id=1, source_target_pairs={{0,1},{1,0},{2,17},{3,16},{4,33},{5,32},{6,49},{7,48},{8,65},{9,64... | collective-permute-start | bytes 884744 | tf_op jit(solution)/shard_map/ppermute | solution.py:66
  12.5 0.1 reshape.14
  12.7 0.4 copy.18
  13.1 0.2 collective-permute-done.1
  13.4 2.7 %broadcast_in_dim.37 = bf16[384,6144]{0,1:T(8,128)(2,1)} broadcast(bf16[]{:T(256)} %constant.98.clone.1), dimensions={} | broadcast | bytes 4718594 | tf_op jit(solution)/shard_map/broadcast_in_dim | solution.py:38
  16.1 1.5 constant_dynamic-update-slice_fusion.7
  17.7 18.5 %collective-permute-start.2 = (bf16[384,768]{0,1:T(8,128)(2,1)}, bf16[384,768]{0,1:T(8,128)(2,1)}, u32[]{:S(2)}, u32[]{:S(2)}) collective-permute-start(bf16[384,768]{0,1:T(8,128)(2,1)} %bitcast.17), channel_id=1, source_target_pairs={{0,16},{16,0},{32,48},{48,32},{64,80},{80,64},{96,112},{112,96},{1... | collective-permute-start | bytes 1769480 | tf_op jit(solution)/shard_map/ppermute | solution.py:47
  36.1 13.2 %collective-permute-start.3 = (bf16[384,768]{0,1:T(8,128)(2,1)}, bf16[384,768]{0,1:T(8,128)(2,1)S(1)}, u32[]{:S(2)}, u32[]{:S(2)}) collective-permute-start(bf16[384,768]{0,1:T(8,128)(2,1)} %bitcast.18), channel_id=1, source_target_pairs={{0,32},{16,48},{32,64},{48,80},{64,96},{80,112},{96,0},{112,16},{1... | collective-permute-start | bytes 1769480 | tf_op jit(solution)/shard_map/ppermute | solution.py:47
  49.3 1.6 collective-permute-start.4
  51.0 2.2 collective-permute-start.5
  53.2 2.4 %collective-permute-start.6 = (bf16[384,768]{0,1:T(8,128)(2,1)}, bf16[384,768]{0,1:T(8,128)(2,1)S(1)}, u32[]{:S(2)}, u32[]{:S(2)}) collective-permute-start(bf16[384,768]{0,1:T(8,128)(2,1)} %bitcast.21), channel_id=1, source_target_pairs={{0,80},{16,64},{32,112},{48,96},{64,16},{80,0},{96,48},{112,32},{1... | collective-permute-start | bytes 1769480 | tf_op jit(solution)/shard_map/ppermute | solution.py:47
  55.9 0.4 copy.17
  56.3 39.5 %collective-permute-start.7 = (bf16[384,768]{0,1:T(8,128)(2,1)}, bf16[384,768]{0,1:T(8,128)(2,1)S(1)}, u32[]{:S(2)}, u32[]{:S(2)}) collective-permute-start(bf16[384,768]{0,1:T(8,128)(2,1)} %bitcast.22), channel_id=1, source_target_pairs={{0,96},{16,112},{32,0},{48,16},{64,32},{80,48},{96,64},{112,80},{1... | collective-permute-start | bytes 1769480 | tf_op jit(solution)/shard_map/ppermute | solution.py:47
  95.8 2.0 constant_dynamic-update-slice_fusion.6
  97.8 3.4 %collective-permute-start.8 = (bf16[384,768]{0,1:T(8,128)(2,1)}, bf16[384,768]{0,1:T(8,128)(2,1)S(1)}, u32[]{:S(2)}, u32[]{:S(2)}) collective-permute-start(bf16[384,768]{0,1:T(8,128)(2,1)} %bitcast.23), channel_id=1, source_target_pairs={{0,112},{16,96},{32,16},{48,0},{64,48},{80,32},{96,80},{112,64},{1... | collective-permute-start | bytes 1769480 | tf_op jit(solution)/shard_map/ppermute | solution.py:47
  101.2 0.9 constant_dynamic-update-slice_fusion.5
  102.1 0.9 constant_dynamic-update-slice_fusion.4
  103.0 0.8 collective-permute-done.5
  103.8 0.9 constant_dynamic-update-slice_fusion.3
  104.7 16.6 %collective-permute-done.6 = bf16[384,768]{0,1:T(8,128)(2,1)S(1)} collective-permute-done((bf16[384,768]{0,1:T(8,128)(2,1)}, bf16[384,768]{0,1:T(8,128)(2,1)S(1)}, u32[]{:S(2)}, u32[]{:S(2)}) %collective-permute-start.6) | collective-permute-done | bytes 589856 | tf_op jit(solution)/shard_map/ppermute | solution.py:47
  121.3 0.9 constant_dynamic-update-slice_fusion.2
  122.2 0.9 constant_dynamic-update-slice_fusion.1
  123.1 3.2 %collective-permute-done.8 = bf16[384,768]{0,1:T(8,128)(2,1)S(1)} collective-permute-done((bf16[384,768]{0,1:T(8,128)(2,1)}, bf16[384,768]{0,1:T(8,128)(2,1)S(1)}, u32[]{:S(2)}, u32[]{:S(2)}) %collective-permute-start.8) | collective-permute-done | bytes 589856 | tf_op jit(solution)/shard_map/ppermute | solution.py:47
  126.3 0.9 constant_dynamic-update-slice_fusion
  127.1 15.1 %all-gather.3.cloned.1.call-done = bf16[768,6144]{1,0:T(8,128)(2,1)} async-done(((bf16[768,384]{1,0:T(8,128)(2,1)}), bf16[768,6144]{1,0:T(8,128)(2,1)}) %all-gather.3.cloned.1.call-update) | async-done | bytes 9437200 | tf_op jit(solution)/shard_map/all_gather | solution.py:100
  142.2 9.7 %fusion.2 = (bf16[768,384]{1,0:T(8,128)(2,1)}, f32[768,384]{1,0:T(8,128)S(1)}) fusion(pred[768,384]{1,0:T(32,128)(4,1)S(1)} %copy.17, bf16[768,6144]{1,0:T(8,128)(2,1)} %all-gather.3.cloned.1.call-done, bf16[384,6144]{0,1:T(8,128)(2,1)} %constant_dynamic-update-slice_fusion), kind=kOutput, calls=%fused_computation.27 | convolution fusion | flops 3624468480 | bytes 16220160 | tf_op jit(solution)/shard_map/dot_general | solution.py:74
  151.9 65.2 %all-gather.5.cloned.1.call-done = bf16[768,6144]{1,0:T(8,128)(2,1)} async-done(((bf16[768,384]{1,0:T(8,128)(2,1)}), bf16[768,6144]{1,0:T(8,128)(2,1)}) %all-gather.5.cloned.1.call-update) | async-done | bytes 9437200 | tf_op jit(solution)/shard_map/all_gather | solution.py:104
  217.1 9.7 %select_convert_fusion = bf16[768,384]{1,0:T(8,128)(2,1)} fusion(pred[768,384]{1,0:T(32,128)(4,1)S(1)} %copy.18, f32[768,384]{1,0:T(8,128)S(1)} %get-tuple-element.14, bf16[768,6144]{1,0:T(8,128)(2,1)} %all-gather.5.cloned.1.call-done, bf16[384,6144]{0,1:T(8,128)(2,1)} %constant_dynamic-update-slice_fusion), kind=kOutput, calls=%fused_computation.2 | convolution fusion | flops 3625353216 | bytes 16220160 | tf_op jit(solution)/shard_map/dot_general | solution.py:74
  (25 shorter events, 0.8 us)
Async XLA Ops:
  6.5 5.6 %copy-start = (s32[96,3]{0,1:T(4,128)S(1)}, s32[96,3]{0,1:T(4,128)}, u32[]{:S(2)}) copy-start(s32[96,3]{0,1:T(4,128)} %param.3) | copy-start | bytes 3460
  6.5 9.5 %copy-start.1 = (bf16[768,384]{1,0:T(8,128)(2,1)S(1)}, bf16[768,384]{1,0:T(8,128)(2,1)}, u32[]{:S(2)}) copy-start(bf16[768,384]{1,0:T(8,128)(2,1)} %param.2) | copy-start | bytes 1769476
  6.5 135.7 %all-gather.3.cloned.1.call-start = ((), (), s32[]{:S(2)}) async-start(), calls=%async_computation | async-start | bytes 10027008 | tf_op jit(solution)/shard_map/all_gather | solution.py:100
  7.9 5.2 %collective-permute-start = (bf16[384,384]{0,1:T(8,128)(2,1)S(1)}, bf16[384,384]{0,1:T(8,128)(2,1)S(1)}, u32[]{:S(2)}, u32[]{:S(2)}) collective-permute-start(bf16[384,384]{0,1:T(8,128)(2,1)S(1)} %copy.19), channel_id=1, source_target_pairs={{0,0},{1,1},{2,16},{3,17},{4,32},{5,33},{6,48},{7,49},{8,64},{9,65... | collective-permute-start | bytes 884744 | tf_op jit(solution)/shard_map/ppermute | solution.py:66
  8.9 4.5 %collective-permute-start.1 = (bf16[384,384]{0,1:T(8,128)(2,1)S(1)}, bf16[384,384]{0,1:T(8,128)(2,1)S(1)}, u32[]{:S(2)}, u32[]{:S(2)}) collective-permute-start(bf16[384,384]{0,1:T(8,128)(2,1)S(1)} %copy.20), channel_id=1, source_target_pairs={{0,1},{1,0},{2,17},{3,16},{4,33},{5,32},{6,49},{7,48},{8,65},{9,64... | collective-permute-start | bytes 884744 | tf_op jit(solution)/shard_map/ppermute | solution.py:66
  17.6 199.5 %all-gather.5.cloned.1.call-start = ((), (), s32[]{:S(2)}) async-start(), calls=%async_computation.1 | async-start | bytes 10027008 | tf_op jit(solution)/shard_map/all_gather | solution.py:104
  17.7 38.6 %collective-permute-start.2 = (bf16[384,768]{0,1:T(8,128)(2,1)}, bf16[384,768]{0,1:T(8,128)(2,1)}, u32[]{:S(2)}, u32[]{:S(2)}) collective-permute-start(bf16[384,768]{0,1:T(8,128)(2,1)} %bitcast.17), channel_id=1, source_target_pairs={{0,16},{16,0},{32,48},{48,32},{64,80},{80,64},{96,112},{112,96},{1... | collective-permute-start | bytes 1769480 | tf_op jit(solution)/shard_map/ppermute | solution.py:47
  36.1 61.6 %collective-permute-start.3 = (bf16[384,768]{0,1:T(8,128)(2,1)}, bf16[384,768]{0,1:T(8,128)(2,1)S(1)}, u32[]{:S(2)}, u32[]{:S(2)}) collective-permute-start(bf16[384,768]{0,1:T(8,128)(2,1)} %bitcast.18), channel_id=1, source_target_pairs={{0,32},{16,48},{32,64},{48,80},{64,96},{80,112},{96,0},{112,16},{1... | collective-permute-start | bytes 1769480 | tf_op jit(solution)/shard_map/ppermute | solution.py:47
  49.3 52.8 %collective-permute-start.4 = (bf16[384,768]{0,1:T(8,128)(2,1)}, bf16[384,768]{0,1:T(8,128)(2,1)S(1)}, u32[]{:S(2)}, u32[]{:S(2)}) collective-permute-start(bf16[384,768]{0,1:T(8,128)(2,1)} %bitcast.19), channel_id=1, source_target_pairs={{0,48},{16,32},{32,80},{48,64},{64,112},{80,96},{96,16},{112,0},{1... | collective-permute-start | bytes 1769480 | tf_op jit(solution)/shard_map/ppermute | solution.py:47
  51.0 52.8 %collective-permute-start.5 = (bf16[384,768]{0,1:T(8,128)(2,1)}, bf16[384,768]{0,1:T(8,128)(2,1)S(1)}, u32[]{:S(2)}, u32[]{:S(2)}) collective-permute-start(bf16[384,768]{0,1:T(8,128)(2,1)} %bitcast.20), channel_id=1, source_target_pairs={{0,64},{16,80},{32,96},{48,112},{64,0},{80,16},{96,32},{112,48},{1... | collective-permute-start | bytes 1769480 | tf_op jit(solution)/shard_map/ppermute | solution.py:47
  53.2 68.1 %collective-permute-start.6 = (bf16[384,768]{0,1:T(8,128)(2,1)}, bf16[384,768]{0,1:T(8,128)(2,1)S(1)}, u32[]{:S(2)}, u32[]{:S(2)}) collective-permute-start(bf16[384,768]{0,1:T(8,128)(2,1)} %bitcast.21), channel_id=1, source_target_pairs={{0,80},{16,64},{32,112},{48,96},{64,16},{80,0},{96,48},{112,32},{1... | collective-permute-start | bytes 1769480 | tf_op jit(solution)/shard_map/ppermute | solution.py:47
  56.3 65.9 %collective-permute-start.7 = (bf16[384,768]{0,1:T(8,128)(2,1)}, bf16[384,768]{0,1:T(8,128)(2,1)S(1)}, u32[]{:S(2)}, u32[]{:S(2)}) collective-permute-start(bf16[384,768]{0,1:T(8,128)(2,1)} %bitcast.22), channel_id=1, source_target_pairs={{0,96},{16,112},{32,0},{48,16},{64,32},{80,48},{96,64},{112,80},{1... | collective-permute-start | bytes 1769480 | tf_op jit(solution)/shard_map/ppermute | solution.py:47
  97.8 28.5 %collective-permute-start.8 = (bf16[384,768]{0,1:T(8,128)(2,1)}, bf16[384,768]{0,1:T(8,128)(2,1)S(1)}, u32[]{:S(2)}, u32[]{:S(2)}) collective-permute-start(bf16[384,768]{0,1:T(8,128)(2,1)} %bitcast.23), channel_id=1, source_target_pairs={{0,112},{16,96},{32,16},{48,0},{64,48},{80,32},{96,80},{112,64},{1... | collective-permute-start | bytes 1769480 | tf_op jit(solution)/shard_map/ppermute | solution.py:47
Sparse Core Ops, SparseCore 0:
  17.7 124.4 all-gather.2
  152.0 65.0 all-gather.4

commit v12 on v10

--- a/solution.py
+++ b/solution.py
@@ -30,7 +30,7 @@
     return jnp.concatenate(parts, 0)
 
 
-def ring_gather(tile_t, panel, plane):
+def ring_gather(tile_t, plane, pieces):
     ring = lax.axis_size("y")
     up = [(i, (i + 1) % ring) for i in range(ring)]
     down = [(i, (i - 1) % ring) for i in range(ring)]
@@ -38,20 +38,25 @@
     from_above = chunked_shift(tile_t, "y", down)
     from_two_below = chunked_shift(from_below, "y", up)
     y_id = lax.axis_index("y")
-    width = tile_t.shape[1]
-    for offset, part in ((0, tile_t), (-1, from_below), (-2, from_two_below), (1, from_above)):
-        position = ((y_id + offset) % ring) * 2 + plane
+    for offset, part in ((0, tile_t), (-1, from_below), (1, from_above), (-2, from_two_below)):
+        pieces.append((part, ((y_id + offset) % ring) * 2 + plane))
+
+
+def column_pieces_t(tile_t):
+    partner = chunked_shift(tile_t, "zh", [(0, 1), (1, 0)])
+    zh_id = lax.axis_index("zh")
+    pieces = []
+    ring_gather(tile_t, zh_id, pieces)
+    ring_gather(partner, 1 - zh_id, pieces)
+    return pieces
+
+
+def assemble(pieces):
+    width = pieces[0][0].shape[1]
+    panel = jnp.zeros((pieces[0][0].shape[0], len(pieces) * width), pieces[0][0].dtype)
+    for part, position in pieces:
         panel = lax.dynamic_update_slice_in_dim(panel, part, position * width, 1)
     return panel
-
-
-def column_panel_t(tile_t):
-    partner = chunked_shift(tile_t, "zh", [(0, 1), (1, 0)])
-    zh_id = lax.axis_index("zh")
-    ring = lax.axis_size("y")
-    panel = jnp.zeros((tile_t.shape[0], 2 * ring * tile_t.shape[1]), tile_t.dtype)
-    panel = ring_gather(tile_t, panel, zh_id)
-    return ring_gather(partner, panel, 1 - zh_id)
 
 
 def mirror_tile(upper_stored, rows, cols):
@@ -102,8 +107,13 @@
     density_full = diagonal + value_scale * symmetric.astype(jnp.float32)
     density = jnp.where(near_own, density_full, 0.0).astype(jnp.bfloat16)
     row_panel = lax.all_gather(density, COL, axis=1, tiled=True)
-    col_panel_t = column_panel_t(density.T)
-    square = jnp.where(far_own, dot_t(row_panel, col_panel_t), 0.0)
+    pieces = column_pieces_t(density.T)
+    product = None
+    for part, position in pieces:
+        term = dot_t(lax.dynamic_slice_in_dim(row_panel, position * tile_side, tile_side, 1), part)
+        product = term if product is None else product + term
+    square = jnp.where(far_own, product, 0.0)
+    col_panel_t = assemble(pieces)
     square_low = square.astype(jnp.bfloat16)
     low_panel = lax.all_gather(square_low, COL, axis=1, tiled=True)
     cubic = dot_t(low_panel, col_panel_t)

time: 194 us -> 197 us (1.015)
  matrix products: 19.4 us -> 23.9 us
  waiting for transfers between devices: 88.4 us -> 84.7 us
    all_gather x1, waiting for transfers between devices: 0.01 us -> 23 us  [per_device(): row_panel = lax.all_gather(density, COL, axis=1, tiled=True)]
    ppermute x7, waiting for transfers between devices: 28.6 us -> 8.27 us  [chunked_shift(): lax.ppermute(value[i * step:(i + 1) * step], axis, pairs)]
    all_gather x1, waiting for transfers between devices: 59.6 us -> 53.2 us  [per_device(): low_panel = lax.all_gather(square_low, COL, axis=1, tiled=True)]
    dot_general x2 -> x9, matrix products: 19.4 us -> 23.9 us  [dot_t(): lax.dot_general(left, right_t, (((1,), (1,)), ((), ())), preferred_elemen...]
  transfers between devices with their start and end apart: 11 -> 11, of which waited for: 6 -> 5; matrix products, arithmetic and copies ran while one was open for 5% -> 11% of each run, Pallas kernels for 0% -> 0%
where the time goes in v12:
time: 197 us
  waiting for transfers between devices  84.7 us (43%)
  starting transfers between devices  58 us (29%)
  matrix products  23.9 us (12%)
  local copies, waits for them, and re-layouts  14.8 us (8%)
  between operations  13.7 us (7%)
    ppermute x7, starting transfers between devices, chunked_shift(): lax.ppermute(value[i * step:(i + 1) * step], axis, pairs)  54 us
    all_gather x1, waiting for transfers between devices, per_device(): low_panel = lax.all_gather(square_low, COL, axis=1, tiled=True)  53.2 us
    dot_general x9, matrix products, dot_t(): lax.dot_general(left, right_t, (((1,), (1,)), ((), ())), preferred_elemen...  23.9 us
    all_gather x1, waiting for transfers between devices, per_device(): row_panel = lax.all_gather(density, COL, axis=1, tiled=True)  23 us
    dynamic_update_slice x7, local copies, waits for them, and re-layouts, assemble(): panel = lax.dynamic_update_slice_in_dim(panel, part, position * width, 1)  8.35 us
    ppermute x7, waiting for transfers between devices, chunked_shift(): lax.ppermute(value[i * step:(i + 1) * step], axis, pairs)  8.27 us
    ppermute x2, starting transfers between devices, mirror_tile(): pieces.append(lax.ppermute(piece, ROW + COL, pairs))  3.97 us
  transfers between devices with their start and end apart: 11, of which 5 were waited for; matrix products, arithmetic and copies ran while one was open for 11% of the time, Pallas kernels for 0%

profile of v12, /device:TPU:1, one launch (start us, length us, event | category | flops | bytes accessed | tf_op | source)
XLA Modules:
  0.0 196.7 jit_solution(7796699603238276896)
XLA Ops:
  6.5 1.1 constant_dynamic-slice_fusion.1
  7.9 0.7 collective-permute-start
  8.8 3.3 %collective-permute-start.1 = (bf16[384,384]{0,1:T(8,128)(2,1)S(1)}, bf16[384,384]{0,1:T(8,128)(2,1)S(1)}, u32[]{:S(2)}, u32[]{:S(2)}) collective-permute-start(bf16[384,384]{0,1:T(8,128)(2,1)S(1)} %copy.20), channel_id=1, source_target_pairs={{0,1},{1,0},{2,17},{3,16},{4,33},{5,32},{6,49},{7,48},{8,65},{9,64... | collective-permute-start | bytes 884744 | tf_op jit(solution)/shard_map/ppermute | solution.py:75
  12.6 0.4 copy.18
  13.4 2.6 %broadcast_in_dim.37 = bf16[384,6144]{0,1:T(8,128)(2,1)} broadcast(bf16[]{:T(256)} %constant.104.clone.1), dimensions={} | broadcast | bytes 4718594 | tf_op jit(solution)/shard_map/broadcast_in_dim | solution.py:56
  16.0 1.5 constant_dynamic-update-slice_fusion.7
  17.6 18.5 %collective-permute-start.5 = (bf16[384,768]{0,1:T(8,128)(2,1)}, bf16[384,768]{0,1:T(8,128)(2,1)S(1)}, u32[]{:S(2)}, u32[]{:S(2)}) collective-permute-start(bf16[384,768]{0,1:T(8,128)(2,1)} %bitcast.23), channel_id=1, source_target_pairs={{0,16},{16,0},{1,17},{17,1},{2,18},{18,2},{3,19},{19,3},{4,20},{20... | collective-permute-start | bytes 1769480 | tf_op jit(solution)/shard_map/ppermute | solution.py:29
  36.1 13.2 %collective-permute-start.2 = (bf16[384,768]{0,1:T(8,128)(2,1)}, bf16[384,768]{0,1:T(8,128)(2,1)S(1)}, u32[]{:S(2)}, u32[]{:S(2)}) collective-permute-start(bf16[384,768]{0,1:T(8,128)(2,1)} %bitcast.24), channel_id=1, source_target_pairs={{0,32},{32,64},{64,96},{96,0},{1,33},{33,65},{65,97},{97,1},{2,34}... | collective-permute-start | bytes 1769480 | tf_op jit(solution)/shard_map/ppermute | solution.py:29
  49.3 0.4 collective-permute-done.5
  49.6 16.8 %collective-permute-start.6 = (bf16[384,768]{0,1:T(8,128)(2,1)S(1)}, bf16[384,768]{0,1:T(8,128)(2,1)S(1)}, u32[]{:S(2)}, u32[]{:S(2)}) collective-permute-start(bf16[384,768]{0,1:T(8,128)(2,1)S(1)} %collective-permute-done.5), channel_id=1, source_target_pairs={{0,32},{32,64},{64,96},{96,0},{1,33},{33,65},{65,97},{97,1},{2,34}... | collective-permute-start | bytes 1769480 | tf_op jit(solution)/shard_map/ppermute | solution.py:29
  66.4 4.1 %collective-permute-start.3 = (bf16[384,768]{0,1:T(8,128)(2,1)}, bf16[384,768]{0,1:T(8,128)(2,1)S(1)}, u32[]{:S(2)}, u32[]{:S(2)}) collective-permute-start(bf16[384,768]{0,1:T(8,128)(2,1)} %bitcast.25), channel_id=1, source_target_pairs={{0,96},{32,0},{64,32},{96,64},{1,97},{33,1},{65,33},{97,65},{2,98}... | collective-permute-start | bytes 1769480 | tf_op jit(solution)/shard_map/ppermute | solution.py:29
  70.7 1.1 copy.17
  71.8 1.5 collective-permute-start.7
  73.3 7.9 %collective-permute-done.6 = bf16[384,768]{0,1:T(8,128)(2,1)S(1)} collective-permute-done((bf16[384,768]{0,1:T(8,128)(2,1)S(1)}, bf16[384,768]{0,1:T(8,128)(2,1)S(1)}, u32[]{:S(2)}, u32[]{:S(2)}) %collective-permute-start.6) | collective-permute-done | bytes 589856 | tf_op jit(solution)/shard_map/ppermute | solution.py:29
  81.2 23.0 %all-gather.3.cloned.1.call-done = bf16[768,6144]{1,0:T(8,128)(2,1)} async-done(((bf16[768,384]{1,0:T(8,128)(2,1)}), bf16[768,6144]{1,0:T(8,128)(2,1)}) %all-gather.3.cloned.1.call-update) | async-done | bytes 9437200 | tf_op jit(solution)/shard_map/all_gather | solution.py:109
  104.2 2.2 %fusion.12 = f32[768,384]{1,0:T(8,128)S(1)} fusion(bf16[768,384]{1,0:T(8,128)(2,1)S(1)} %copy-done.2, bf16[768,6144]{1,0:T(8,128)(2,1)} %all-gather.3.cloned.1.call-done, s32[]{:T(128)S(6)} %select_n.126), kind=kOutput, calls=%fused_computation.19 | convolution fusion | flops 452984832 | bytes 2949124 | tf_op jit(solution)/shard_map/dot_general | solution.py:83
  106.4 2.6 %convolution_add_fusion.4 = f32[768,384]{1,0:T(8,128)S(1)} fusion(f32[768,384]{1,0:T(8,128)S(1)} %fusion.12, bf16[384,768]{0,1:T(8,128)(2,1)S(1)} %collective-permute-done.2, bf16[768,6144]{1,0:T(8,128)(2,1)} %all-gather.3.cloned.1.call-done, s32[]{:T(128)S(6)} %select_n.128), kind=kOutput, calls=%fused_computation.6 | convolution fusion | flops 453279744 | bytes 4128772 | tf_op jit(solution)/shard_map/dot_general | solution.py:83
  109.0 2.1 %convolution_add_fusion.3 = f32[768,384]{1,0:T(8,128)S(1)} fusion(f32[768,384]{1,0:T(8,128)S(1)} %convolution_add_fusion.4, bf16[384,768]{0,1:T(8,128)(2,1)S(1)} %collective-permute-done.3, bf16[768,6144]{1,0:T(8,128)(2,1)} %all-gather.3.cloned.1.call-done, s32[]{:T(128)S(6)} %select_n.130), kind=kOutput, calls=%fused_computation.5 | convolution fusion | flops 453279744 | bytes 4128772 | tf_op jit(solution)/shard_map/dot_general | solution.py:83
  111.1 0.8 fusion.7
  111.9 1.8 fusion.1
  113.8 0.8 fusion.4
  114.6 0.8 fusion
  115.5 3.1 %fusion.24 = (bf16[768,384]{1,0:T(8,128)(2,1)}, f32[768,384]{1,0:T(8,128)}) fusion(pred[768,384]{1,0:T(32,128)(4,1)S(1)} %copy-done.7, f32[768,384]{1,0:T(8,128)S(1)} %fusion, bf16[384,768]{0,1:T(8,128)(2,1)} %collective-permute-done.8, bf16[768,6144]{1,0:T(8,128)(2,1)S(1)} %copy-done.1, s32[]{:T(128)S(6)} %select_n.136), kind=kOutput, calls=%fused_computation.53 | convolution fusion | flops 453869568 | bytes 5013508 | tf_op jit(solution)/shard_map/dot_general | solution.py:83
  118.6 0.9 constant_dynamic-update-slice_fusion.6
  119.5 0.9 constant_dynamic-update-slice_fusion.5
  120.4 1.9 constant_dynamic-update-slice_fusion.4
  122.3 0.9 constant_dynamic-update-slice_fusion.3
  123.2 0.9 constant_dynamic-update-slice_fusion.2
  124.1 0.9 constant_dynamic-update-slice_fusion.1
  125.0 2.0 %constant_dynamic-update-slice_fusion = bf16[384,6144]{0,1:T(8,128)(2,1)} fusion(bf16[384,6144]{0,1:T(8,128)(2,1)} %constant_dynamic-update-slice_fusion.1, bf16[384,768]{0,1:T(8,128)(2,1)} %collective-permute-done.8, s32[]{:T(128)S(6)} %select_n.136), kind=kLoop, calls=%fused_computation.29 | loop fusion | bytes 1179652 | tf_op jit(solution)/shard_map/dynamic_update_slice | solution.py:58
  126.9 53.2 %all-gather.5.cloned.1.call-done = bf16[768,6144]{1,0:T(8,128)(2,1)} async-done(((bf16[768,384]{1,0:T(8,128)(2,1)}), bf16[768,6144]{1,0:T(8,128)(2,1)}) %all-gather.5.cloned.1.call-update) | async-done | bytes 9437200 | tf_op jit(solution)/shard_map/all_gather | solution.py:118
  180.1 9.8 %select_convert_fusion = bf16[768,384]{1,0:T(8,128)(2,1)} fusion(pred[768,384]{1,0:T(32,128)(4,1)S(1)} %copy-done.5, f32[768,384]{1,0:T(8,128)S(1)} %copy-done.6, bf16[768,6144]{1,0:T(8,128)(2,1)} %all-gather.5.cloned.1.call-done, bf16[384,6144]{0,1:T(8,128)(2,1)} %constant_dynamic-update-slice_fusion), kind=kOutput, calls=%fused_computation.9 | convolution fusion | flops 3625353216 | bytes 16220160 | tf_op jit(solution)/shard_map/dot_general | solution.py:83
  (44 shorter events, 1.7 us)
Async XLA Ops:
  6.5 5.6 %copy-start = (s32[96,3]{0,1:T(4,128)S(1)}, s32[96,3]{0,1:T(4,128)}, u32[]{:S(2)}) copy-start(s32[96,3]{0,1:T(4,128)} %param.3) | copy-start | bytes 3460
  6.5 97.7 %all-gather.3.cloned.1.call-start = ((), (), s32[]{:S(2)}) async-start(), calls=%async_computation | async-start | bytes 10027008 | tf_op jit(solution)/shard_map/all_gather | solution.py:109
  7.9 5.2 %collective-permute-start = (bf16[384,384]{0,1:T(8,128)(2,1)S(1)}, bf16[384,384]{0,1:T(8,128)(2,1)S(1)}, u32[]{:S(2)}, u32[]{:S(2)}) collective-permute-start(bf16[384,384]{0,1:T(8,128)(2,1)S(1)} %copy.19), channel_id=1, source_target_pairs={{0,0},{1,1},{2,16},{3,17},{4,32},{5,33},{6,48},{7,49},{8,64},{9,65... | collective-permute-start | bytes 884744 | tf_op jit(solution)/shard_map/ppermute | solution.py:75
  8.8 4.5 %collective-permute-start.1 = (bf16[384,384]{0,1:T(8,128)(2,1)S(1)}, bf16[384,384]{0,1:T(8,128)(2,1)S(1)}, u32[]{:S(2)}, u32[]{:S(2)}) collective-permute-start(bf16[384,384]{0,1:T(8,128)(2,1)S(1)} %copy.20), channel_id=1, source_target_pairs={{0,1},{1,0},{2,17},{3,16},{4,33},{5,32},{6,49},{7,48},{8,65},{9,64... | collective-permute-start | bytes 884744 | tf_op jit(solution)/shard_map/ppermute | solution.py:75
  13.0 3.0 %copy-start.4 = (pred[768,384]{1,0:T(32,128)(4,1)}, pred[768,384]{1,0:T(32,128)(4,1)S(1)}, u32[]{:S(2)}) copy-start(pred[768,384]{1,0:T(32,128)(4,1)S(1)} %copy.18) | copy-start | bytes 884740
  13.3 2.6 %copy-start.3 = (bf16[768,384]{1,0:T(8,128)(2,1)S(1)}, bf16[768,384]{1,0:T(8,128)(2,1)}, u32[]{:S(2)}) copy-start(bf16[768,384]{1,0:T(8,128)(2,1)} %param.2) | copy-start | bytes 1769476
  17.5 86.7 %copy-start.2 = (bf16[768,384]{1,0:T(8,128)(2,1)S(1)}, bf16[768,384]{1,0:T(8,128)(2,1)}, u32[]{:S(2)}) copy-start(bf16[768,384]{1,0:T(8,128)(2,1)} %get-tuple-element.6) | copy-start | bytes 1769476
  17.5 162.6 %all-gather.5.cloned.1.call-start = ((), (), s32[]{:S(2)}) async-start(), calls=%async_computation.1 | async-start | bytes 10027008 | tf_op jit(solution)/shard_map/all_gather | solution.py:118
  17.6 32.0 %collective-permute-start.5 = (bf16[384,768]{0,1:T(8,128)(2,1)}, bf16[384,768]{0,1:T(8,128)(2,1)S(1)}, u32[]{:S(2)}, u32[]{:S(2)}) collective-permute-start(bf16[384,768]{0,1:T(8,128)(2,1)} %bitcast.23), channel_id=1, source_target_pairs={{0,16},{16,0},{1,17},{17,1},{2,18},{18,2},{3,19},{19,3},{4,20},{20... | collective-permute-start | bytes 1769480 | tf_op jit(solution)/shard_map/ppermute | solution.py:29
  36.1 37.2 %collective-permute-start.2 = (bf16[384,768]{0,1:T(8,128)(2,1)}, bf16[384,768]{0,1:T(8,128)(2,1)S(1)}, u32[]{:S(2)}, u32[]{:S(2)}) collective-permute-start(bf16[384,768]{0,1:T(8,128)(2,1)} %bitcast.24), channel_id=1, source_target_pairs={{0,32},{32,64},{64,96},{96,0},{1,33},{33,65},{65,97},{97,1},{2,34}... | collective-permute-start | bytes 1769480 | tf_op jit(solution)/shard_map/ppermute | solution.py:29
  49.6 31.6 %collective-permute-start.6 = (bf16[384,768]{0,1:T(8,128)(2,1)S(1)}, bf16[384,768]{0,1:T(8,128)(2,1)S(1)}, u32[]{:S(2)}, u32[]{:S(2)}) collective-permute-start(bf16[384,768]{0,1:T(8,128)(2,1)S(1)} %collective-permute-done.5), channel_id=1, source_target_pairs={{0,32},{32,64},{64,96},{96,0},{1,33},{33,65},{65,97},{97,1},{2,34}... | collective-permute-start | bytes 1769480 | tf_op jit(solution)/shard_map/ppermute | solution.py:29
  66.4 42.6 %collective-permute-start.3 = (bf16[384,768]{0,1:T(8,128)(2,1)}, bf16[384,768]{0,1:T(8,128)(2,1)S(1)}, u32[]{:S(2)}, u32[]{:S(2)}) collective-permute-start(bf16[384,768]{0,1:T(8,128)(2,1)} %bitcast.25), channel_id=1, source_target_pairs={{0,96},{32,0},{64,32},{96,64},{1,97},{33,1},{65,33},{97,65},{2,98}... | collective-permute-start | bytes 1769480 | tf_op jit(solution)/shard_map/ppermute | solution.py:29
  71.8 41.9 %collective-permute-start.7 = (bf16[384,768]{0,1:T(8,128)(2,1)S(1)}, bf16[384,768]{0,1:T(8,128)(2,1)S(1)}, u32[]{:S(2)}, u32[]{:S(2)}) collective-permute-start(bf16[384,768]{0,1:T(8,128)(2,1)S(1)} %collective-permute-done.5), channel_id=1, source_target_pairs={{0,96},{32,0},{64,32},{96,64},{1,97},{33,1},{65,33},{97,65},{2,98}... | collective-permute-start | bytes 1769480 | tf_op jit(solution)/shard_map/ppermute | solution.py:29
  73.3 38.6 %collective-permute-start.4 = (bf16[384,768]{0,1:T(8,128)(2,1)S(1)}, bf16[384,768]{0,1:T(8,128)(2,1)}, u32[]{:S(2)}, u32[]{:S(2)}) collective-permute-start(bf16[384,768]{0,1:T(8,128)(2,1)S(1)} %collective-permute-done.2), channel_id=1, source_target_pairs={{0,32},{32,64},{64,96},{96,0},{1,33},{33,65},{65,97},{97,1},{2,34}... | collective-permute-start | bytes 1769480 | tf_op jit(solution)/shard_map/ppermute | solution.py:29
  81.2 34.2 %collective-permute-start.8 = (bf16[384,768]{0,1:T(8,128)(2,1)S(1)}, bf16[384,768]{0,1:T(8,128)(2,1)}, u32[]{:S(2)}, u32[]{:S(2)}) collective-permute-start(bf16[384,768]{0,1:T(8,128)(2,1)S(1)} %collective-permute-done.6), channel_id=1, source_target_pairs={{0,32},{32,64},{64,96},{96,0},{1,33},{33,65},{65,97},{97,1},{2,34}... | collective-permute-start | bytes 1769480 | tf_op jit(solution)/shard_map/ppermute | solution.py:29
  104.2 6.9 %copy-start.1 = (bf16[768,6144]{1,0:T(8,128)(2,1)S(1)}, bf16[768,6144]{1,0:T(8,128)(2,1)}, u32[]{:S(2)}) copy-start(bf16[768,6144]{1,0:T(8,128)(2,1)} %all-gather.3.cloned.1.call-done) | copy-start | bytes 28311556
  114.5 1.0 copy-start.7
  124.1 56.0 %copy-start.5 = (pred[768,384]{1,0:T(32,128)(4,1)S(1)}, pred[768,384]{1,0:T(32,128)(4,1)}, u32[]{:S(2)}) copy-start(pred[768,384]{1,0:T(32,128)(4,1)} %copy-done.4) | copy-start | bytes 884740
  124.1 56.0 %copy-start.6 = (f32[768,384]{1,0:T(8,128)S(1)}, f32[768,384]{1,0:T(8,128)}, u32[]{:S(2)}) copy-start(f32[768,384]{1,0:T(8,128)} %get-tuple-element.14) | copy-start | bytes 3538948
Sparse Core Ops, SparseCore 0:
  17.7 86.4 all-gather.2
  118.7 61.3 all-gather.4

commit v13 on v10

--- a/solution.py
+++ b/solution.py
@@ -30,7 +30,7 @@
     return jnp.concatenate(parts, 0)
 
 
-def ring_gather(tile_t, panel, plane):
+def ring_gather(tile_t, panel, plane, last=None):
     ring = lax.axis_size("y")
     up = [(i, (i + 1) % ring) for i in range(ring)]
     down = [(i, (i - 1) % ring) for i in range(ring)]
@@ -41,6 +41,9 @@
     width = tile_t.shape[1]
     for offset, part in ((0, tile_t), (-1, from_below), (-2, from_two_below), (1, from_above)):
         position = ((y_id + offset) % ring) * 2 + plane
+        if offset == -2 and last is not None:
+            last.append((part, position))
+            continue
         panel = lax.dynamic_update_slice_in_dim(panel, part, position * width, 1)
     return panel
 
@@ -51,7 +54,9 @@
     ring = lax.axis_size("y")
     panel = jnp.zeros((tile_t.shape[0], 2 * ring * tile_t.shape[1]), tile_t.dtype)
     panel = ring_gather(tile_t, panel, zh_id)
-    return ring_gather(partner, panel, 1 - zh_id)
+    last = []
+    panel = ring_gather(partner, panel, 1 - zh_id, last)
+    return panel, last[0]
 
 
 def mirror_tile(upper_stored, rows, cols):
@@ -102,11 +107,16 @@
     density_full = diagonal + value_scale * symmetric.astype(jnp.float32)
     density = jnp.where(near_own, density_full, 0.0).astype(jnp.bfloat16)
     row_panel = lax.all_gather(density, COL, axis=1, tiled=True)
-    col_panel_t = column_panel_t(density.T)
-    square = jnp.where(far_own, dot_t(row_panel, col_panel_t), 0.0)
+    col_panel_t, (last_t, last_position) = column_panel_t(density.T)
+
+    def product(left):
+        left_last = lax.dynamic_slice_in_dim(left, last_position * tile_side, tile_side, 1)
+        return dot_t(left, col_panel_t) + dot_t(left_last, last_t)
+
+    square = jnp.where(far_own, product(row_panel), 0.0)
     square_low = square.astype(jnp.bfloat16)
     low_panel = lax.all_gather(square_low, COL, axis=1, tiled=True)
-    cubic = dot_t(low_panel, col_panel_t)
+    cubic = product(low_panel)
     return jnp.where(near_own, 3.0 * square - 2.0 * cubic, 0.0).astype(jnp.bfloat16)
 
 

time: 194 us -> 197 us (1.015)
  matrix products: 19.4 us -> 23.8 us
  waiting for transfers between devices: 88.4 us -> 86.2 us
    ppermute x7, waiting for transfers between devices: 28.6 us -> 20.7 us  [chunked_shift(): lax.ppermute(value[i * step:(i + 1) * step], axis, pairs)]
    dot_general x2 -> x4, matrix products: 19.4 us -> 23.8 us  [dot_t(): lax.dot_general(left, right_t, (((1,), (1,)), ((), ())), preferred_elemen...]
    all_gather x1, waiting for transfers between devices: 0.01 us -> 3.65 us  [per_device(): row_panel = lax.all_gather(density, COL, axis=1, tiled=True)]
    dynamic_update_slice x7 -> x6, local copies, waits for them, and re-layouts: 7.3 us -> 7.47 us  [ring_gather(): panel = lax.dynamic_update_slice_in_dim(panel, part, position * width, 1)]
  transfers between devices with their start and end apart: 11 -> 11, of which waited for: 6 -> 6; matrix products, arithmetic and copies ran while one was open for 5% -> 9% of each run, Pallas kernels for 0% -> 0%
where the time goes in v13:
time: 197 us
  waiting for transfers between devices  86.2 us (44%)
  starting transfers between devices  58.1 us (29%)
  matrix products  23.8 us (12%)
  between operations  13.6 us (7%)
  local copies, waits for them, and re-layouts  13.1 us (7%)
    all_gather x1, waiting for transfers between devices, per_device(): low_panel = lax.all_gather(square_low, COL, axis=1, tiled=True)  61.5 us
    ppermute x7, starting transfers between devices, chunked_shift(): lax.ppermute(value[i * step:(i + 1) * step], axis, pairs)  54.1 us
    dot_general x4, matrix products, dot_t(): lax.dot_general(left, right_t, (((1,), (1,)), ((), ())), preferred_elemen...  23.8 us
    ppermute x7, waiting for transfers between devices, chunked_shift(): lax.ppermute(value[i * step:(i + 1) * step], axis, pairs)  20.7 us
    dynamic_update_slice x6, local copies, waits for them, and re-layouts, ring_gather(): panel = lax.dynamic_update_slice_in_dim(panel, part, position * width, 1)  7.47 us
    ppermute x2, starting transfers between devices, mirror_tile(): pieces.append(lax.ppermute(piece, ROW + COL, pairs))  3.97 us
  transfers between devices with their start and end apart: 11, of which 6 were waited for; matrix products, arithmetic and copies ran while one was open for 9% of the time, Pallas kernels for 0%

profile of v13, /device:TPU:1, one launch (start us, length us, event | category | flops | bytes accessed | tf_op | source)
XLA Modules:
  0.0 196.5 jit_solution(1252832593554019384)
XLA Ops:
  6.5 1.2 constant_dynamic-slice_fusion.1
  7.7 0.2 copy.19
  7.9 0.7 collective-permute-start
  8.6 0.2 copy.20
  8.8 3.3 %collective-permute-start.1 = (bf16[384,384]{0,1:T(8,128)(2,1)S(1)}, bf16[384,384]{0,1:T(8,128)(2,1)S(1)}, u32[]{:S(2)}, u32[]{:S(2)}) collective-permute-start(bf16[384,384]{0,1:T(8,128)(2,1)S(1)} %copy.20), channel_id=1, source_target_pairs={{0,1},{1,0},{2,17},{3,16},{4,33},{5,32},{6,49},{7,48},{8,65},{9,64... | collective-permute-start | bytes 884744 | tf_op jit(solution)/shard_map/ppermute | solution.py:75
  12.5 0.1 reshape.14
  12.7 0.4 copy.18
  13.1 0.2 collective-permute-done.1
  13.4 2.7 %broadcast_in_dim.37 = bf16[384,6144]{0,1:T(8,128)(2,1)} broadcast(bf16[]{:T(256)} %constant.98.clone.1), dimensions={} | broadcast | bytes 4718594 | tf_op jit(solution)/shard_map/broadcast_in_dim | solution.py:55
  16.1 1.5 constant_dynamic-update-slice_fusion.6
  17.7 18.5 %collective-permute-start.5 = (bf16[384,768]{0,1:T(8,128)(2,1)}, bf16[384,768]{0,1:T(8,128)(2,1)S(1)}, u32[]{:S(2)}, u32[]{:S(2)}) collective-permute-start(bf16[384,768]{0,1:T(8,128)(2,1)} %bitcast.19), channel_id=1, source_target_pairs={{0,16},{16,0},{1,17},{17,1},{2,18},{18,2},{3,19},{19,3},{4,20},{20... | collective-permute-start | bytes 1769480 | tf_op jit(solution)/shard_map/ppermute | solution.py:29
  36.1 13.2 %collective-permute-start.2 = (bf16[384,768]{0,1:T(8,128)(2,1)}, bf16[384,768]{0,1:T(8,128)(2,1)S(1)}, u32[]{:S(2)}, u32[]{:S(2)}) collective-permute-start(bf16[384,768]{0,1:T(8,128)(2,1)} %bitcast.20), channel_id=1, source_target_pairs={{0,32},{32,64},{64,96},{96,0},{1,33},{33,65},{65,97},{97,1},{2,34}... | collective-permute-start | bytes 1769480 | tf_op jit(solution)/shard_map/ppermute | solution.py:29
  49.3 0.4 collective-permute-done.5
  49.7 16.7 %collective-permute-start.6 = (bf16[384,768]{0,1:T(8,128)(2,1)S(1)}, bf16[384,768]{0,1:T(8,128)(2,1)S(1)}, u32[]{:S(2)}, u32[]{:S(2)}) collective-permute-start(bf16[384,768]{0,1:T(8,128)(2,1)S(1)} %collective-permute-done.5), channel_id=1, source_target_pairs={{0,32},{32,64},{64,96},{96,0},{1,33},{33,65},{65,97},{97,1},{2,34}... | collective-permute-start | bytes 1769480 | tf_op jit(solution)/shard_map/ppermute | solution.py:29
  66.4 2.0 %collective-permute-start.3 = (bf16[384,768]{0,1:T(8,128)(2,1)S(1)}, bf16[384,768]{0,1:T(8,128)(2,1)}, u32[]{:S(2)}, u32[]{:S(2)}) collective-permute-start(bf16[384,768]{0,1:T(8,128)(2,1)S(1)} %collective-permute-done.2), channel_id=1, source_target_pairs={{0,32},{32,64},{64,96},{96,0},{1,33},{33,65},{65,97},{97,1},{2,34}... | collective-permute-start | bytes 1769480 | tf_op jit(solution)/shard_map/ppermute | solution.py:29
  68.4 2.2 %collective-permute-start.4 = (bf16[384,768]{0,1:T(8,128)(2,1)}, bf16[384,768]{0,1:T(8,128)(2,1)}, u32[]{:S(2)}, u32[]{:S(2)}) collective-permute-start(bf16[384,768]{0,1:T(8,128)(2,1)} %bitcast.21), channel_id=1, source_target_pairs={{0,96},{32,0},{64,32},{96,64},{1,97},{33,1},{65,33},{97,65},{2,98}... | collective-permute-start | bytes 1769480 | tf_op jit(solution)/shard_map/ppermute | solution.py:29
  70.9 0.4 copy.17
  71.3 1.5 collective-permute-start.7
  72.8 0.9 constant_dynamic-update-slice_fusion.5
  73.7 7.6 %collective-permute-done.6 = bf16[384,768]{0,1:T(8,128)(2,1)S(1)} collective-permute-done((bf16[384,768]{0,1:T(8,128)(2,1)S(1)}, bf16[384,768]{0,1:T(8,128)(2,1)S(1)}, u32[]{:S(2)}, u32[]{:S(2)}) %collective-permute-start.6) | collective-permute-done | bytes 589856 | tf_op jit(solution)/shard_map/ppermute | solution.py:29
  81.3 12.7 %collective-permute-done.3 = bf16[384,768]{0,1:T(8,128)(2,1)} collective-permute-done((bf16[384,768]{0,1:T(8,128)(2,1)S(1)}, bf16[384,768]{0,1:T(8,128)(2,1)}, u32[]{:S(2)}, u32[]{:S(2)}) %collective-permute-start.3) | collective-permute-done | bytes 589856 | tf_op jit(solution)/shard_map/ppermute | solution.py:29
  94.0 1.9 constant_dynamic-update-slice_fusion.4
  96.0 2.0 constant_dynamic-update-slice_fusion.3
  97.9 0.9 constant_dynamic-update-slice_fusion.2
  98.8 0.9 constant_dynamic-update-slice_fusion.1
  99.7 0.9 constant_dynamic-update-slice_fusion
  100.6 3.7 %all-gather.3.cloned.1.call-done = bf16[768,6144]{1,0:T(8,128)(2,1)} async-done(((bf16[768,384]{1,0:T(8,128)(2,1)}), bf16[768,6144]{1,0:T(8,128)(2,1)}) %all-gather.3.cloned.1.call-update) | async-done | bytes 9437200 | tf_op jit(solution)/shard_map/all_gather | solution.py:109
  104.3 9.0 %fusion.12 = f32[768,384]{1,0:T(8,128)S(1)} fusion(bf16[768,6144]{1,0:T(8,128)(2,1)} %all-gather.3.cloned.1.call-done, bf16[384,6144]{0,1:T(8,128)(2,1)} %constant_dynamic-update-slice_fusion), kind=kOutput, calls=%fused_computation.35 | convolution fusion | flops 3623878656 | bytes 15335424 | tf_op jit(solution)/shard_map/dot_general | solution.py:83
  113.3 2.9 %fusion.11 = (bf16[768,384]{1,0:T(8,128)(2,1)}, f32[768,384]{1,0:T(8,128)S(1)}) fusion(pred[768,384]{1,0:T(32,128)(4,1)S(1)} %copy.17, f32[768,384]{1,0:T(8,128)S(1)} %fusion.12, bf16[384,768]{0,1:T(8,128)(2,1)S(1)} %collective-permute-done.8, bf16[768,6144]{1,0:T(8,128)(2,1)} %all-gather.3.cloned.1.call-done, s32[]{:T(128)S(6)} %select_n.129), kind=kOutput, calls=%fused_computation.34 | convolution fusion | flops 453869568 | bytes 5013508 | tf_op jit(solution)/shard_map/dot_general | solution.py:83
  116.2 61.5 %all-gather.5.cloned.1.call-done = bf16[768,6144]{1,0:T(8,128)(2,1)} async-done(((bf16[768,384]{1,0:T(8,128)(2,1)}), bf16[768,6144]{1,0:T(8,128)(2,1)}) %all-gather.5.cloned.1.call-update) | async-done | bytes 9437200 | tf_op jit(solution)/shard_map/all_gather | solution.py:118
  177.7 9.0 %fusion.13 = f32[768,384]{1,0:T(8,128)S(1)} fusion(bf16[768,6144]{1,0:T(8,128)(2,1)} %all-gather.5.cloned.1.call-done, bf16[384,6144]{0,1:T(8,128)(2,1)} %constant_dynamic-update-slice_fusion), kind=kOutput, calls=%fused_computation.36 | convolution fusion | flops 3623878656 | bytes 15335424 | tf_op jit(solution)/shard_map/dot_general | solution.py:83
  186.7 3.0 %fusion.4 = bf16[768,384]{1,0:T(8,128)(2,1)} fusion(pred[768,384]{1,0:T(32,128)(4,1)S(1)} %copy.18, f32[768,384]{1,0:T(8,128)S(1)} %fusion.13, bf16[384,768]{0,1:T(8,128)(2,1)S(1)} %collective-permute-done.8, bf16[768,6144]{1,0:T(8,128)(2,1)} %all-gather.5.cloned.1.call-done, s32[]{:T(128)S(6)} %select_n.129, f32[768,384]{1,0:T(8,128)S(1)} %get-tuple-element.14), kind=kOutput, calls=%fused_computation.6 | convolution fusion | flops 454754304 | bytes 5013508 | tf_op jit(solution)/shard_map/dot_general | solution.py:83
  (26 shorter events, 0.8 us)
Async XLA Ops:
  6.5 5.6 %copy-start = (s32[96,3]{0,1:T(4,128)S(1)}, s32[96,3]{0,1:T(4,128)}, u32[]{:S(2)}) copy-start(s32[96,3]{0,1:T(4,128)} %param.3) | copy-start | bytes 3460
  6.5 9.5 %copy-start.1 = (bf16[768,384]{1,0:T(8,128)(2,1)S(1)}, bf16[768,384]{1,0:T(8,128)(2,1)}, u32[]{:S(2)}) copy-start(bf16[768,384]{1,0:T(8,128)(2,1)} %param.2) | copy-start | bytes 1769476
  6.5 97.7 %all-gather.3.cloned.1.call-start = ((), (), s32[]{:S(2)}) async-start(), calls=%async_computation | async-start | bytes 10027008 | tf_op jit(solution)/shard_map/all_gather | solution.py:109
  7.9 5.2 %collective-permute-start = (bf16[384,384]{0,1:T(8,128)(2,1)S(1)}, bf16[384,384]{0,1:T(8,128)(2,1)S(1)}, u32[]{:S(2)}, u32[]{:S(2)}) collective-permute-start(bf16[384,384]{0,1:T(8,128)(2,1)S(1)} %copy.19), channel_id=1, source_target_pairs={{0,0},{1,1},{2,16},{3,17},{4,32},{5,33},{6,48},{7,49},{8,64},{9,65... | collective-permute-start | bytes 884744 | tf_op jit(solution)/shard_map/ppermute | solution.py:75
  8.8 4.5 %collective-permute-start.1 = (bf16[384,384]{0,1:T(8,128)(2,1)S(1)}, bf16[384,384]{0,1:T(8,128)(2,1)S(1)}, u32[]{:S(2)}, u32[]{:S(2)}) collective-permute-start(bf16[384,384]{0,1:T(8,128)(2,1)S(1)} %copy.20), channel_id=1, source_target_pairs={{0,1},{1,0},{2,17},{3,16},{4,33},{5,32},{6,49},{7,48},{8,65},{9,64... | collective-permute-start | bytes 884744 | tf_op jit(solution)/shard_map/ppermute | solution.py:75
  17.6 160.1 %all-gather.5.cloned.1.call-start = ((), (), s32[]{:S(2)}) async-start(), calls=%async_computation.1 | async-start | bytes 10027008 | tf_op jit(solution)/shard_map/all_gather | solution.py:118
  17.7 32.0 %collective-permute-start.5 = (bf16[384,768]{0,1:T(8,128)(2,1)}, bf16[384,768]{0,1:T(8,128)(2,1)S(1)}, u32[]{:S(2)}, u32[]{:S(2)}) collective-permute-start(bf16[384,768]{0,1:T(8,128)(2,1)} %bitcast.19), channel_id=1, source_target_pairs={{0,16},{16,0},{1,17},{17,1},{2,18},{18,2},{3,19},{19,3},{4,20},{20... | collective-permute-start | bytes 1769480 | tf_op jit(solution)/shard_map/ppermute | solution.py:29
  36.1 30.3 %collective-permute-start.2 = (bf16[384,768]{0,1:T(8,128)(2,1)}, bf16[384,768]{0,1:T(8,128)(2,1)S(1)}, u32[]{:S(2)}, u32[]{:S(2)}) collective-permute-start(bf16[384,768]{0,1:T(8,128)(2,1)} %bitcast.20), channel_id=1, source_target_pairs={{0,32},{32,64},{64,96},{96,0},{1,33},{33,65},{65,97},{97,1},{2,34}... | collective-permute-start | bytes 1769480 | tf_op jit(solution)/shard_map/ppermute | solution.py:29
  49.7 31.6 %collective-permute-start.6 = (bf16[384,768]{0,1:T(8,128)(2,1)S(1)}, bf16[384,768]{0,1:T(8,128)(2,1)S(1)}, u32[]{:S(2)}, u32[]{:S(2)}) collective-permute-start(bf16[384,768]{0,1:T(8,128)(2,1)S(1)} %collective-permute-done.5), channel_id=1, source_target_pairs={{0,32},{32,64},{64,96},{96,0},{1,33},{33,65},{65,97},{97,1},{2,34}... | collective-permute-start | bytes 1769480 | tf_op jit(solution)/shard_map/ppermute | solution.py:29
  66.4 27.6 %collective-permute-start.3 = (bf16[384,768]{0,1:T(8,128)(2,1)S(1)}, bf16[384,768]{0,1:T(8,128)(2,1)}, u32[]{:S(2)}, u32[]{:S(2)}) collective-permute-start(bf16[384,768]{0,1:T(8,128)(2,1)S(1)} %collective-permute-done.2), channel_id=1, source_target_pairs={{0,32},{32,64},{64,96},{96,0},{1,33},{33,65},{65,97},{97,1},{2,34}... | collective-permute-start | bytes 1769480 | tf_op jit(solution)/shard_map/ppermute | solution.py:29
  68.4 27.5 %collective-permute-start.4 = (bf16[384,768]{0,1:T(8,128)(2,1)}, bf16[384,768]{0,1:T(8,128)(2,1)}, u32[]{:S(2)}, u32[]{:S(2)}) collective-permute-start(bf16[384,768]{0,1:T(8,128)(2,1)} %bitcast.21), channel_id=1, source_target_pairs={{0,96},{32,0},{64,32},{96,64},{1,97},{33,1},{65,33},{97,65},{2,98}... | collective-permute-start | bytes 1769480 | tf_op jit(solution)/shard_map/ppermute | solution.py:29
  71.3 28.4 %collective-permute-start.7 = (bf16[384,768]{0,1:T(8,128)(2,1)S(1)}, bf16[384,768]{0,1:T(8,128)(2,1)S(1)}, u32[]{:S(2)}, u32[]{:S(2)}) collective-permute-start(bf16[384,768]{0,1:T(8,128)(2,1)S(1)} %collective-permute-done.5), channel_id=1, source_target_pairs={{0,96},{32,0},{64,32},{96,64},{1,97},{33,1},{65,33},{97,65},{2,98}... | collective-permute-start | bytes 1769480 | tf_op jit(solution)/shard_map/ppermute | solution.py:29
  81.3 32.0 %collective-permute-start.8 = (bf16[384,768]{0,1:T(8,128)(2,1)S(1)}, bf16[384,768]{0,1:T(8,128)(2,1)S(1)}, u32[]{:S(2)}, u32[]{:S(2)}) collective-permute-start(bf16[384,768]{0,1:T(8,128)(2,1)S(1)} %collective-permute-done.6), channel_id=1, source_target_pairs={{0,32},{32,64},{64,96},{96,0},{1,33},{33,65},{65,97},{97,1},{2,34}... | collective-permute-start | bytes 1769480 | tf_op jit(solution)/shard_map/ppermute | solution.py:29
Sparse Core Ops, SparseCore 0:
  17.7 86.4 all-gather.2
  116.3 61.3 all-gather.4

commit v14 on v6

--- a/solution.py
+++ b/solution.py
@@ -55,21 +55,20 @@
 
 
 def mirror_tile(upper_stored, rows, cols):
-    tile_side, half_width = upper_stored.shape
+    half_width = upper_stored.shape[1]
     col_id = lax.axis_index(COL)
-    pieces = []
-    for k in range(2):
-        half = (col_id + k) % 2
-        piece = lax.dynamic_slice_in_dim(upper_stored, half * half_width, half_width, 0)
-        pairs = []
-        for a in range(rows):
-            for b in range(cols):
-                h = (b + k) % 2
-                pairs.append((a * cols + b, (b // 2) * cols + 2 * a + h))
-        pieces.append(lax.ppermute(piece, ROW + COL, pairs))
     h_own = col_id % 2
-    first = jnp.where(h_own == 0, pieces[0], pieces[1])
-    second = jnp.where(h_own == 0, pieces[1], pieces[0])
+    pairs = []
+    for a in range(rows):
+        for b in range(cols):
+            if a <= b // 2:
+                pairs.append((a * cols + b, (b // 2) * cols + 2 * a + b % 2))
+    received = lax.ppermute(upper_stored, ROW + COL, pairs)
+    keep = lax.dynamic_slice_in_dim(received, h_own * half_width, half_width, 0)
+    give = lax.dynamic_slice_in_dim(received, (1 - h_own) * half_width, half_width, 0)
+    got = lax.ppermute(give, "core", [(0, 1), (1, 0)])
+    first = jnp.where(h_own == 0, keep, got)
+    second = jnp.where(h_own == 0, got, keep)
     return jnp.concatenate([first, second], 1).T
 
 

time: 196 us -> 197 us (level)
  starting transfers between devices: 54.6 us -> 59.7 us
  waiting for transfers between devices: 93.6 us -> 89.3 us
    ppermute x7, starting transfers between devices: 52.4 us -> 57.5 us  [chunked_shift(): lax.ppermute(value[i * step:(i + 1) * step], axis, pairs)]
    ppermute x7, waiting for transfers between devices: 31.3 us -> 28.8 us  [chunked_shift(): lax.ppermute(value[i * step:(i + 1) * step], axis, pairs)]
    all_gather x1, waiting for transfers between devices: 62 us -> 59.9 us  [per_device(): low_panel = lax.all_gather(square_low, COL, axis=1, tiled=True)]
where the time goes in v14:
time: 197 us
  waiting for transfers between devices  89.3 us (45%)
  starting transfers between devices  59.7 us (30%)
  matrix products  19.4 us (10%)
  between operations  13.6 us (7%)
  local copies, waits for them, and re-layouts  12.8 us (6%)
    all_gather x1, waiting for transfers between devices, per_device(): low_panel = lax.all_gather(square_low, COL, axis=1, tiled=True)  59.9 us
    ppermute x7, starting transfers between devices, chunked_shift(): lax.ppermute(value[i * step:(i + 1) * step], axis, pairs)  57.5 us
    ppermute x7, waiting for transfers between devices, chunked_shift(): lax.ppermute(value[i * step:(i + 1) * step], axis, pairs)  28.8 us
    dot_general x2, matrix products, dot_t(): lax.dot_general(left, right_t, (((1,), (1,)), ((), ())), preferred_elemen...  19.4 us
    dynamic_update_slice x7, local copies, waits for them, and re-layouts, ring_gather(): panel = lax.dynamic_update_slice_in_dim(panel, part, position * width, 1)  7.35 us
  transfers between devices with their start and end apart: 11, of which 6 were waited for; matrix products, arithmetic and copies ran while one was open for 5% of the time, Pallas kernels for 0%

profile of v14, /device:TPU:1, one launch (start us, length us, event | category | flops | bytes accessed | tf_op | source)
XLA Modules:
  0.0 196.6 jit_solution(6274785615004182780)
XLA Ops:
  6.5 1.4 copy.12
  7.9 0.7 collective-permute-start
  8.8 0.1 fusion.1
  8.9 1.5 collective-permute-start.1
  10.5 0.1 reshape.14
  10.7 0.4 copy.15
  11.1 0.5 collective-permute-done.1
  11.6 0.1 broadcast_select_fusion.1
  11.8 2.7 %broadcast_in_dim.37 = bf16[384,6144]{0,1:T(8,128)(2,1)} broadcast(bf16[]{:T(256)} %constant.92.clone.1), dimensions={} | broadcast | bytes 4718594 | tf_op jit(solution)/shard_map/broadcast_in_dim | solution.py:52
  14.4 1.5 constant_dynamic-update-slice_fusion.7
  16.0 22.2 %collective-permute-start.5 = (bf16[384,768]{0,1:T(8,128)(2,1)}, bf16[384,768]{0,1:T(8,128)(2,1)S(1)}, u32[]{:S(2)}, u32[]{:S(2)}) collective-permute-start(bf16[384,768]{0,1:T(8,128)(2,1)} %bitcast.17), channel_id=1, source_target_pairs={{0,16},{16,0},{1,17},{17,1},{2,18},{18,2},{3,19},{19,3},{4,20},{20... | collective-permute-start | bytes 1769480 | tf_op jit(solution)/shard_map/ppermute | solution.py:29
  38.2 13.0 %collective-permute-start.2 = (bf16[384,768]{0,1:T(8,128)(2,1)}, bf16[384,768]{0,1:T(8,128)(2,1)S(1)}, u32[]{:S(2)}, u32[]{:S(2)}) collective-permute-start(bf16[384,768]{0,1:T(8,128)(2,1)} %bitcast.18), channel_id=1, source_target_pairs={{0,32},{32,64},{64,96},{96,0},{1,33},{33,65},{65,97},{97,1},{2,34}... | collective-permute-start | bytes 1769480 | tf_op jit(solution)/shard_map/ppermute | solution.py:29
  51.2 0.5 collective-permute-done.5
  51.8 16.6 %collective-permute-start.6 = (bf16[384,768]{0,1:T(8,128)(2,1)S(1)}, bf16[384,768]{0,1:T(8,128)(2,1)S(1)}, u32[]{:S(2)}, u32[]{:S(2)}) collective-permute-start(bf16[384,768]{0,1:T(8,128)(2,1)S(1)} %collective-permute-done.5), channel_id=1, source_target_pairs={{0,32},{32,64},{64,96},{96,0},{1,33},{33,65},{65,97},{97,1},{2,34}... | collective-permute-start | bytes 1769480 | tf_op jit(solution)/shard_map/ppermute | solution.py:29
  68.4 0.6 collective-permute-start.3
  69.0 3.6 %collective-permute-start.4 = (bf16[384,768]{0,1:T(8,128)(2,1)}, bf16[384,768]{0,1:T(8,128)(2,1)S(1)}, u32[]{:S(2)}, u32[]{:S(2)}) collective-permute-start(bf16[384,768]{0,1:T(8,128)(2,1)} %bitcast.19), channel_id=1, source_target_pairs={{0,96},{32,0},{64,32},{96,64},{1,97},{33,1},{65,33},{97,65},{2,98}... | collective-permute-start | bytes 1769480 | tf_op jit(solution)/shard_map/ppermute | solution.py:29
  72.7 0.1 reshape.16
  72.8 0.4 copy.14
  73.3 1.5 collective-permute-start.8
  74.7 8.5 %collective-permute-done.6 = bf16[384,768]{0,1:T(8,128)(2,1)S(1)} collective-permute-done((bf16[384,768]{0,1:T(8,128)(2,1)S(1)}, bf16[384,768]{0,1:T(8,128)(2,1)S(1)}, u32[]{:S(2)}, u32[]{:S(2)}) %collective-permute-start.6) | collective-permute-done | bytes 589856 | tf_op jit(solution)/shard_map/ppermute | solution.py:29
  83.3 0.9 constant_dynamic-update-slice_fusion.6
  84.2 11.8 %collective-permute-done.3 = bf16[384,768]{0,1:T(8,128)(2,1)} collective-permute-done((bf16[384,768]{0,1:T(8,128)(2,1)S(1)}, bf16[384,768]{0,1:T(8,128)(2,1)}, u32[]{:S(2)}, u32[]{:S(2)}) %collective-permute-start.3) | collective-permute-done | bytes 589856 | tf_op jit(solution)/shard_map/ppermute | solution.py:29
  96.0 2.0 constant_dynamic-update-slice_fusion.5
  98.0 0.9 constant_dynamic-update-slice_fusion.4
  98.9 0.9 constant_dynamic-update-slice_fusion.3
  99.8 0.9 constant_dynamic-update-slice_fusion.2
  100.7 7.9 %collective-permute-done.7 = bf16[384,768]{0,1:T(8,128)(2,1)S(1)} collective-permute-done((bf16[384,768]{0,1:T(8,128)(2,1)S(1)}, bf16[384,768]{0,1:T(8,128)(2,1)S(1)}, u32[]{:S(2)}, u32[]{:S(2)}) %collective-permute-start.7) | collective-permute-done | bytes 589856 | tf_op jit(solution)/shard_map/ppermute | solution.py:29
  108.6 0.9 constant_dynamic-update-slice_fusion.1
  109.5 0.9 constant_dynamic-update-slice_fusion
  110.3 9.7 %fusion.2 = (bf16[768,384]{1,0:T(8,128)(2,1)}, f32[768,384]{1,0:T(8,128)S(1)}) fusion(pred[768,384]{1,0:T(32,128)(4,1)S(1)} %copy.14, bf16[768,6144]{1,0:T(8,128)(2,1)} %all-gather.3.cloned.1.call-done, bf16[384,6144]{0,1:T(8,128)(2,1)} %constant_dynamic-update-slice_fusion), kind=kOutput, calls=%fused_computation.26 | convolution fusion | flops 3624468480 | bytes 16220160 | tf_op jit(solution)/shard_map/dot_general | solution.py:76
  120.1 59.9 %all-gather.5.cloned.1.call-done = bf16[768,6144]{1,0:T(8,128)(2,1)} async-done(((bf16[768,384]{1,0:T(8,128)(2,1)}), bf16[768,6144]{1,0:T(8,128)(2,1)}) %all-gather.5.cloned.1.call-update) | async-done | bytes 9437200 | tf_op jit(solution)/shard_map/all_gather | solution.py:106
  180.0 9.8 %select_convert_fusion = bf16[768,384]{1,0:T(8,128)(2,1)} fusion(pred[768,384]{1,0:T(32,128)(4,1)S(1)} %copy.15, f32[768,384]{1,0:T(8,128)S(1)} %get-tuple-element.12, bf16[768,6144]{1,0:T(8,128)(2,1)} %all-gather.5.cloned.1.call-done, bf16[384,6144]{0,1:T(8,128)(2,1)} %constant_dynamic-update-slice_fusion), kind=kOutput, calls=%fused_computation.2 | convolution fusion | flops 3625353216 | bytes 16220160 | tf_op jit(solution)/shard_map/dot_general | solution.py:76
  (24 shorter events, 0.6 us)
Async XLA Ops:
  6.5 2.1 %copy-start = (s32[96,3]{0,1:T(4,128)S(1)}, s32[96,3]{0,1:T(4,128)}, u32[]{:S(2)}) copy-start(s32[96,3]{0,1:T(4,128)} %param.3) | copy-start | bytes 3460
  6.5 7.9 %copy-start.1 = (bf16[768,384]{1,0:T(8,128)(2,1)S(1)}, bf16[768,384]{1,0:T(8,128)(2,1)}, u32[]{:S(2)}) copy-start(bf16[768,384]{1,0:T(8,128)(2,1)} %param.2) | copy-start | bytes 1769476
  6.5 103.8 %all-gather.3.cloned.1.call-start = ((), (), s32[]{:S(2)}) async-start(), calls=%async_computation | async-start | bytes 10027008 | tf_op jit(solution)/shard_map/all_gather | solution.py:102
  7.9 1.0 collective-permute-start
  8.9 2.7 %collective-permute-start.1 = (bf16[384,384]{0,1:T(8,128)(2,1)S(1)}, bf16[384,384]{0,1:T(8,128)(2,1)S(1)}, u32[]{:S(2)}, u32[]{:S(2)}) collective-permute-start(bf16[384,384]{0,1:T(8,128)(2,1)S(1)} %constant_dynamic-slice_fusion), channel_id=1, source_target_pairs={{0,1},{1,0},{2,3},{3,2},{4,5},{5,4},{6,7},{7,6},{8,9},{9,8},{10,11... | collective-permute-start | bytes 884744 | tf_op jit(solution)/shard_map/ppermute | solution.py:69
  16.0 164.0 %all-gather.5.cloned.1.call-start = ((), (), s32[]{:S(2)}) async-start(), calls=%async_computation.1 | async-start | bytes 10027008 | tf_op jit(solution)/shard_map/all_gather | solution.py:106
  16.0 35.7 %collective-permute-start.5 = (bf16[384,768]{0,1:T(8,128)(2,1)}, bf16[384,768]{0,1:T(8,128)(2,1)S(1)}, u32[]{:S(2)}, u32[]{:S(2)}) collective-permute-start(bf16[384,768]{0,1:T(8,128)(2,1)} %bitcast.17), channel_id=1, source_target_pairs={{0,16},{16,0},{1,17},{17,1},{2,18},{18,2},{3,19},{19,3},{4,20},{20... | collective-permute-start | bytes 1769480 | tf_op jit(solution)/shard_map/ppermute | solution.py:29
  38.2 30.1 %collective-permute-start.2 = (bf16[384,768]{0,1:T(8,128)(2,1)}, bf16[384,768]{0,1:T(8,128)(2,1)S(1)}, u32[]{:S(2)}, u32[]{:S(2)}) collective-permute-start(bf16[384,768]{0,1:T(8,128)(2,1)} %bitcast.18), channel_id=1, source_target_pairs={{0,32},{32,64},{64,96},{96,0},{1,33},{33,65},{65,97},{97,1},{2,34}... | collective-permute-start | bytes 1769480 | tf_op jit(solution)/shard_map/ppermute | solution.py:29
  51.8 31.5 %collective-permute-start.6 = (bf16[384,768]{0,1:T(8,128)(2,1)S(1)}, bf16[384,768]{0,1:T(8,128)(2,1)S(1)}, u32[]{:S(2)}, u32[]{:S(2)}) collective-permute-start(bf16[384,768]{0,1:T(8,128)(2,1)S(1)} %collective-permute-done.5), channel_id=1, source_target_pairs={{0,32},{32,64},{64,96},{96,0},{1,33},{33,65},{65,97},{97,1},{2,34}... | collective-permute-start | bytes 1769480 | tf_op jit(solution)/shard_map/ppermute | solution.py:29
  68.4 27.7 %collective-permute-start.3 = (bf16[384,768]{0,1:T(8,128)(2,1)S(1)}, bf16[384,768]{0,1:T(8,128)(2,1)}, u32[]{:S(2)}, u32[]{:S(2)}) collective-permute-start(bf16[384,768]{0,1:T(8,128)(2,1)S(1)} %collective-permute-done.2), channel_id=1, source_target_pairs={{0,32},{32,64},{64,96},{96,0},{1,33},{33,65},{65,97},{97,1},{2,34}... | collective-permute-start | bytes 1769480 | tf_op jit(solution)/shard_map/ppermute | solution.py:29
  69.0 29.0 %collective-permute-start.4 = (bf16[384,768]{0,1:T(8,128)(2,1)}, bf16[384,768]{0,1:T(8,128)(2,1)S(1)}, u32[]{:S(2)}, u32[]{:S(2)}) collective-permute-start(bf16[384,768]{0,1:T(8,128)(2,1)} %bitcast.19), channel_id=1, source_target_pairs={{0,96},{32,0},{64,32},{96,64},{1,97},{33,1},{65,33},{97,65},{2,98}... | collective-permute-start | bytes 1769480 | tf_op jit(solution)/shard_map/ppermute | solution.py:29
  73.3 36.2 %collective-permute-start.8 = (bf16[384,768]{0,1:T(8,128)(2,1)S(1)}, bf16[384,768]{0,1:T(8,128)(2,1)S(1)}, u32[]{:S(2)}, u32[]{:S(2)}) collective-permute-start(bf16[384,768]{0,1:T(8,128)(2,1)S(1)} %collective-permute-done.5), channel_id=1, source_target_pairs={{0,96},{32,0},{64,32},{96,64},{1,97},{33,1},{65,33},{97,65},{2,98}... | collective-permute-start | bytes 1769480 | tf_op jit(solution)/shard_map/ppermute | solution.py:29
  83.3 25.3 %collective-permute-start.7 = (bf16[384,768]{0,1:T(8,128)(2,1)S(1)}, bf16[384,768]{0,1:T(8,128)(2,1)S(1)}, u32[]{:S(2)}, u32[]{:S(2)}) collective-permute-start(bf16[384,768]{0,1:T(8,128)(2,1)S(1)} %collective-permute-done.6), channel_id=1, source_target_pairs={{0,32},{32,64},{64,96},{96,0},{1,33},{33,65},{65,97},{97,1},{2,34}... | collective-permute-start | bytes 1769480 | tf_op jit(solution)/shard_map/ppermute | solution.py:29
Sparse Core Ops, SparseCore 0:
  16.1 91.0 all-gather.2
  120.2 59.7 all-gather.4

commit v15 on v11

--- a/solution.py
+++ b/solution.py
@@ -6,13 +6,13 @@
 from jax.sharding import Mesh
 from jax.sharding import PartitionSpec as P
 
+
 BLK = 64
 BOX = 16
 NEAR = 40
 FAR = 90
 ROW = ("y", "zh")
 COL = ("zl", "x", "core")
-CHUNKS = 1
 
 
 def cell_mask(block_cells, row_start, row_count, col_start, col_count, bound_sq):
@@ -24,34 +24,29 @@
     return jnp.repeat(jnp.repeat(keep, BLK, axis=0), BLK, axis=1)
 
 
-def chunked_shift(value, axis, pairs):
-    step = value.shape[0] // CHUNKS
-    parts = [lax.ppermute(value[i * step:(i + 1) * step], axis, pairs) for i in range(CHUNKS)]
-    return jnp.concatenate(parts, 0)
-
-
 def column_panel_t(tile_t):
     ring = lax.axis_size("y")
     y_id = lax.axis_index("y")
     zh_id = lax.axis_index("zh")
     width = tile_t.shape[1]
     panel = jnp.zeros((tile_t.shape[0], 2 * ring * width), tile_t.dtype)
-    panel = lax.dynamic_update_slice_in_dim(panel, tile_t, (y_id * 2 + zh_id) * width, 1)
-    for dy in range(ring):
-        for dz in range(2):
-            if dy == 0 and dz == 0:
-                continue
-            pairs = [
-                (y * 2 + z, ((y + dy) % ring) * 2 + (z ^ dz)) for y in range(ring) for z in range(2)
-            ]
-            part = lax.ppermute(tile_t, ROW, pairs)
-            source = ((y_id - dy) % ring) * 2 + (zh_id ^ dz)
-            panel = lax.dynamic_update_slice_in_dim(panel, part, source * width, 1)
-    return panel
+
+    def send(value, dy, dz):
+        pairs = [(y * 2 + z, ((y + dy) % ring) * 2 + (z ^ dz)) for y in range(ring) for z in range(2)]
+        return lax.ppermute(value, ROW, pairs)
+
+    partner = send(tile_t, 0, 1)
+    received = [(1, 0, send(tile_t, 1, 0)), (-1, 0, send(tile_t, -1, 0)), (2, 0, send(tile_t, 2, 0)),
+                (2, 1, send(tile_t, 2, 1)), (0, 1, partner)]
+    received += [(1, 1, send(partner, 1, 0)), (-1, 1, send(partner, -1, 0))]
+    for dy, dz, part in received:
+        source = ((y_id - dy) % ring) * 2 + (zh_id ^ dz)
+        panel = lax.dynamic_update_slice_in_dim(panel, part, source * width, 1)
+    return lax.dynamic_update_slice_in_dim(panel, tile_t, (y_id * 2 + zh_id) * width, 1)
 
 
 def mirror_tile(upper_stored, rows, cols):
-    tile_side, half_width = upper_stored.shape
+    _, half_width = upper_stored.shape
     col_id = lax.axis_index(COL)
     pieces = []
     for k in range(2):
@@ -74,7 +69,7 @@
     return lax.dot_general(left, right_t, (((1,), (1,)), ((), ())), preferred_element_type=jnp.float32)
 
 
-def per_device(upper_stored, block_cells):
+def per_device_body(upper_stored, block_cells):
     rows = lax.axis_size(ROW)
     cols = lax.axis_size(COL)
     row_id = lax.axis_index(ROW)
@@ -111,7 +106,7 @@
     x_size = mesh.devices.shape[1] // 4
     split_mesh = Mesh(mesh.devices.reshape(y_size, 2, 2, x_size, 2), ROW + COL)
     return jax.shard_map(
-        per_device,
+        per_device_body,
         mesh=split_mesh,
         in_specs=(P(ROW, COL), P()),
         out_specs=P(ROW, COL),

time: 234 us -> 202 us (0.86)
  starting transfers between devices: 84.9 us -> 56.2 us
  waiting for transfers between devices: 101 us -> 97.2 us
    ppermute x7, starting transfers between devices: 80.9 us -> 52.1 us  [send(): return lax.ppermute(value, ROW, pairs)]
    all_gather x2, waiting for transfers between devices: 80.2 us -> 70.7 us  [the longest x1 61.5 us: per_device_body(): low_panel = lax.all_gather(square_low, COL, axis=1, tiled=True)]
    ppermute x7, waiting for transfers between devices: 20.5 us -> 26.2 us  [send(): return lax.ppermute(value, ROW, pairs)]
  transfers between devices with their start and end apart: 11 -> 11, of which waited for: 6 -> 6; matrix products, arithmetic and copies ran while one was open for 4% -> 6% of each run, Pallas kernels for 0% -> 0%
where the time goes in v15:
time: 202 us
  waiting for transfers between devices  97.2 us (48%)
  starting transfers between devices  56.2 us (28%)
  matrix products  19.4 us (10%)
  local copies, waits for them, and re-layouts  14 us (7%)
  between operations  13.6 us (7%)
    all_gather x1, waiting for transfers between devices, per_device_body(): low_panel = lax.all_gather(square_low, COL, axis=1, tiled=True)  61.5 us
    ppermute x7, starting transfers between devices, send(): return lax.ppermute(value, ROW, pairs)  52.1 us
    ppermute x7, waiting for transfers between devices, send(): return lax.ppermute(value, ROW, pairs)  26.2 us
    dot_general x2, matrix products, dot_t(): lax.dot_general(left, right_t, (((1,), (1,)), ((), ())), preferred_elemen...  19.4 us
    all_gather x1, waiting for transfers between devices, per_device_body(): row_panel = lax.all_gather(density, COL, axis=1, tiled=True)  9.22 us
    dynamic_update_slice x7, local copies, waits for them, and re-layouts, column_panel_t(): panel = lax.dynamic_update_slice_in_dim(panel, part, source * width, 1)  7.44 us
  transfers between devices with their start and end apart: 11, of which 6 were waited for; matrix products, arithmetic and copies ran while one was open for 6% of the time, Pallas kernels for 0%

profile of v15, /device:TPU:1, one launch (start us, length us, event | category | flops | bytes accessed | tf_op | source)
XLA Modules:
  0.0 201.9 jit_solution(3002609308852099784)
XLA Ops:
  6.5 1.2 constant_dynamic-slice_fusion.1
  7.7 0.2 copy.19
  7.9 0.7 collective-permute-start
  8.6 0.2 copy.20
  8.9 3.3 %collective-permute-start.1 = (bf16[384,384]{0,1:T(8,128)(2,1)S(1)}, bf16[384,384]{0,1:T(8,128)(2,1)S(1)}, u32[]{:S(2)}, u32[]{:S(2)}) collective-permute-start(bf16[384,384]{0,1:T(8,128)(2,1)S(1)} %copy.20), channel_id=1, source_target_pairs={{0,1},{1,0},{2,17},{3,16},{4,33},{5,32},{6,49},{7,48},{8,65},{9,64... | collective-permute-start | bytes 884744 | tf_op jit(solution)/shard_map/ppermute | solution.py:61
  12.7 0.4 copy.18
  13.1 0.2 collective-permute-done.1
  13.4 1.3 select_convert_fusion.1
  14.8 18.4 %collective-permute-start.6 = (bf16[384,768]{0,1:T(8,128)(2,1)}, bf16[384,768]{0,1:T(8,128)(2,1)S(1)}, u32[]{:S(2)}, u32[]{:S(2)}) collective-permute-start(bf16[384,768]{0,1:T(8,128)(2,1)} %bitcast.16), channel_id=1, source_target_pairs={{0,16},{16,0},{32,48},{48,32},{64,80},{80,64},{96,112},{112,96},{1... | collective-permute-start | bytes 1769480 | tf_op jit(solution)/shard_map/ppermute | solution.py:36
  33.3 13.2 %collective-permute-start.2 = (bf16[384,768]{0,1:T(8,128)(2,1)}, bf16[384,768]{0,1:T(8,128)(2,1)}, u32[]{:S(2)}, u32[]{:S(2)}) collective-permute-start(bf16[384,768]{0,1:T(8,128)(2,1)} %bitcast.17), channel_id=1, source_target_pairs={{0,32},{16,48},{32,64},{48,80},{64,96},{80,112},{96,0},{112,16},{1... | collective-permute-start | bytes 1769480 | tf_op jit(solution)/shard_map/ppermute | solution.py:36
  46.5 2.7 %collective-permute-start.3 = (bf16[384,768]{0,1:T(8,128)(2,1)}, bf16[384,768]{0,1:T(8,128)(2,1)S(1)}, u32[]{:S(2)}, u32[]{:S(2)}) collective-permute-start(bf16[384,768]{0,1:T(8,128)(2,1)} %bitcast.18), channel_id=1, source_target_pairs={{0,96},{16,112},{32,0},{48,16},{64,32},{80,48},{96,64},{112,80},{1... | collective-permute-start | bytes 1769480 | tf_op jit(solution)/shard_map/ppermute | solution.py:36
  49.1 1.2 collective-permute-start.4
  50.3 1.7 collective-permute-start.5
  52.3 0.4 copy.17
  52.7 10.9 %collective-permute-start.7 = (bf16[384,768]{0,1:T(8,128)(2,1)S(1)}, bf16[384,768]{0,1:T(8,128)(2,1)S(1)}, u32[]{:S(2)}, u32[]{:S(2)}) collective-permute-start(bf16[384,768]{0,1:T(8,128)(2,1)S(1)} %collective-permute-done.6), channel_id=1, source_target_pairs={{0,32},{16,48},{32,64},{48,80},{64,96},{80,112},{96,0},{112,16},{1... | collective-permute-start | bytes 1769480 | tf_op jit(solution)/shard_map/ppermute | solution.py:36
  63.6 4.0 %collective-permute-start.8 = (bf16[384,768]{0,1:T(8,128)(2,1)S(1)}, bf16[384,768]{0,1:T(8,128)(2,1)S(1)}, u32[]{:S(2)}, u32[]{:S(2)}) collective-permute-start(bf16[384,768]{0,1:T(8,128)(2,1)S(1)} %collective-permute-done.6), channel_id=1, source_target_pairs={{0,96},{16,112},{32,0},{48,16},{64,32},{80,48},{96,64},{112,80},{1... | collective-permute-start | bytes 1769480 | tf_op jit(solution)/shard_map/ppermute | solution.py:36
  67.7 2.7 %broadcast_in_dim.37 = bf16[384,6144]{0,1:T(8,128)(2,1)} broadcast(bf16[]{:T(256)} %constant.98.clone.1), dimensions={} | broadcast | bytes 4718594 | tf_op jit(solution)/shard_map/broadcast_in_dim | solution.py:32
  70.3 2.1 %constant_dynamic-update-slice_fusion.7 = bf16[384,6144]{0,1:T(8,128)(2,1)} fusion(bf16[384,6144]{0,1:T(8,128)(2,1)} %broadcast_in_dim.37, bf16[384,768]{0,1:T(8,128)(2,1)} %collective-permute-done.2, s32[]{:T(128)S(6)} %select_n.116), kind=kLoop, calls=%fused_computation.19 | loop fusion | bytes 1179652 | tf_op jit(solution)/shard_map/dynamic_update_slice | solution.py:44
  72.4 0.9 constant_dynamic-update-slice_fusion.6
  73.3 2.6 %collective-permute-done.4 = bf16[384,768]{0,1:T(8,128)(2,1)S(1)} collective-permute-done((bf16[384,768]{0,1:T(8,128)(2,1)}, bf16[384,768]{0,1:T(8,128)(2,1)S(1)}, u32[]{:S(2)}, u32[]{:S(2)}) %collective-permute-start.4) | collective-permute-done | bytes 589856 | tf_op jit(solution)/shard_map/ppermute | solution.py:36
  76.0 0.9 constant_dynamic-update-slice_fusion.5
  76.8 11.9 %collective-permute-done.5 = bf16[384,768]{0,1:T(8,128)(2,1)S(1)} collective-permute-done((bf16[384,768]{0,1:T(8,128)(2,1)}, bf16[384,768]{0,1:T(8,128)(2,1)S(1)}, u32[]{:S(2)}, u32[]{:S(2)}) %collective-permute-start.5) | collective-permute-done | bytes 589856 | tf_op jit(solution)/shard_map/ppermute | solution.py:36
  88.7 0.9 constant_dynamic-update-slice_fusion.4
  89.6 0.9 constant_dynamic-update-slice_fusion.3
  90.5 11.7 %collective-permute-done.7 = bf16[384,768]{0,1:T(8,128)(2,1)S(1)} collective-permute-done((bf16[384,768]{0,1:T(8,128)(2,1)S(1)}, bf16[384,768]{0,1:T(8,128)(2,1)S(1)}, u32[]{:S(2)}, u32[]{:S(2)}) %collective-permute-start.7) | collective-permute-done | bytes 589856 | tf_op jit(solution)/shard_map/ppermute | solution.py:36
  102.2 0.9 constant_dynamic-update-slice_fusion.2
  103.1 0.9 constant_dynamic-update-slice_fusion.1
  104.0 0.9 constant_dynamic-update-slice_fusion
  104.9 9.2 %all-gather.3.cloned.1.call-done = bf16[768,6144]{1,0:T(8,128)(2,1)} async-done(((bf16[768,384]{1,0:T(8,128)(2,1)}), bf16[768,6144]{1,0:T(8,128)(2,1)}) %all-gather.3.cloned.1.call-update) | async-done | bytes 9437200 | tf_op jit(solution)/shard_map/all_gather | solution.py:95
  114.1 9.7 %fusion.2 = (bf16[768,384]{1,0:T(8,128)(2,1)}, f32[768,384]{1,0:T(8,128)S(1)}) fusion(pred[768,384]{1,0:T(32,128)(4,1)S(1)} %copy.17, bf16[768,6144]{1,0:T(8,128)(2,1)} %all-gather.3.cloned.1.call-done, bf16[384,6144]{0,1:T(8,128)(2,1)} %constant_dynamic-update-slice_fusion), kind=kOutput, calls=%fused_computation.27 | convolution fusion | flops 3624468480 | bytes 16220160 | tf_op jit(solution)/shard_map/dot_general | solution.py:69
  123.8 61.5 %all-gather.5.cloned.1.call-done = bf16[768,6144]{1,0:T(8,128)(2,1)} async-done(((bf16[768,384]{1,0:T(8,128)(2,1)}), bf16[768,6144]{1,0:T(8,128)(2,1)}) %all-gather.5.cloned.1.call-update) | async-done | bytes 9437200 | tf_op jit(solution)/shard_map/all_gather | solution.py:99
  185.3 9.7 %select_convert_fusion = bf16[768,384]{1,0:T(8,128)(2,1)} fusion(pred[768,384]{1,0:T(32,128)(4,1)S(1)} %copy.18, f32[768,384]{1,0:T(8,128)S(1)} %get-tuple-element.12, bf16[768,6144]{1,0:T(8,128)(2,1)} %all-gather.5.cloned.1.call-done, bf16[384,6144]{0,1:T(8,128)(2,1)} %constant_dynamic-update-slice_fusion), kind=kOutput, calls=%fused_computation.2 | convolution fusion | flops 3625353216 | bytes 16220160 | tf_op jit(solution)/shard_map/dot_general | solution.py:69
  (28 shorter events, 0.9 us)
Async XLA Ops:
  6.5 5.6 %copy-start = (s32[96,3]{0,1:T(4,128)S(1)}, s32[96,3]{0,1:T(4,128)}, u32[]{:S(2)}) copy-start(s32[96,3]{0,1:T(4,128)} %param.3) | copy-start | bytes 3460
  6.5 6.9 %copy-start.2 = (bf16[768,384]{1,0:T(8,128)(2,1)S(1)}, bf16[768,384]{1,0:T(8,128)(2,1)}, u32[]{:S(2)}) copy-start(bf16[768,384]{1,0:T(8,128)(2,1)} %param.2) | copy-start | bytes 1769476
  6.5 107.6 %all-gather.3.cloned.1.call-start = ((), (), s32[]{:S(2)}) async-start(), calls=%async_computation | async-start | bytes 10027008 | tf_op jit(solution)/shard_map/all_gather | solution.py:95
  7.9 5.2 %collective-permute-start = (bf16[384,384]{0,1:T(8,128)(2,1)S(1)}, bf16[384,384]{0,1:T(8,128)(2,1)S(1)}, u32[]{:S(2)}, u32[]{:S(2)}) collective-permute-start(bf16[384,384]{0,1:T(8,128)(2,1)S(1)} %copy.19), channel_id=1, source_target_pairs={{0,0},{1,1},{2,16},{3,17},{4,32},{5,33},{6,48},{7,49},{8,64},{9,65... | collective-permute-start | bytes 884744 | tf_op jit(solution)/shard_map/ppermute | solution.py:61
  8.9 4.5 %collective-permute-start.1 = (bf16[384,384]{0,1:T(8,128)(2,1)S(1)}, bf16[384,384]{0,1:T(8,128)(2,1)S(1)}, u32[]{:S(2)}, u32[]{:S(2)}) collective-permute-start(bf16[384,384]{0,1:T(8,128)(2,1)S(1)} %copy.20), channel_id=1, source_target_pairs={{0,1},{1,0},{2,17},{3,16},{4,33},{5,32},{6,49},{7,48},{8,65},{9,64... | collective-permute-start | bytes 884744 | tf_op jit(solution)/shard_map/ppermute | solution.py:61
  14.8 170.5 %all-gather.5.cloned.1.call-start = ((), (), s32[]{:S(2)}) async-start(), calls=%async_computation.1 | async-start | bytes 10027008 | tf_op jit(solution)/shard_map/all_gather | solution.py:99
  14.8 37.9 %collective-permute-start.6 = (bf16[384,768]{0,1:T(8,128)(2,1)}, bf16[384,768]{0,1:T(8,128)(2,1)S(1)}, u32[]{:S(2)}, u32[]{:S(2)}) collective-permute-start(bf16[384,768]{0,1:T(8,128)(2,1)} %bitcast.16), channel_id=1, source_target_pairs={{0,16},{16,0},{32,48},{48,32},{64,80},{80,64},{96,112},{112,96},{1... | collective-permute-start | bytes 1769480 | tf_op jit(solution)/shard_map/ppermute | solution.py:36
  33.3 30.4 %collective-permute-start.2 = (bf16[384,768]{0,1:T(8,128)(2,1)}, bf16[384,768]{0,1:T(8,128)(2,1)}, u32[]{:S(2)}, u32[]{:S(2)}) collective-permute-start(bf16[384,768]{0,1:T(8,128)(2,1)} %bitcast.17), channel_id=1, source_target_pairs={{0,32},{16,48},{32,64},{48,80},{64,96},{80,112},{96,0},{112,16},{1... | collective-permute-start | bytes 1769480 | tf_op jit(solution)/shard_map/ppermute | solution.py:36
  46.5 25.9 %collective-permute-start.3 = (bf16[384,768]{0,1:T(8,128)(2,1)}, bf16[384,768]{0,1:T(8,128)(2,1)S(1)}, u32[]{:S(2)}, u32[]{:S(2)}) collective-permute-start(bf16[384,768]{0,1:T(8,128)(2,1)} %bitcast.18), channel_id=1, source_target_pairs={{0,96},{16,112},{32,0},{48,16},{64,32},{80,48},{96,64},{112,80},{1... | collective-permute-start | bytes 1769480 | tf_op jit(solution)/shard_map/ppermute | solution.py:36
  49.1 26.8 %collective-permute-start.4 = (bf16[384,768]{0,1:T(8,128)(2,1)}, bf16[384,768]{0,1:T(8,128)(2,1)S(1)}, u32[]{:S(2)}, u32[]{:S(2)}) collective-permute-start(bf16[384,768]{0,1:T(8,128)(2,1)} %bitcast.19), channel_id=1, source_target_pairs={{0,64},{16,80},{32,96},{48,112},{64,0},{80,16},{96,32},{112,48},{1... | collective-permute-start | bytes 1769480 | tf_op jit(solution)/shard_map/ppermute | solution.py:36
  50.3 38.4 %collective-permute-start.5 = (bf16[384,768]{0,1:T(8,128)(2,1)}, bf16[384,768]{0,1:T(8,128)(2,1)S(1)}, u32[]{:S(2)}, u32[]{:S(2)}) collective-permute-start(bf16[384,768]{0,1:T(8,128)(2,1)} %bitcast.20), channel_id=1, source_target_pairs={{0,80},{16,64},{32,112},{48,96},{64,16},{80,0},{96,48},{112,32},{1... | collective-permute-start | bytes 1769480 | tf_op jit(solution)/shard_map/ppermute | solution.py:36
  52.7 49.5 %collective-permute-start.7 = (bf16[384,768]{0,1:T(8,128)(2,1)S(1)}, bf16[384,768]{0,1:T(8,128)(2,1)S(1)}, u32[]{:S(2)}, u32[]{:S(2)}) collective-permute-start(bf16[384,768]{0,1:T(8,128)(2,1)S(1)} %collective-permute-done.6), channel_id=1, source_target_pairs={{0,32},{16,48},{32,64},{48,80},{64,96},{80,112},{96,0},{112,16},{1... | collective-permute-start | bytes 1769480 | tf_op jit(solution)/shard_map/ppermute | solution.py:36
  63.6 39.5 %collective-permute-start.8 = (bf16[384,768]{0,1:T(8,128)(2,1)S(1)}, bf16[384,768]{0,1:T(8,128)(2,1)S(1)}, u32[]{:S(2)}, u32[]{:S(2)}) collective-permute-start(bf16[384,768]{0,1:T(8,128)(2,1)S(1)} %collective-permute-done.6), channel_id=1, source_target_pairs={{0,96},{16,112},{32,0},{48,16},{64,32},{80,48},{96,64},{112,80},{1... | collective-permute-start | bytes 1769480 | tf_op jit(solution)/shard_map/ppermute | solution.py:36
  70.3 33.7 %copy-start.1 = (bf16[768,384]{1,0:T(8,128)(2,1)S(1)}, bf16[768,384]{1,0:T(8,128)(2,1)}, u32[]{:S(2)}) copy-start(bf16[768,384]{1,0:T(8,128)(2,1)} %select_convert_fusion.1) | copy-start | bytes 1769476
Sparse Core Ops, SparseCore 0:
  14.9 99.1 all-gather.2
  124.0 61.3 all-gather.4

commit v16 on v10

--- a/solution.py
+++ b/solution.py
@@ -5,6 +5,7 @@
 from jax import lax
 from jax.sharding import Mesh
 from jax.sharding import PartitionSpec as P
+
 
 BLK = 64
 BOX = 16
@@ -55,7 +56,7 @@
 
 
 def mirror_tile(upper_stored, rows, cols):
-    tile_side, half_width = upper_stored.shape
+    _, half_width = upper_stored.shape
     col_id = lax.axis_index(COL)
     pieces = []
     for k in range(2):
@@ -74,11 +75,21 @@
     return jnp.concatenate([first, second], 1).T
 
 
+GATHER_ORDER = ("core", "zl", "x")
+
+
+def to_gather_order(panel_t, block):
+    rows, width = panel_t.shape
+    x_size = width // (4 * block)
+    shaped = panel_t.reshape(rows, 2, x_size, 2, block)
+    return shaped.transpose(0, 3, 1, 2, 4).reshape(rows, width)
+
+
 def dot_t(left, right_t):
     return lax.dot_general(left, right_t, (((1,), (1,)), ((), ())), preferred_element_type=jnp.float32)
 
 
-def per_device(upper_stored, block_cells):
+def per_device_body(upper_stored, block_cells):
     rows = lax.axis_size(ROW)
     cols = lax.axis_size(COL)
     row_id = lax.axis_index(ROW)
@@ -101,11 +112,12 @@
     value_scale = 2.0 / math.sqrt(order_total)
     density_full = diagonal + value_scale * symmetric.astype(jnp.float32)
     density = jnp.where(near_own, density_full, 0.0).astype(jnp.bfloat16)
-    row_panel = lax.all_gather(density, COL, axis=1, tiled=True)
+    row_panel = lax.all_gather(density, GATHER_ORDER, axis=1, tiled=True)
     col_panel_t = column_panel_t(density.T)
+    col_panel_t = to_gather_order(col_panel_t, half_width)
     square = jnp.where(far_own, dot_t(row_panel, col_panel_t), 0.0)
     square_low = square.astype(jnp.bfloat16)
-    low_panel = lax.all_gather(square_low, COL, axis=1, tiled=True)
+    low_panel = lax.all_gather(square_low, GATHER_ORDER, axis=1, tiled=True)
     cubic = dot_t(low_panel, col_panel_t)
     return jnp.where(near_own, 3.0 * square - 2.0 * cubic, 0.0).astype(jnp.bfloat16)
 
@@ -115,7 +127,7 @@
     x_size = mesh.devices.shape[1] // 4
     split_mesh = Mesh(mesh.devices.reshape(y_size, 2, 2, x_size, 2), ROW + COL)
     return jax.shard_map(
-        per_device,
+        per_device_body,
         mesh=split_mesh,
         in_specs=(P(ROW, COL), P()),
         out_specs=P(ROW, COL),

time: 194 us -> 200 us (1.031)
  local copies, waits for them, and re-layouts: 13 us -> 17 us
    transpose x0 -> x1, local copies, waits for them, and re-layouts: none -> 5.2 us  [to_gather_order(): return shaped.transpose(0, 3, 1, 2, 4).reshape(rows, width)]
  transfers between devices with their start and end apart: 11 -> 11, of which waited for: 6 -> 6; matrix products, arithmetic and copies ran while one was open for 5% -> 7% of each run, Pallas kernels for 0% -> 0%
where the time goes in v16:
time: 200 us; the launch traced here: 199 us
  waiting for transfers between devices  89.4 us (45%)
  starting transfers between devices  58.1 us (29%)
  matrix products  19.4 us (10%)
  local copies, waits for them, and re-layouts  17 us (8%)
  between operations  13.6 us (7%)
    all_gather x1, waiting for transfers between devices, per_device_body(): low_panel = lax.all_gather(square_low, GATHER_ORDER, axis=1, tiled=True)  59.6 us
    ppermute x7, starting transfers between devices, chunked_shift(): lax.ppermute(value[i * step:(i + 1) * step], axis, pairs)  54.1 us
    ppermute x7, waiting for transfers between devices, chunked_shift(): lax.ppermute(value[i * step:(i + 1) * step], axis, pairs)  29.6 us
    dot_general x2, matrix products, dot_t(): lax.dot_general(left, right_t, (((1,), (1,)), ((), ())), preferred_elemen...  19.4 us
    dynamic_update_slice x7, local copies, waits for them, and re-layouts, ring_gather(): panel = lax.dynamic_update_slice_in_dim(panel, part, position * width, 1)  6.22 us
    transpose x1, local copies, waits for them, and re-layouts, to_gather_order(): return shaped.transpose(0, 3, 1, 2, 4).reshape(rows, width)  5.2 us
  transfers between devices with their start and end apart: 11, of which 6 were waited for; matrix products, arithmetic and copies ran while one was open for 7% of the time, Pallas kernels for 0%

profile of v16, /device:TPU:1, one launch (start us, length us, event | category | flops | bytes accessed | tf_op | source)
XLA Modules:
  0.0 199.3 jit_solution(5989740823324944301)
XLA Ops:
  6.5 1.2 constant_dynamic-slice_fusion.1
  7.7 0.2 copy.28
  7.9 0.7 collective-permute-start
  8.6 0.2 copy.29
  8.9 3.3 %collective-permute-start.1 = (bf16[384,384]{0,1:T(8,128)(2,1)S(1)}, bf16[384,384]{0,1:T(8,128)(2,1)S(1)}, u32[]{:S(2)}, u32[]{:S(2)}) collective-permute-start(bf16[384,384]{0,1:T(8,128)(2,1)S(1)} %copy.29), channel_id=1, source_target_pairs={{0,1},{1,0},{2,17},{3,16},{4,33},{5,32},{6,49},{7,48},{8,65},{9,64... | collective-permute-start | bytes 884744 | tf_op jit(solution)/shard_map/ppermute | solution.py:71
  12.5 0.1 reshape.20
  12.7 0.4 copy.27
  13.1 0.2 collective-permute-done.1
  13.4 2.5 %broadcast_in_dim.37 = bf16[384,6144]{0,1:T(8,128)(2,1)} broadcast(bf16[]{:T(256)} %constant.98.clone.1), dimensions={} | broadcast | bytes 4718594 | tf_op jit(solution)/shard_map/broadcast_in_dim | solution.py:53
  15.9 1.6 constant_dynamic-update-slice_fusion.7
  17.6 18.4 %collective-permute-start.5 = (bf16[384,768]{0,1:T(8,128)(2,1)}, bf16[384,768]{0,1:T(8,128)(2,1)S(1)}, u32[]{:S(2)}, u32[]{:S(2)}) collective-permute-start(bf16[384,768]{0,1:T(8,128)(2,1)} %bitcast.23), channel_id=1, source_target_pairs={{0,16},{16,0},{1,17},{17,1},{2,18},{18,2},{3,19},{19,3},{4,20},{20... | collective-permute-start | bytes 1769480 | tf_op jit(solution)/shard_map/ppermute | solution.py:30
  36.0 13.2 %collective-permute-start.2 = (bf16[384,768]{0,1:T(8,128)(2,1)}, bf16[384,768]{0,1:T(8,128)(2,1)S(1)}, u32[]{:S(2)}, u32[]{:S(2)}) collective-permute-start(bf16[384,768]{0,1:T(8,128)(2,1)} %bitcast.24), channel_id=1, source_target_pairs={{0,32},{32,64},{64,96},{96,0},{1,33},{33,65},{65,97},{97,1},{2,34}... | collective-permute-start | bytes 1769480 | tf_op jit(solution)/shard_map/ppermute | solution.py:30
  49.2 0.3 collective-permute-done.5
  49.6 16.8 %collective-permute-start.6 = (bf16[384,768]{0,1:T(8,128)(2,1)S(1)}, bf16[384,768]{0,1:T(8,128)(2,1)S(1)}, u32[]{:S(2)}, u32[]{:S(2)}) collective-permute-start(bf16[384,768]{0,1:T(8,128)(2,1)S(1)} %collective-permute-done.5), channel_id=1, source_target_pairs={{0,32},{32,64},{64,96},{96,0},{1,33},{33,65},{65,97},{97,1},{2,34}... | collective-permute-start | bytes 1769480 | tf_op jit(solution)/shard_map/ppermute | solution.py:30
  66.4 2.0 %collective-permute-start.3 = (bf16[384,768]{0,1:T(8,128)(2,1)S(1)}, bf16[384,768]{0,1:T(8,128)(2,1)S(1)}, u32[]{:S(2)}, u32[]{:S(2)}) collective-permute-start(bf16[384,768]{0,1:T(8,128)(2,1)S(1)} %collective-permute-done.2), channel_id=1, source_target_pairs={{0,32},{32,64},{64,96},{96,0},{1,33},{33,65},{65,97},{97,1},{2,34}... | collective-permute-start | bytes 1769480 | tf_op jit(solution)/shard_map/ppermute | solution.py:30
  68.4 2.1 %collective-permute-start.4 = (bf16[384,768]{0,1:T(8,128)(2,1)}, bf16[384,768]{0,1:T(8,128)(2,1)S(1)}, u32[]{:S(2)}, u32[]{:S(2)}) collective-permute-start(bf16[384,768]{0,1:T(8,128)(2,1)} %bitcast.25), channel_id=1, source_target_pairs={{0,96},{32,0},{64,32},{96,64},{1,97},{33,1},{65,33},{97,65},{2,98}... | collective-permute-start | bytes 1769480 | tf_op jit(solution)/shard_map/ppermute | solution.py:30
  70.8 0.4 copy.26
  71.2 1.5 collective-permute-start.8
  72.7 8.5 %collective-permute-done.6 = bf16[384,768]{0,1:T(8,128)(2,1)S(1)} collective-permute-done((bf16[384,768]{0,1:T(8,128)(2,1)S(1)}, bf16[384,768]{0,1:T(8,128)(2,1)S(1)}, u32[]{:S(2)}, u32[]{:S(2)}) %collective-permute-start.6) | collective-permute-done | bytes 589856 | tf_op jit(solution)/shard_map/ppermute | solution.py:30
  81.2 0.9 constant_dynamic-update-slice_fusion.6
  82.1 11.7 %collective-permute-done.3 = bf16[384,768]{0,1:T(8,128)(2,1)S(1)} collective-permute-done((bf16[384,768]{0,1:T(8,128)(2,1)S(1)}, bf16[384,768]{0,1:T(8,128)(2,1)S(1)}, u32[]{:S(2)}, u32[]{:S(2)}) %collective-permute-start.3) | collective-permute-done | bytes 589856 | tf_op jit(solution)/shard_map/ppermute | solution.py:30
  93.8 0.9 constant_dynamic-update-slice_fusion.5
  94.7 0.9 constant_dynamic-update-slice_fusion.4
  95.6 0.9 constant_dynamic-update-slice_fusion.3
  96.5 0.9 constant_dynamic-update-slice_fusion.2
  97.4 9.1 %collective-permute-done.7 = bf16[384,768]{0,1:T(8,128)(2,1)S(1)} collective-permute-done((bf16[384,768]{0,1:T(8,128)(2,1)S(1)}, bf16[384,768]{0,1:T(8,128)(2,1)S(1)}, u32[]{:S(2)}, u32[]{:S(2)}) %collective-permute-start.7) | collective-permute-done | bytes 589856 | tf_op jit(solution)/shard_map/ppermute | solution.py:30
  106.5 0.9 constant_dynamic-update-slice_fusion.1
  107.3 0.9 constant_dynamic-update-slice_fusion
  108.2 5.2 %copy.25 = bf16[384,2,2,4,384]{0,4,3,2,1:T(8,128)(2,1)} copy(bf16[384,2,2,4,384]{0,4,1,3,2:T(8,128)(2,1)} %bitcast.5) | data formatting | bytes 9437184 | tf_op jit(solution)/shard_map/transpose | solution.py:85
  113.4 9.7 %fusion.5 = (bf16[768,384]{1,0:T(8,128)(2,1)}, f32[768,384]{1,0:T(8,128)S(1)}) fusion(pred[768,384]{1,0:T(32,128)(4,1)S(1)} %copy.26, bf16[768,6144]{1,0:T(8,128)(2,1)} %all-gather.3.cloned.1.call-done, bf16[384,6144]{0,1:T(8,128)(2,1)} %bitcast.21), kind=kOutput, calls=%fused_computation.29 | convolution fusion | flops 3624468480 | bytes 16220160 | tf_op jit(solution)/shard_map/dot_general | solution.py:89
  123.2 59.6 %all-gather.5.cloned.1.call-done = bf16[768,6144]{1,0:T(8,128)(2,1)} async-done(((bf16[768,384]{1,0:T(8,128)(2,1)}), bf16[768,6144]{1,0:T(8,128)(2,1)}) %all-gather.5.cloned.1.call-update) | async-done | bytes 9437200 | tf_op jit(solution)/shard_map/all_gather | solution.py:120
  182.7 9.7 %fusion.2 = bf16[768,384]{1,0:T(8,128)(2,1)} fusion(pred[768,384]{1,0:T(32,128)(4,1)S(1)} %copy.27, bf16[768,6144]{1,0:T(8,128)(2,1)} %all-gather.5.cloned.1.call-done, bf16[384,6144]{0,1:T(8,128)(2,1)} %bitcast.22, f32[768,384]{1,0:T(8,128)S(1)} %get-tuple-element.14), kind=kOutput, calls=%fused_computation.4 | convolution fusion | flops 3625353216 | bytes 16220160 | tf_op jit(solution)/shard_map/dot_general | solution.py:89
  (26 shorter events, 0.8 us)
Async XLA Ops:
  6.5 5.6 %copy-start = (s32[96,3]{0,1:T(4,128)S(1)}, s32[96,3]{0,1:T(4,128)}, u32[]{:S(2)}) copy-start(s32[96,3]{0,1:T(4,128)} %param.3) | copy-start | bytes 3460
  6.5 9.4 %copy-start.1 = (bf16[768,384]{1,0:T(8,128)(2,1)S(1)}, bf16[768,384]{1,0:T(8,128)(2,1)}, u32[]{:S(2)}) copy-start(bf16[768,384]{1,0:T(8,128)(2,1)} %param.2) | copy-start | bytes 1769476
  6.5 106.9 %all-gather.3.cloned.1.call-start = ((), (), s32[]{:S(2)}) async-start(), calls=%async_computation | async-start | bytes 10027008 | tf_op jit(solution)/shard_map/all_gather | solution.py:115
  7.9 5.2 %collective-permute-start = (bf16[384,384]{0,1:T(8,128)(2,1)S(1)}, bf16[384,384]{0,1:T(8,128)(2,1)S(1)}, u32[]{:S(2)}, u32[]{:S(2)}) collective-permute-start(bf16[384,384]{0,1:T(8,128)(2,1)S(1)} %copy.28), channel_id=1, source_target_pairs={{0,0},{1,1},{2,16},{3,17},{4,32},{5,33},{6,48},{7,49},{8,64},{9,65... | collective-permute-start | bytes 884744 | tf_op jit(solution)/shard_map/ppermute | solution.py:71
  8.9 4.5 %collective-permute-start.1 = (bf16[384,384]{0,1:T(8,128)(2,1)S(1)}, bf16[384,384]{0,1:T(8,128)(2,1)S(1)}, u32[]{:S(2)}, u32[]{:S(2)}) collective-permute-start(bf16[384,384]{0,1:T(8,128)(2,1)S(1)} %copy.29), channel_id=1, source_target_pairs={{0,1},{1,0},{2,17},{3,16},{4,33},{5,32},{6,49},{7,48},{8,65},{9,64... | collective-permute-start | bytes 884744 | tf_op jit(solution)/shard_map/ppermute | solution.py:71
  17.5 165.2 %all-gather.5.cloned.1.call-start = ((), (), s32[]{:S(2)}) async-start(), calls=%async_computation.1 | async-start | bytes 10027008 | tf_op jit(solution)/shard_map/all_gather | solution.py:120
  17.6 32.0 %collective-permute-start.5 = (bf16[384,768]{0,1:T(8,128)(2,1)}, bf16[384,768]{0,1:T(8,128)(2,1)S(1)}, u32[]{:S(2)}, u32[]{:S(2)}) collective-permute-start(bf16[384,768]{0,1:T(8,128)(2,1)} %bitcast.23), channel_id=1, source_target_pairs={{0,16},{16,0},{1,17},{17,1},{2,18},{18,2},{3,19},{19,3},{4,20},{20... | collective-permute-start | bytes 1769480 | tf_op jit(solution)/shard_map/ppermute | solution.py:30
  36.0 30.4 %collective-permute-start.2 = (bf16[384,768]{0,1:T(8,128)(2,1)}, bf16[384,768]{0,1:T(8,128)(2,1)S(1)}, u32[]{:S(2)}, u32[]{:S(2)}) collective-permute-start(bf16[384,768]{0,1:T(8,128)(2,1)} %bitcast.24), channel_id=1, source_target_pairs={{0,32},{32,64},{64,96},{96,0},{1,33},{33,65},{65,97},{97,1},{2,34}... | collective-permute-start | bytes 1769480 | tf_op jit(solution)/shard_map/ppermute | solution.py:30
  49.6 31.6 %collective-permute-start.6 = (bf16[384,768]{0,1:T(8,128)(2,1)S(1)}, bf16[384,768]{0,1:T(8,128)(2,1)S(1)}, u32[]{:S(2)}, u32[]{:S(2)}) collective-permute-start(bf16[384,768]{0,1:T(8,128)(2,1)S(1)} %collective-permute-done.5), channel_id=1, source_target_pairs={{0,32},{32,64},{64,96},{96,0},{1,33},{33,65},{65,97},{97,1},{2,34}... | collective-permute-start | bytes 1769480 | tf_op jit(solution)/shard_map/ppermute | solution.py:30
  66.4 27.4 %collective-permute-start.3 = (bf16[384,768]{0,1:T(8,128)(2,1)S(1)}, bf16[384,768]{0,1:T(8,128)(2,1)S(1)}, u32[]{:S(2)}, u32[]{:S(2)}) collective-permute-start(bf16[384,768]{0,1:T(8,128)(2,1)S(1)} %collective-permute-done.2), channel_id=1, source_target_pairs={{0,32},{32,64},{64,96},{96,0},{1,33},{33,65},{65,97},{97,1},{2,34}... | collective-permute-start | bytes 1769480 | tf_op jit(solution)/shard_map/ppermute | solution.py:30
  68.4 26.3 %collective-permute-start.4 = (bf16[384,768]{0,1:T(8,128)(2,1)}, bf16[384,768]{0,1:T(8,128)(2,1)S(1)}, u32[]{:S(2)}, u32[]{:S(2)}) collective-permute-start(bf16[384,768]{0,1:T(8,128)(2,1)} %bitcast.25), channel_id=1, source_target_pairs={{0,96},{32,0},{64,32},{96,64},{1,97},{33,1},{65,33},{97,65},{2,98}... | collective-permute-start | bytes 1769480 | tf_op jit(solution)/shard_map/ppermute | solution.py:30
  71.2 36.1 %collective-permute-start.8 = (bf16[384,768]{0,1:T(8,128)(2,1)S(1)}, bf16[384,768]{0,1:T(8,128)(2,1)S(1)}, u32[]{:S(2)}, u32[]{:S(2)}) collective-permute-start(bf16[384,768]{0,1:T(8,128)(2,1)S(1)} %collective-permute-done.5), channel_id=1, source_target_pairs={{0,96},{32,0},{64,32},{96,64},{1,97},{33,1},{65,33},{97,65},{2,98}... | collective-permute-start | bytes 1769480 | tf_op jit(solution)/shard_map/ppermute | solution.py:30
  81.2 25.3 %collective-permute-start.7 = (bf16[384,768]{0,1:T(8,128)(2,1)S(1)}, bf16[384,768]{0,1:T(8,128)(2,1)S(1)}, u32[]{:S(2)}, u32[]{:S(2)}) collective-permute-start(bf16[384,768]{0,1:T(8,128)(2,1)S(1)} %collective-permute-done.6), channel_id=1, source_target_pairs={{0,32},{32,64},{64,96},{96,0},{1,33},{33,65},{65,97},{97,1},{2,34}... | collective-permute-start | bytes 1769480 | tf_op jit(solution)/shard_map/ppermute | solution.py:30
Sparse Core Ops, SparseCore 0:
  17.7 86.4 all-gather.2
  123.3 59.3 all-gather.4

commit v17 on v10

--- a/solution.py
+++ b/solution.py
@@ -5,6 +5,7 @@
 from jax import lax
 from jax.sharding import Mesh
 from jax.sharding import PartitionSpec as P
+
 
 BLK = 64
 BOX = 16
@@ -55,7 +56,7 @@
 
 
 def mirror_tile(upper_stored, rows, cols):
-    tile_side, half_width = upper_stored.shape
+    _, half_width = upper_stored.shape
     col_id = lax.axis_index(COL)
     pieces = []
     for k in range(2):
@@ -78,7 +79,7 @@
     return lax.dot_general(left, right_t, (((1,), (1,)), ((), ())), preferred_element_type=jnp.float32)
 
 
-def per_device(upper_stored, block_cells):
+def per_device_body(upper_stored, block_cells):
     rows = lax.axis_size(ROW)
     cols = lax.axis_size(COL)
     row_id = lax.axis_index(ROW)
@@ -115,7 +116,7 @@
     x_size = mesh.devices.shape[1] // 4
     split_mesh = Mesh(mesh.devices.reshape(y_size, 2, 2, x_size, 2), ROW + COL)
     return jax.shard_map(
-        per_device,
+        per_device_body,
         mesh=split_mesh,
         in_specs=(P(ROW, COL), P()),
         out_specs=P(ROW, COL),

time: 194 us -> 194 us (level)
  no operation moved by 1% of the time
where the time goes in v17:
time: 194 us
  waiting for transfers between devices  88.4 us (46%)
  starting transfers between devices  58.1 us (30%)
  matrix products  19.4 us (10%)
  between operations  13.6 us (7%)
  local copies, waits for them, and re-layouts  13 us (7%)
    all_gather x1, waiting for transfers between devices, per_device_body(): low_panel = lax.all_gather(square_low, COL, axis=1, tiled=True)  59.6 us
    ppermute x7, starting transfers between devices, chunked_shift(): lax.ppermute(value[i * step:(i + 1) * step], axis, pairs)  54.1 us
    ppermute x7, waiting for transfers between devices, chunked_shift(): lax.ppermute(value[i * step:(i + 1) * step], axis, pairs)  28.6 us
    dot_general x2, matrix products, dot_t(): lax.dot_general(left, right_t, (((1,), (1,)), ((), ())), preferred_elemen...  19.4 us
    dynamic_update_slice x7, local copies, waits for them, and re-layouts, ring_gather(): panel = lax.dynamic_update_slice_in_dim(panel, part, position * width, 1)  7.3 us
    ppermute x2, starting transfers between devices, mirror_tile(): pieces.append(lax.ppermute(piece, ROW + COL, pairs))  3.97 us
  transfers between devices with their start and end apart: 11, of which 6 were waited for; matrix products, arithmetic and copies ran while one was open for 5% of the time, Pallas kernels for 0%

profile of v17, /device:TPU:1, one launch (start us, length us, event | category | flops | bytes accessed | tf_op | source)
XLA Modules:
  0.0 194.2 jit_solution(1421929608432124653)
XLA Ops:
  6.5 1.2 constant_dynamic-slice_fusion.1
  7.7 0.2 copy.19
  7.9 0.7 collective-permute-start
  8.6 0.2 copy.20
  8.9 3.3 %collective-permute-start.1 = (bf16[384,384]{0,1:T(8,128)(2,1)S(1)}, bf16[384,384]{0,1:T(8,128)(2,1)S(1)}, u32[]{:S(2)}, u32[]{:S(2)}) collective-permute-start(bf16[384,384]{0,1:T(8,128)(2,1)S(1)} %copy.20), channel_id=1, source_target_pairs={{0,1},{1,0},{2,17},{3,16},{4,33},{5,32},{6,49},{7,48},{8,65},{9,64... | collective-permute-start | bytes 884744 | tf_op jit(solution)/shard_map/ppermute | solution.py:71
  12.5 0.1 reshape.14
  12.7 0.4 copy.18
  13.1 0.2 collective-permute-done.1
  13.4 2.7 %broadcast_in_dim.37 = bf16[384,6144]{0,1:T(8,128)(2,1)} broadcast(bf16[]{:T(256)} %constant.98.clone.1), dimensions={} | broadcast | bytes 4718594 | tf_op jit(solution)/shard_map/broadcast_in_dim | solution.py:53
  16.1 1.5 constant_dynamic-update-slice_fusion.7
  17.7 18.5 %collective-permute-start.5 = (bf16[384,768]{0,1:T(8,128)(2,1)}, bf16[384,768]{0,1:T(8,128)(2,1)S(1)}, u32[]{:S(2)}, u32[]{:S(2)}) collective-permute-start(bf16[384,768]{0,1:T(8,128)(2,1)} %bitcast.17), channel_id=1, source_target_pairs={{0,16},{16,0},{1,17},{17,1},{2,18},{18,2},{3,19},{19,3},{4,20},{20... | collective-permute-start | bytes 1769480 | tf_op jit(solution)/shard_map/ppermute | solution.py:30
  36.1 13.2 %collective-permute-start.2 = (bf16[384,768]{0,1:T(8,128)(2,1)}, bf16[384,768]{0,1:T(8,128)(2,1)S(1)}, u32[]{:S(2)}, u32[]{:S(2)}) collective-permute-start(bf16[384,768]{0,1:T(8,128)(2,1)} %bitcast.18), channel_id=1, source_target_pairs={{0,32},{32,64},{64,96},{96,0},{1,33},{33,65},{65,97},{97,1},{2,34}... | collective-permute-start | bytes 1769480 | tf_op jit(solution)/shard_map/ppermute | solution.py:30
  49.3 0.4 collective-permute-done.5
  49.7 16.7 %collective-permute-start.6 = (bf16[384,768]{0,1:T(8,128)(2,1)S(1)}, bf16[384,768]{0,1:T(8,128)(2,1)S(1)}, u32[]{:S(2)}, u32[]{:S(2)}) collective-permute-start(bf16[384,768]{0,1:T(8,128)(2,1)S(1)} %collective-permute-done.5), channel_id=1, source_target_pairs={{0,32},{32,64},{64,96},{96,0},{1,33},{33,65},{65,97},{97,1},{2,34}... | collective-permute-start | bytes 1769480 | tf_op jit(solution)/shard_map/ppermute | solution.py:30
  66.4 2.0 %collective-permute-start.3 = (bf16[384,768]{0,1:T(8,128)(2,1)S(1)}, bf16[384,768]{0,1:T(8,128)(2,1)}, u32[]{:S(2)}, u32[]{:S(2)}) collective-permute-start(bf16[384,768]{0,1:T(8,128)(2,1)S(1)} %collective-permute-done.2), channel_id=1, source_target_pairs={{0,32},{32,64},{64,96},{96,0},{1,33},{33,65},{65,97},{97,1},{2,34}... | collective-permute-start | bytes 1769480 | tf_op jit(solution)/shard_map/ppermute | solution.py:30
  68.4 2.2 %collective-permute-start.4 = (bf16[384,768]{0,1:T(8,128)(2,1)}, bf16[384,768]{0,1:T(8,128)(2,1)S(1)}, u32[]{:S(2)}, u32[]{:S(2)}) collective-permute-start(bf16[384,768]{0,1:T(8,128)(2,1)} %bitcast.19), channel_id=1, source_target_pairs={{0,96},{32,0},{64,32},{96,64},{1,97},{33,1},{65,33},{97,65},{2,98}... | collective-permute-start | bytes 1769480 | tf_op jit(solution)/shard_map/ppermute | solution.py:30
  70.7 0.1 reshape.16
  70.9 0.4 copy.17
  71.3 1.5 collective-permute-start.8
  72.8 8.5 %collective-permute-done.6 = bf16[384,768]{0,1:T(8,128)(2,1)S(1)} collective-permute-done((bf16[384,768]{0,1:T(8,128)(2,1)S(1)}, bf16[384,768]{0,1:T(8,128)(2,1)S(1)}, u32[]{:S(2)}, u32[]{:S(2)}) %collective-permute-start.6) | collective-permute-done | bytes 589856 | tf_op jit(solution)/shard_map/ppermute | solution.py:30
  81.3 0.9 constant_dynamic-update-slice_fusion.6
  82.2 11.9 %collective-permute-done.3 = bf16[384,768]{0,1:T(8,128)(2,1)} collective-permute-done((bf16[384,768]{0,1:T(8,128)(2,1)S(1)}, bf16[384,768]{0,1:T(8,128)(2,1)}, u32[]{:S(2)}, u32[]{:S(2)}) %collective-permute-start.3) | collective-permute-done | bytes 589856 | tf_op jit(solution)/shard_map/ppermute | solution.py:30
  94.0 1.9 %constant_dynamic-update-slice_fusion.5 = bf16[384,6144]{0,1:T(8,128)(2,1)} fusion(bf16[384,6144]{0,1:T(8,128)(2,1)} %constant_dynamic-update-slice_fusion.6, bf16[384,768]{0,1:T(8,128)(2,1)} %collective-permute-done.3, s32[]{:T(128)S(6)} %select_n.122), kind=kLoop, calls=%fused_computation.17 | loop fusion | bytes 1179652 | tf_op jit(solution)/shard_map/dynamic_update_slice | solution.py:45
  96.0 0.9 constant_dynamic-update-slice_fusion.4
  96.9 0.9 constant_dynamic-update-slice_fusion.3
  97.8 0.9 constant_dynamic-update-slice_fusion.2
  98.7 7.9 %collective-permute-done.7 = bf16[384,768]{0,1:T(8,128)(2,1)S(1)} collective-permute-done((bf16[384,768]{0,1:T(8,128)(2,1)S(1)}, bf16[384,768]{0,1:T(8,128)(2,1)S(1)}, u32[]{:S(2)}, u32[]{:S(2)}) %collective-permute-start.7) | collective-permute-done | bytes 589856 | tf_op jit(solution)/shard_map/ppermute | solution.py:30
  106.6 0.9 constant_dynamic-update-slice_fusion.1
  107.5 0.9 constant_dynamic-update-slice_fusion
  108.3 9.7 %fusion.2 = (bf16[768,384]{1,0:T(8,128)(2,1)}, f32[768,384]{1,0:T(8,128)S(1)}) fusion(pred[768,384]{1,0:T(32,128)(4,1)S(1)} %copy.17, bf16[768,6144]{1,0:T(8,128)(2,1)} %all-gather.3.cloned.1.call-done, bf16[384,6144]{0,1:T(8,128)(2,1)} %constant_dynamic-update-slice_fusion), kind=kOutput, calls=%fused_computation.27 | convolution fusion | flops 3624468480 | bytes 16220160 | tf_op jit(solution)/shard_map/dot_general | solution.py:79
  118.1 59.6 %all-gather.5.cloned.1.call-done = bf16[768,6144]{1,0:T(8,128)(2,1)} async-done(((bf16[768,384]{1,0:T(8,128)(2,1)}), bf16[768,6144]{1,0:T(8,128)(2,1)}) %all-gather.5.cloned.1.call-update) | async-done | bytes 9437200 | tf_op jit(solution)/shard_map/all_gather | solution.py:109
  177.6 9.7 %select_convert_fusion = bf16[768,384]{1,0:T(8,128)(2,1)} fusion(pred[768,384]{1,0:T(32,128)(4,1)S(1)} %copy.18, f32[768,384]{1,0:T(8,128)S(1)} %get-tuple-element.14, bf16[768,6144]{1,0:T(8,128)(2,1)} %all-gather.5.cloned.1.call-done, bf16[384,6144]{0,1:T(8,128)(2,1)} %constant_dynamic-update-slice_fusion), kind=kOutput, calls=%fused_computation.2 | convolution fusion | flops 3625353216 | bytes 16220160 | tf_op jit(solution)/shard_map/dot_general | solution.py:79
  (25 shorter events, 0.7 us)
Async XLA Ops:
  6.5 5.6 %copy-start = (s32[96,3]{0,1:T(4,128)S(1)}, s32[96,3]{0,1:T(4,128)}, u32[]{:S(2)}) copy-start(s32[96,3]{0,1:T(4,128)} %param.3) | copy-start | bytes 3460
  6.5 9.5 %copy-start.1 = (bf16[768,384]{1,0:T(8,128)(2,1)S(1)}, bf16[768,384]{1,0:T(8,128)(2,1)}, u32[]{:S(2)}) copy-start(bf16[768,384]{1,0:T(8,128)(2,1)} %param.2) | copy-start | bytes 1769476
  6.5 101.8 %all-gather.3.cloned.1.call-start = ((), (), s32[]{:S(2)}) async-start(), calls=%async_computation | async-start | bytes 10027008 | tf_op jit(solution)/shard_map/all_gather | solution.py:105
  7.9 5.2 %collective-permute-start = (bf16[384,384]{0,1:T(8,128)(2,1)S(1)}, bf16[384,384]{0,1:T(8,128)(2,1)S(1)}, u32[]{:S(2)}, u32[]{:S(2)}) collective-permute-start(bf16[384,384]{0,1:T(8,128)(2,1)S(1)} %copy.19), channel_id=1, source_target_pairs={{0,0},{1,1},{2,16},{3,17},{4,32},{5,33},{6,48},{7,49},{8,64},{9,65... | collective-permute-start | bytes 884744 | tf_op jit(solution)/shard_map/ppermute | solution.py:71
  8.9 4.5 %collective-permute-start.1 = (bf16[384,384]{0,1:T(8,128)(2,1)S(1)}, bf16[384,384]{0,1:T(8,128)(2,1)S(1)}, u32[]{:S(2)}, u32[]{:S(2)}) collective-permute-start(bf16[384,384]{0,1:T(8,128)(2,1)S(1)} %copy.20), channel_id=1, source_target_pairs={{0,1},{1,0},{2,17},{3,16},{4,33},{5,32},{6,49},{7,48},{8,65},{9,64... | collective-permute-start | bytes 884744 | tf_op jit(solution)/shard_map/ppermute | solution.py:71
  17.6 160.0 %all-gather.5.cloned.1.call-start = ((), (), s32[]{:S(2)}) async-start(), calls=%async_computation.1 | async-start | bytes 10027008 | tf_op jit(solution)/shard_map/all_gather | solution.py:109
  17.7 32.0 %collective-permute-start.5 = (bf16[384,768]{0,1:T(8,128)(2,1)}, bf16[384,768]{0,1:T(8,128)(2,1)S(1)}, u32[]{:S(2)}, u32[]{:S(2)}) collective-permute-start(bf16[384,768]{0,1:T(8,128)(2,1)} %bitcast.17), channel_id=1, source_target_pairs={{0,16},{16,0},{1,17},{17,1},{2,18},{18,2},{3,19},{19,3},{4,20},{20... | collective-permute-start | bytes 1769480 | tf_op jit(solution)/shard_map/ppermute | solution.py:30
  36.1 30.3 %collective-permute-start.2 = (bf16[384,768]{0,1:T(8,128)(2,1)}, bf16[384,768]{0,1:T(8,128)(2,1)S(1)}, u32[]{:S(2)}, u32[]{:S(2)}) collective-permute-start(bf16[384,768]{0,1:T(8,128)(2,1)} %bitcast.18), channel_id=1, source_target_pairs={{0,32},{32,64},{64,96},{96,0},{1,33},{33,65},{65,97},{97,1},{2,34}... | collective-permute-start | bytes 1769480 | tf_op jit(solution)/shard_map/ppermute | solution.py:30
  49.7 31.6 %collective-permute-start.6 = (bf16[384,768]{0,1:T(8,128)(2,1)S(1)}, bf16[384,768]{0,1:T(8,128)(2,1)S(1)}, u32[]{:S(2)}, u32[]{:S(2)}) collective-permute-start(bf16[384,768]{0,1:T(8,128)(2,1)S(1)} %collective-permute-done.5), channel_id=1, source_target_pairs={{0,32},{32,64},{64,96},{96,0},{1,33},{33,65},{65,97},{97,1},{2,34}... | collective-permute-start | bytes 1769480 | tf_op jit(solution)/shard_map/ppermute | solution.py:30
  66.4 27.6 %collective-permute-start.3 = (bf16[384,768]{0,1:T(8,128)(2,1)S(1)}, bf16[384,768]{0,1:T(8,128)(2,1)}, u32[]{:S(2)}, u32[]{:S(2)}) collective-permute-start(bf16[384,768]{0,1:T(8,128)(2,1)S(1)} %collective-permute-done.2), channel_id=1, source_target_pairs={{0,32},{32,64},{64,96},{96,0},{1,33},{33,65},{65,97},{97,1},{2,34}... | collective-permute-start | bytes 1769480 | tf_op jit(solution)/shard_map/ppermute | solution.py:30
  68.4 27.5 %collective-permute-start.4 = (bf16[384,768]{0,1:T(8,128)(2,1)}, bf16[384,768]{0,1:T(8,128)(2,1)S(1)}, u32[]{:S(2)}, u32[]{:S(2)}) collective-permute-start(bf16[384,768]{0,1:T(8,128)(2,1)} %bitcast.19), channel_id=1, source_target_pairs={{0,96},{32,0},{64,32},{96,64},{1,97},{33,1},{65,33},{97,65},{2,98}... | collective-permute-start | bytes 1769480 | tf_op jit(solution)/shard_map/ppermute | solution.py:30
  71.3 36.1 %collective-permute-start.8 = (bf16[384,768]{0,1:T(8,128)(2,1)S(1)}, bf16[384,768]{0,1:T(8,128)(2,1)S(1)}, u32[]{:S(2)}, u32[]{:S(2)}) collective-permute-start(bf16[384,768]{0,1:T(8,128)(2,1)S(1)} %collective-permute-done.5), channel_id=1, source_target_pairs={{0,96},{32,0},{64,32},{96,64},{1,97},{33,1},{65,33},{97,65},{2,98}... | collective-permute-start | bytes 1769480 | tf_op jit(solution)/shard_map/ppermute | solution.py:30
  81.3 25.3 %collective-permute-start.7 = (bf16[384,768]{0,1:T(8,128)(2,1)S(1)}, bf16[384,768]{0,1:T(8,128)(2,1)S(1)}, u32[]{:S(2)}, u32[]{:S(2)}) collective-permute-start(bf16[384,768]{0,1:T(8,128)(2,1)S(1)} %collective-permute-done.6), channel_id=1, source_target_pairs={{0,32},{32,64},{64,96},{96,0},{1,33},{33,65},{65,97},{97,1},{2,34}... | collective-permute-start | bytes 1769480 | tf_op jit(solution)/shard_map/ppermute | solution.py:30
Sparse Core Ops, SparseCore 0:
  17.7 86.4 all-gather.2
  118.2 59.4 all-gather.4
